TPU v7x, 512 devices: a whole 4x8x8 slice. The times are simulated.
512 devices in a mesh: seq: 128 (over y, z, core), tp: 4 (over x).
Axes of the slice: x: 4, y: 8, z: 8, core: 2. Of those that a mesh axis runs over, the one named last changes fastest.
Arguments:
- tokens: bfloat16 [32768, 1280], P('seq', 'tp'), may hold values from -6 to 6
- first_gain: float32 [1280], replicated, may hold values from 0.1 to 1.9
- w_query: bfloat16 [1280, 1280], P(None, 'tp')
- w_key: bfloat16 [1280, 1280], P(None, 'tp')
- w_value: bfloat16 [1280, 1280], P(None, 'tp'), may hold values from -0.15625 to 0.15625
- w_out: bfloat16 [1280, 1280], P('tp'), may hold values from -0.625 to 0.625
- segment_ids: int32 [32768], P('seq'), may hold values from 0 to 191, never falling along the last dimension, each value on 1 to 512 neighbouring positions
- keep_mask: int32 [32768], P('seq'), may hold values 0 or 1
- merge_gain: float32 [1280], replicated, may hold values from 0.1 to 1.9
- w_merge: bfloat16 [5120, 640], P('tp'), may hold values from -0.078125 to 0.078125
- merge_index: int32 [8192, 4], P('seq'), may hold values from 0 to 32767, as said below
- destination: int32 [8192], P('seq'), may hold values from 0 to 8191, as said below
Outputs:
- delivered: bfloat16 [8192, 640], P('seq', 'tp')
Inputs may be any that keep to these rules, and one draw needn't show every extreme that they name: `segment_ids`: segment numbers never fall along the tokens; each picture or clip holds 1 to 512 tokens and one holds exactly 512. `merge_index`: the four entries of merged row m are different tokens of the device that holds row m, that is of rows (m // 64) * 256 to that plus 256 - 1; every token lies in exactly one group. `destination`: a permutation of the merged rows. The owner of row m is destination[m] // 64; the 64 rows of each device go to exactly 32 owners, exactly 2 rows to each.
All inputs are finite; a program needn't handle non-finite values. No bound on the sum of `keep_mask` on one device may be relied on, other than what follows from the above.
Results may differ from a plain program's by a relative error of at most 0.022.
Values may be sent and summed in bfloat16 or wider, within the bound.
No kernel may reach another device: no remote copies, remote signals or barrier semaphores. Data moves between devices by JAX's collectives and lax.ppermute only.
A program may use at most 64 MiB of HBM per device.

v0:
```python
import jax
import jax.numpy as jnp
from jax import lax
from jax.sharding import PartitionSpec as P

HD = 80


EPS = 1e-06


def from_behind(shard, axis, by):
    length = lax.axis_size(axis)
    pairs = [(i, i + by) for i in range(length) if 0 <= i + by < length]
    return lax.ppermute(shard, axis, pairs)


def layer_norm(activations, norm_gain):
    activations = activations.astype(jnp.float32)
    row_mean = jnp.mean(activations, axis=-1, keepdims=True)
    centered = activations - row_mean
    variance = jnp.mean(centered * centered, axis=-1, keepdims=True)
    return centered * lax.rsqrt(variance + EPS) * norm_gain


def body(
    tokens,
    first_gain,
    w_query,
    w_key,
    w_value,
    w_out,
    segment_ids,
    keep_mask,
    merge_gain,
    w_merge,
    merge_index,
    destination,
):
    row_count = tokens.shape[0]
    local_width = w_query.shape[1]
    heads_here = local_width // HD
    gathered = lax.all_gather(tokens, "tp", axis=1, tiled=True)
    normed = layer_norm(gathered, first_gain).astype(jnp.bfloat16)
    queries = jnp.dot(normed, w_query, preferred_element_type=jnp.float32).astype(jnp.bfloat16)
    key_rows = jnp.dot(normed, w_key, preferred_element_type=jnp.float32).astype(jnp.bfloat16)
    value_rows = jnp.dot(normed, w_value, preferred_element_type=jnp.float32).astype(jnp.bfloat16)
    paired = jnp.concatenate([key_rows, value_rows], axis=1)
    code_query = segment_ids + 1
    code_key = jnp.where(keep_mask > 0, code_query, 0)
    pair_list = [paired]
    code_list = [code_key]
    for offset in (1, 2, -1, -2):
        moved_pair, moved_code = from_behind((paired, code_key), "seq", offset)
        pair_list.append(moved_pair)
        code_list.append(moved_code)
    all_pairs = jnp.concatenate(pair_list, axis=0)
    all_codes = jnp.concatenate(code_list, axis=0)
    window = all_pairs.shape[0]
    key_heads = all_pairs[:, :local_width].reshape(window, heads_here, HD)
    value_heads = all_pairs[:, local_width:].reshape(window, heads_here, HD)
    query_heads = queries.reshape(row_count, heads_here, HD)
    score_scale = HD ** (-0.5)
    scores = (
        jnp.einsum("qhd,khd->hqk", query_heads, key_heads, preferred_element_type=jnp.float32)
        * score_scale
    )
    query_pos = jnp.arange(row_count)[:, None]
    key_pos = jnp.arange(window)[None, :]
    allowed = (code_query[:, None] == all_codes[None, :]) | (key_pos == query_pos)
    scores = jnp.where(allowed[None], scores, -1e30)
    row_max = jnp.max(scores, axis=-1, keepdims=True)
    exponent = jnp.exp(scores - row_max)
    row_total = jnp.sum(exponent, axis=-1, keepdims=True)
    weights = (exponent / row_total).astype(jnp.bfloat16)
    attended = jnp.einsum("hqk,khd->qhd", weights, value_heads, preferred_element_type=jnp.float32)
    attended = attended.reshape(row_count, local_width).astype(jnp.bfloat16)
    partial_sum = jnp.dot(attended, w_out, preferred_element_type=jnp.float32)
    position = lax.axis_index("tp")
    seq_index = lax.axis_index("seq")
    local_index = merge_index - seq_index * row_count
    column = lax.dynamic_slice_in_dim(local_index, position, 1, 1)[:, 0]
    mixed_sum = lax.psum(partial_sum.astype(jnp.bfloat16), "tp").astype(jnp.float32)
    updated = gathered.astype(jnp.float32) + mixed_sum
    merged_norm = layer_norm(updated, merge_gain).astype(jnp.bfloat16)
    picked = jnp.take(merged_norm, column, axis=0)
    partial_proj = jnp.dot(picked, w_merge, preferred_element_type=jnp.float32)
    projected = lax.psum_scatter(
        partial_proj.astype(jnp.bfloat16), "tp", scatter_dimension=1, tiled=True
    )
    slot_count = projected.shape[0]
    slot_range = jnp.arange(slot_count)
    piece_rows = lax.all_gather(projected, "seq", axis=0, tiled=True)
    piece_dest = lax.all_gather(destination, "seq", axis=0, tiled=True)
    piece_slot = piece_dest - seq_index * slot_count
    one_hot = (piece_slot[None, :] == slot_range[:, None]).astype(jnp.bfloat16)
    delivered = jnp.dot(one_hot, piece_rows, preferred_element_type=jnp.float32)
    return delivered.astype(jnp.bfloat16)


def solution(mesh):
    return jax.shard_map(
        body,
        mesh=mesh,
        in_specs=(
            P("seq", "tp"),
            P(),
            P(None, "tp"),
            P(None, "tp"),
            P(None, "tp"),
            P("tp", None),
            P("seq"),
            P("seq"),
            P(),
            P("tp", None),
            P("seq", None),
            P("seq"),
        ),
        out_specs=P("seq", "tp"),
        check_vma=False,
    )
```

profile of v0, /device:TPU:1, one launch (start us, length us, event | category | flops | bytes accessed | tf_op | source)
XLA Modules:
  0.0 671.7 jit_solution(445219230451714577)
XLA Ops:
  6.5 11.7 %all_gather.10 = bf16[256,1280]{0,1:T(8,128)(2,1)S(1)} all-gather(bf16[256,320]{0,1:T(8,128)(2,1)} %param.12), channel_id=1, replica_groups=mesh['seq'=128,'tp'=4] {'tp'}, dimensions={1}, use_global_device_ids=true | all-gather | bytes 819200 | tf_op jit(solution)/shard_map/all_gather | solution.py:43
  21.6 7.4 %collective-permute-start = (bf16[256,640]{0,1:T(8,128)(2,1)}, bf16[256,640]{0,1:T(8,128)(2,1)}, u32[]{:S(2)}, u32[]{:S(2)}) collective-permute-start(bf16[256,640]{0,1:T(8,128)(2,1)} %get-tuple-element.11), channel_id=1, source_target_pairs={{0,4},{4,8},{8,12},{12,16},{16,20},{20,24},{24,28},{28,32},{32,36}... | collective-permute-start | bytes 983048 | tf_op jit(solution)/shard_map/ppermute | solution.py:15
  29.1 4.0 collective-permute-start.1
  33.1 2.3 collective-permute-start.2
  35.4 1.3 collective-permute-start.3
  36.8 4.0 collective-permute-start.4
  40.8 2.3 convolution_convert_fusion.1
  43.1 4.0 collective-permute-start.5
  47.8 1.9 collective-permute-start.6
  49.8 4.0 collective-permute-done.6
  53.8 1.3 collective-permute-start.7
  55.1 3.8 collective-permute-done.7
  58.9 1.0 fusion.13
  61.0 1.0 fusion.35
  62.0 3.1 exponential_reduce_fusion
  65.2 4.5 fusion.16
  69.7 2.3 convolution_convert_fusion
  72.1 62.8 %all-reduce.3.cloned.1.call-done = bf16[256,1280]{1,0:T(8,128)(2,1)} async-done(((bf16[256,1280]{1,0:T(8,128)(2,1)}), bf16[256,1280]{1,0:T(8,128)(2,1)}) %all-reduce.3.cloned.1.call-update) | async-done | bytes 655376 | tf_op jit(solution)/shard_map/psum | solution.py:83
  134.9 1.4 fusion.15
  139.1 26.7 %reduce-scatter.4.cloned.1.call-done = bf16[160,64]{1,0:T(8,128)(2,1)} async-done(((bf16[640,64]{1,0:T(8,128)(2,1)}), bf16[160,64]{1,0:T(8,128)(2,1)}) %reduce-scatter.4.cloned.1.call-update) | async-done | bytes 20496
  165.8 1.5 copy.16
  167.4 1.3 dynamic-slice
  169.6 492.1 %all-reduce = s32[8192]{0:T(1024)S(1)} all-reduce(s32[8192]{0:T(1024)S(1)} %dynamic-update-slice), channel_id=1, replica_groups=mesh['seq'=128,'tp'=4] {'seq'}, use_global_device_ids=true, to_apply=%add | all-reduce | flops 8192 | bytes 65536
  661.7 3.5 fusion.17
  (72 shorter events, 8.3 us)
Async XLA Ops:
  6.5 131.3 %copy-start = (bf16[1280,640]{1,0:T(8,128)(2,1)S(1)}, bf16[1280,640]{1,0:T(8,128)(2,1)}, u32[]{:S(2)}) copy-start(bf16[1280,640]{1,0:T(8,128)(2,1)} %param.21) | copy-start | bytes 4915204
  6.5 128.4 %all-reduce.3.cloned.1.call-start = ((), (), s32[]{:S(2)}) async-start(), calls=%async_computation.1 | async-start | bytes 1310720 | tf_op jit(solution)/shard_map/psum | solution.py:83
  18.4 1.1 copy-start.10
  18.9 1.2 copy-start.11
  20.2 16.6 %copy-start.8 = (s32[256]{0:T(256)S(1)}, s32[256]{0:T(256)}, u32[]{:S(2)}) copy-start(s32[256]{0:T(256)} %param.18) | copy-start | bytes 3076
  20.2 16.6 %copy-start.9 = (s32[256]{0:T(256)S(1)}, s32[256]{0:T(256)}, u32[]{:S(2)}) copy-start(s32[256]{0:T(256)} %param.19) | copy-start | bytes 3076
  21.6 38.2 %collective-permute-start = (bf16[256,640]{0,1:T(8,128)(2,1)}, bf16[256,640]{0,1:T(8,128)(2,1)}, u32[]{:S(2)}, u32[]{:S(2)}) collective-permute-start(bf16[256,640]{0,1:T(8,128)(2,1)} %get-tuple-element.11), channel_id=1, source_target_pairs={{0,4},{4,8},{8,12},{12,16},{16,20},{20,24},{24,28},{28,32},{32,36}... | collective-permute-start | bytes 983048 | tf_op jit(solution)/shard_map/ppermute | solution.py:15
  29.1 31.8 %collective-permute-start.1 = (bf16[256,640]{0,1:T(8,128)(2,1)}, bf16[256,640]{0,1:T(8,128)(2,1)S(1)}, u32[]{:S(2)}, u32[]{:S(2)}) collective-permute-start(bf16[256,640]{0,1:T(8,128)(2,1)} %get-tuple-element.11), channel_id=1, source_target_pairs={{0,8},{4,12},{8,16},{12,20},{16,24},{20,28},{24,32},{28,36},{32,40... | collective-permute-start | bytes 983048 | tf_op jit(solution)/shard_map/ppermute | solution.py:15
  33.1 27.8 %collective-permute-start.2 = (bf16[256,640]{0,1:T(8,128)(2,1)}, bf16[256,640]{0,1:T(8,128)(2,1)S(1)}, u32[]{:S(2)}, u32[]{:S(2)}) collective-permute-start(bf16[256,640]{0,1:T(8,128)(2,1)} %get-tuple-element.11), channel_id=1, source_target_pairs={{4,0},{8,4},{12,8},{16,12},{20,16},{24,20},{28,24},{32,28},{36,32}... | collective-permute-start | bytes 983048 | tf_op jit(solution)/shard_map/ppermute | solution.py:15
  35.4 25.5 %collective-permute-start.3 = (bf16[256,640]{0,1:T(8,128)(2,1)}, bf16[256,640]{0,1:T(8,128)(2,1)S(1)}, u32[]{:S(2)}, u32[]{:S(2)}) collective-permute-start(bf16[256,640]{0,1:T(8,128)(2,1)} %get-tuple-element.11), channel_id=1, source_target_pairs={{8,0},{12,4},{16,8},{20,12},{24,16},{28,20},{32,24},{36,28},{40,32... | collective-permute-start | bytes 983048 | tf_op jit(solution)/shard_map/ppermute | solution.py:15
  36.8 23.1 %copy-start.2 = (bf16[1280,640]{0,1:T(8,128)(2,1)S(1)}, bf16[1280,640]{0,1:T(8,128)(2,1)}, u32[]{:S(2)}) copy-start(bf16[1280,640]{0,1:T(8,128)(2,1)} %get-tuple-element.12) | copy-start | bytes 4915204
  36.8 6.3 collective-permute-start.4
  43.1 4.7 collective-permute-start.5
  47.8 6.0 collective-permute-start.6
  53.8 5.1 collective-permute-start.7
  61.0 1.0 copy-start.5
  62.0 3.1 copy-start.4
  65.1 4.5 copy-start.3
  69.7 2.4 copy-start.7
  72.0 93.8 %reduce-scatter.4.cloned.1.call-start = ((), (), s32[]{:S(2)}) async-start(), calls=%async_computation.3 | async-start | bytes 204800
  72.1 64.6 %copy-start.6 = (f32[1280]{0:T(1024)S(1)}, f32[1280]{0:T(1024)}, u32[]{:S(2)}) copy-start(f32[1280]{0:T(1024)} %param.20) | copy-start | bytes 15364
  134.9 1.4 copy-start.1
  137.8 31.5 %copy-start.13 = (s32[64]{0:T(128)S(1)}, s32[64]{0:T(128)}, u32[]{:S(2)}) copy-start(s32[64]{0:T(128)} %param.23) | copy-start | bytes 772
  139.1 522.6 %all-gather.2.cloned.1.call-start = ((), (), s32[]{:S(2)}) async-start(), calls=%async_computation.2 | async-start | bytes 4227072 | tf_op jit(solution)/shard_map/all_gather | solution.py:93
  (1 other events, 0.8 us)
Sparse Core Ops, SparseCore 0:
  72.1 62.7 all-reduce.2
  139.2 26.5 reduce-scatter.3
  169.0 86.8 all-gather.1
where the time goes:
time: 675 us; the launch traced here: 672 us
  blocking collectives  504 us (75%)
  waiting for transfers between devices  98.1 us (15%)
  starting transfers between devices  26.3 us (4%)
  matrix products  17.2 us (3%)
  between operations  14.1 us (2%)
  local copies, waits for them, and re-layouts  7.64 us (1%)
    unnamed x1, blocking collectives  492 us
    psum x1, waiting for transfers between devices, body(): lax.psum(partial_sum.astype(jnp.bfloat16), 'tp').astype(jnp.float32)  62.8 us
    unnamed x4, waiting for transfers between devices  26.7 us
    ppermute x8, starting transfers between devices, from_behind(): return lax.ppermute(shard, axis, pairs)  26.2 us
  transfers between devices with their start and end apart: 11, of which 5 were waited for; matrix products, arithmetic and copies ran while one was open for 1% of the time, Pallas kernels for 0%

commit v1 on v0

--- a/solution.py
+++ b/solution.py
@@ -4,6 +4,7 @@
 from jax.sharding import PartitionSpec as P
 
 HD = 80
+CAP = 2
 
 
 EPS = 1e-06
@@ -40,6 +41,8 @@
     row_count = tokens.shape[0]
     local_width = w_query.shape[1]
     heads_here = local_width // HD
+    tp_size = lax.axis_size("tp")
+    seq_size = lax.axis_size("seq")
     gathered = lax.all_gather(tokens, "tp", axis=1, tiled=True)
     normed = layer_norm(gathered, first_gain).astype(jnp.bfloat16)
     queries = jnp.dot(normed, w_query, preferred_element_type=jnp.float32).astype(jnp.bfloat16)
@@ -75,26 +78,48 @@
     weights = (exponent / row_total).astype(jnp.bfloat16)
     attended = jnp.einsum("hqk,khd->qhd", weights, value_heads, preferred_element_type=jnp.float32)
     attended = attended.reshape(row_count, local_width).astype(jnp.bfloat16)
-    partial_sum = jnp.dot(attended, w_out, preferred_element_type=jnp.float32)
+
     position = lax.axis_index("tp")
     seq_index = lax.axis_index("seq")
     local_index = merge_index - seq_index * row_count
+    order = local_index.T.reshape(row_count)
+    attended_sorted = jnp.take(attended, order, axis=0)
+    partial_sum = jnp.dot(attended_sorted, w_out, preferred_element_type=jnp.float32)
+    mixed_sum = lax.psum_scatter(
+        partial_sum.astype(jnp.bfloat16), "tp", scatter_dimension=0, tiled=True
+    ).astype(jnp.float32)
     column = lax.dynamic_slice_in_dim(local_index, position, 1, 1)[:, 0]
-    mixed_sum = lax.psum(partial_sum.astype(jnp.bfloat16), "tp").astype(jnp.float32)
-    updated = gathered.astype(jnp.float32) + mixed_sum
-    merged_norm = layer_norm(updated, merge_gain).astype(jnp.bfloat16)
-    picked = jnp.take(merged_norm, column, axis=0)
+    residual = jnp.take(gathered, column, axis=0)
+    updated = residual.astype(jnp.float32) + mixed_sum
+    picked = layer_norm(updated, merge_gain).astype(jnp.bfloat16)
     partial_proj = jnp.dot(picked, w_merge, preferred_element_type=jnp.float32)
     projected = lax.psum_scatter(
         partial_proj.astype(jnp.bfloat16), "tp", scatter_dimension=1, tiled=True
     )
     slot_count = projected.shape[0]
-    slot_range = jnp.arange(slot_count)
-    piece_rows = lax.all_gather(projected, "seq", axis=0, tiled=True)
-    piece_dest = lax.all_gather(destination, "seq", axis=0, tiled=True)
-    piece_slot = piece_dest - seq_index * slot_count
-    one_hot = (piece_slot[None, :] == slot_range[:, None]).astype(jnp.bfloat16)
-    delivered = jnp.dot(one_hot, piece_rows, preferred_element_type=jnp.float32)
+    width = projected.shape[1]
+
+    owner = destination // slot_count
+    slot = destination - owner * slot_count
+    lane = jnp.arange(slot_count)
+    same_owner = owner[:, None] == owner[None, :]
+    earlier = lane[None, :] < lane[:, None]
+    rank = jnp.sum(jnp.where(same_owner & earlier, 1, 0), axis=1)
+    send_pos = owner * CAP + rank
+    target = jnp.arange(seq_size * CAP)
+    send_hot = (send_pos[None, :] == target[:, None]).astype(jnp.bfloat16)
+    send_rows = jnp.dot(send_hot, projected, preferred_element_type=jnp.float32)
+    send_rows = send_rows.astype(jnp.bfloat16).reshape(seq_size, CAP, width)
+    slot_code = (slot + 1).astype(jnp.float32)
+    send_slot = jnp.dot(send_hot.astype(jnp.float32), slot_code, precision=lax.Precision.HIGHEST)
+    slot_row = jnp.zeros((seq_size, 1, width), jnp.bfloat16)
+    slot_row = slot_row.at[:, 0, :CAP].set(send_slot.reshape(seq_size, CAP).astype(jnp.bfloat16))
+    send_buf = jnp.concatenate([send_rows, slot_row], axis=1).reshape(seq_size * (CAP + 1), width)
+    recv = lax.all_to_all(send_buf, "seq", 0, 0, tiled=True).reshape(seq_size, CAP + 1, width)
+    recv_rows = recv[:, :CAP, :].reshape(seq_size * CAP, width)
+    recv_slot = recv[:, CAP, :CAP].reshape(seq_size * CAP).astype(jnp.int32) - 1
+    recv_hot = (recv_slot[None, :] == lane[:, None]).astype(jnp.bfloat16)
+    delivered = jnp.dot(recv_hot, recv_rows, preferred_element_type=jnp.float32)
     return delivered.astype(jnp.bfloat16)
 
 

time: 675 us -> 178 us (0.26)
  blocking collectives: 504 us -> 40.5 us
  waiting for transfers between devices: 98.1 us -> 68.4 us
    unnamed x1 -> x0, blocking collectives: 492 us -> none
    psum x1 -> x0, waiting for transfers between devices: 62.8 us -> none  [body(): lax.psum(partial_sum.astype(jnp.bfloat16), 'tp').astype(jnp.float32)]
    reduce_scatter x0 -> x1, waiting for transfers between devices: none -> 34.7 us  [body(): lax.psum_scatter(partial_sum.astype(jnp.bfloat16), 'tp', scatter_dimensio...]
    all_to_all x0 -> x1, blocking collectives: none -> 28.9 us  [body(): lax.all_to_all(send_buf, 'seq', 0, 0, tiled=True)]
    unnamed x4 -> x3, waiting for transfers between devices: 26.7 us -> 25.1 us
  transfers between devices with their start and end apart: 11 -> 10, of which waited for: 5 -> 5; matrix products, arithmetic and copies ran while one was open for 1% -> 4% of each run, Pallas kernels for 0% -> 0%
where the time goes in v1:
time: 178 us; the launch traced here: 177 us
  waiting for transfers between devices  68.4 us (38%)
  blocking collectives  40.5 us (23%)
  starting transfers between devices  26.1 us (15%)
  matrix products  15.1 us (8%)
  between operations  13.8 us (8%)
  local copies, waits for them, and re-layouts  7.86 us (4%)
  other arithmetic  5.42 us (3%)
    reduce_scatter x1, waiting for transfers between devices, body(): lax.psum_scatter(partial_sum.astype(jnp.bfloat16), 'tp', scatter_dimensio...  34.7 us
    all_to_all x1, blocking collectives, body(): lax.all_to_all(send_buf, 'seq', 0, 0, tiled=True)  28.9 us
    ppermute x8, starting transfers between devices, from_behind(): return lax.ppermute(shard, axis, pairs)  26.1 us
    unnamed x3, waiting for transfers between devices  25.1 us
    all_gather x1, blocking collectives, body(): gathered = lax.all_gather(tokens, 'tp', axis=1, tiled=True)  11.7 us
    ppermute x8, waiting for transfers between devices, from_behind(): return lax.ppermute(shard, axis, pairs)  8.52 us
    dot_general x1, matrix products, body(): jnp.einsum('hqk,khd->qhd', weights, value_heads, preferred_element_type=j...  4.14 us
  transfers between devices with their start and end apart: 10, of which 5 were waited for; matrix products, arithmetic and copies ran while one was open for 4% of the time, Pallas kernels for 0%

profile of v1, /device:TPU:1, one launch (start us, length us, event | category | flops | bytes accessed | tf_op | source)
XLA Modules:
  0.0 177.3 jit_solution(7128493967322918882)
XLA Ops:
  6.5 11.7 %all_gather.3 = bf16[256,1280]{0,1:T(8,128)(2,1)S(1)} all-gather(bf16[256,320]{0,1:T(8,128)(2,1)} %param.14), channel_id=1, replica_groups=mesh['seq'=128,'tp'=4] {'tp'}, dimensions={1}, use_global_device_ids=true | all-gather | bytes 819200 | tf_op jit(solution)/shard_map/all_gather | solution.py:46
  20.9 7.4 %collective-permute-start = (bf16[256,640]{0,1:T(8,128)(2,1)}, bf16[256,640]{0,1:T(8,128)(2,1)}, u32[]{:S(2)}, u32[]{:S(2)}) collective-permute-start(bf16[256,640]{0,1:T(8,128)(2,1)} %get-tuple-element.23), channel_id=1, source_target_pairs={{0,4},{4,8},{8,12},{12,16},{16,20},{20,24},{24,28},{28,32},{32,36}... | collective-permute-start | bytes 983048 | tf_op jit(solution)/shard_map/ppermute | solution.py:16
  28.4 4.0 %collective-permute-start.1 = (bf16[256,640]{0,1:T(8,128)(2,1)}, bf16[256,640]{0,1:T(8,128)(2,1)S(1)}, u32[]{:S(2)}, u32[]{:S(2)}) collective-permute-start(bf16[256,640]{0,1:T(8,128)(2,1)} %get-tuple-element.23), channel_id=1, source_target_pairs={{0,8},{4,12},{8,16},{12,20},{16,24},{20,28},{24,32},{28,36},{32,40... | collective-permute-start | bytes 983048 | tf_op jit(solution)/shard_map/ppermute | solution.py:16
  32.4 2.3 %collective-permute-start.2 = (bf16[256,640]{0,1:T(8,128)(2,1)}, bf16[256,640]{0,1:T(8,128)(2,1)S(1)}, u32[]{:S(2)}, u32[]{:S(2)}) collective-permute-start(bf16[256,640]{0,1:T(8,128)(2,1)} %get-tuple-element.23), channel_id=1, source_target_pairs={{4,0},{8,4},{12,8},{16,12},{20,16},{24,20},{28,24},{32,28},{36,32}... | collective-permute-start | bytes 983048 | tf_op jit(solution)/shard_map/ppermute | solution.py:16
  34.7 1.3 collective-permute-start.3
  36.1 3.9 %collective-permute-start.4 = (s32[256]{0:T(256)S(1)}, s32[256]{0:T(256)S(1)}, u32[]{:S(2)}, u32[]{:S(2)}) collective-permute-start(s32[256]{0:T(256)S(1)} %get-tuple-element.20), channel_id=1, source_target_pairs={{0,4},{4,8},{8,12},{12,16},{16,20},{20,24},{24,28},{28,32},{32,36}... | collective-permute-start | bytes 3080 | tf_op jit(solution)/shard_map/ppermute | solution.py:16
  40.2 2.4 %convolution_convert_fusion.1 = bf16[256,320]{0,1:T(8,128)(2,1)} fusion(bf16[1280,320]{0,1:T(8,128)(2,1)} %param.16, bf16[256,1280]{0,1:T(8,128)(2,1)S(1)} %all_gather.3, f32[1280]{0:T(1024)S(1)} %copy-done.10, f32[256]{0:T(256)S(1)} %add_rsqrt_fusion, f32[256]{0:T(256)S(1)} %broadcast_multiply_fusion), kind=kOutput, calls=%fused_computation.23 | convolution fusion | flops 211435520 | bytes 1645568 | tf_op jit(solution)/shard_map/dot_general | solution.py:48
  42.6 4.0 %collective-permute-start.5 = (s32[256]{0:T(256)S(1)}, s32[256]{0:T(256)S(1)}, u32[]{:S(2)}, u32[]{:S(2)}) collective-permute-start(s32[256]{0:T(256)S(1)} %get-tuple-element.20), channel_id=1, source_target_pairs={{0,8},{4,12},{8,16},{12,20},{16,24},{20,28},{24,32},{28,36},{32,40... | collective-permute-start | bytes 3080 | tf_op jit(solution)/shard_map/ppermute | solution.py:16
  47.3 1.9 %collective-permute-start.6 = (s32[256]{0:T(256)S(1)}, s32[256]{0:T(256)S(1)}, u32[]{:S(2)}, u32[]{:S(2)}) collective-permute-start(s32[256]{0:T(256)S(1)} %get-tuple-element.20), channel_id=1, source_target_pairs={{4,0},{8,4},{12,8},{16,12},{20,16},{24,20},{28,24},{32,28},{36,32}... | collective-permute-start | bytes 3080 | tf_op jit(solution)/shard_map/ppermute | solution.py:16
  49.2 4.0 %collective-permute-done.6 = s32[256]{0:T(256)S(1)} collective-permute-done((s32[256]{0:T(256)S(1)}, s32[256]{0:T(256)S(1)}, u32[]{:S(2)}, u32[]{:S(2)}) %collective-permute-start.6) | collective-permute-done | bytes 1056 | tf_op jit(solution)/shard_map/ppermute | solution.py:16
  53.3 1.3 collective-permute-start.7
  54.6 3.8 %collective-permute-done.7 = s32[256]{0:T(256)S(1)} collective-permute-done((s32[256]{0:T(256)S(1)}, s32[256]{0:T(256)S(1)}, u32[]{:S(2)}, u32[]{:S(2)}) %collective-permute-start.7) | collective-permute-done | bytes 1056 | tf_op jit(solution)/shard_map/ppermute | solution.py:16
  60.5 1.0 fusion.54
  61.5 2.9 %exponential_reduce_fusion = f32[4,256]{1,0:T(4,128)S(1)} fusion(pred[256,1280]{1,0:T(8,128)(4,1)S(1)} %copy-done.3, bf16[256,4,80]{0,2,1:T(8,128)(2,1)} %bitcast.38, bf16[1280,4,80]{0,2,1:T(8,128)(2,1)S(1)} %bitcast.31), kind=kOutput, calls=%fused_computation.6 | convolution fusion | flops 214959360 | bytes 1314816 | tf_op jit(solution)/shard_map/sub | solution.py:76
  64.4 4.1 %fusion.13 = bf16[4,80,256]{2,1,0:T(8,128)(2,1)} fusion(bf16[1280,4,80]{0,2,1:T(8,128)(2,1)} %bitcast.33, f32[4,256]{1,0:T(4,128)S(1)} %exponential_reduce_fusion, pred[256,1280]{1,0:T(8,128)(4,1)S(1)} %copy-done.3, bf16[256,4,80]{0,2,1:T(8,128)(2,1)} %bitcast.39, bf16[1280,4,80]{0,2,1:T(8,128)(2,1)S(1)} %bitcast.32), kind=kOutput, calls=%fused_computation.22 | convolution fusion | flops 426068224 | bytes 2297856 | tf_op jit(solution)/shard_map/hqk,khd->qhd/dot_general | solution.py:79
  68.6 1.2 copy.33
  69.7 1.2 gather_fusion.1
  70.9 1.4 convolution_convert_fusion
  73.6 34.7 %reduce-scatter.5.cloned.1.call-done = bf16[64,1280]{1,0:T(8,128)(2,1)} async-done(((bf16[256,1280]{1,0:T(8,128)(2,1)}), bf16[64,1280]{1,0:T(8,128)(2,1)}) %reduce-scatter.5.cloned.1.call-update) | async-done | bytes 163856 | tf_op jit(solution)/shard_map/reduce_scatter | solution.py:88
  108.3 1.1 fusion.18
  109.5 1.2 multiply_reduce_fusion
  110.7 1.4 convolution_convert_fusion.5
  113.3 25.1 %reduce-scatter.7.cloned.1.call-done = bf16[160,64]{1,0:T(8,128)(2,1)} async-done(((bf16[640,64]{1,0:T(8,128)(2,1)}), bf16[160,64]{1,0:T(8,128)(2,1)}) %reduce-scatter.7.cloned.1.call-update) | async-done | bytes 20496
  140.0 28.9 %all_to_all.6 = bf16[128,2,240]{2,1,0:T(2,128)(2,1)S(1)} all-to-all(bf16[128,2,240]{2,1,0:T(2,128)(2,1)S(1)} %reshape.225), channel_id=1, replica_groups=mesh['seq'=128,'tp'=4] {'seq'}, dimensions={0} | all-to-all | bytes 245760 | tf_op jit(solution)/shard_map/all_to_all | solution.py:118
  (83 shorter events, 11.3 us)
Async XLA Ops:
  6.5 104.2 %copy-start = (bf16[1280,640]{1,0:T(8,128)(2,1)S(1)}, bf16[1280,640]{1,0:T(8,128)(2,1)}, u32[]{:S(2)}) copy-start(bf16[1280,640]{1,0:T(8,128)(2,1)} %param.23) | copy-start | bytes 4915204
  6.5 12.1 %copy-start.10 = (f32[1280]{0:T(1024)S(1)}, f32[1280]{0:T(1024)}, u32[]{:S(2)}) copy-start(f32[1280]{0:T(1024)} %param.15) | copy-start | bytes 15364
  6.5 12.1 %copy-start.8 = (bf16[1280,320]{0,1:T(8,128)(2,1)S(1)}, bf16[1280,320]{0,1:T(8,128)(2,1)}, u32[]{:S(2)}) copy-start(bf16[1280,320]{0,1:T(8,128)(2,1)} %param.17) | copy-start | bytes 2457604
  6.5 101.8 %reduce-scatter.5.cloned.1.call-start = ((), (), s32[]{:S(2)}) async-start(), calls=%async_computation.3 | async-start | bytes 819200 | tf_op jit(solution)/shard_map/reduce_scatter | solution.py:88
  18.4 1.1 copy-start.9
  19.6 16.5 %copy-start.6 = (s32[256]{0:T(256)S(1)}, s32[256]{0:T(256)}, u32[]{:S(2)}) copy-start(s32[256]{0:T(256)} %param.20) | copy-start | bytes 3076
  19.6 16.5 %copy-start.7 = (s32[256]{0:T(256)S(1)}, s32[256]{0:T(256)}, u32[]{:S(2)}) copy-start(s32[256]{0:T(256)} %param.21) | copy-start | bytes 3076
  19.6 20.4 %copy-start.5 = (s32[64,4]{0,1:T(4,128)S(1)}, s32[64,4]{0,1:T(4,128)}, u32[]{:S(2)}) copy-start(s32[64,4]{0,1:T(4,128)} %param.24) | copy-start | bytes 3076
  20.9 38.4 %collective-permute-start = (bf16[256,640]{0,1:T(8,128)(2,1)}, bf16[256,640]{0,1:T(8,128)(2,1)}, u32[]{:S(2)}, u32[]{:S(2)}) collective-permute-start(bf16[256,640]{0,1:T(8,128)(2,1)} %get-tuple-element.23), channel_id=1, source_target_pairs={{0,4},{4,8},{8,12},{12,16},{16,20},{20,24},{24,28},{28,32},{32,36}... | collective-permute-start | bytes 983048 | tf_op jit(solution)/shard_map/ppermute | solution.py:16
  28.4 31.9 %collective-permute-start.1 = (bf16[256,640]{0,1:T(8,128)(2,1)}, bf16[256,640]{0,1:T(8,128)(2,1)S(1)}, u32[]{:S(2)}, u32[]{:S(2)}) collective-permute-start(bf16[256,640]{0,1:T(8,128)(2,1)} %get-tuple-element.23), channel_id=1, source_target_pairs={{0,8},{4,12},{8,16},{12,20},{16,24},{20,28},{24,32},{28,36},{32,40... | collective-permute-start | bytes 983048 | tf_op jit(solution)/shard_map/ppermute | solution.py:16
  32.4 28.0 %collective-permute-start.2 = (bf16[256,640]{0,1:T(8,128)(2,1)}, bf16[256,640]{0,1:T(8,128)(2,1)S(1)}, u32[]{:S(2)}, u32[]{:S(2)}) collective-permute-start(bf16[256,640]{0,1:T(8,128)(2,1)} %get-tuple-element.23), channel_id=1, source_target_pairs={{4,0},{8,4},{12,8},{16,12},{20,16},{24,20},{28,24},{32,28},{36,32}... | collective-permute-start | bytes 983048 | tf_op jit(solution)/shard_map/ppermute | solution.py:16
  34.7 25.7 %collective-permute-start.3 = (bf16[256,640]{0,1:T(8,128)(2,1)}, bf16[256,640]{0,1:T(8,128)(2,1)S(1)}, u32[]{:S(2)}, u32[]{:S(2)}) collective-permute-start(bf16[256,640]{0,1:T(8,128)(2,1)} %get-tuple-element.23), channel_id=1, source_target_pairs={{8,0},{12,4},{16,8},{20,12},{24,16},{28,20},{32,24},{36,28},{40,32... | collective-permute-start | bytes 983048 | tf_op jit(solution)/shard_map/ppermute | solution.py:16
  36.1 6.5 %collective-permute-start.4 = (s32[256]{0:T(256)S(1)}, s32[256]{0:T(256)S(1)}, u32[]{:S(2)}, u32[]{:S(2)}) collective-permute-start(s32[256]{0:T(256)S(1)} %get-tuple-element.20), channel_id=1, source_target_pairs={{0,4},{4,8},{8,12},{12,16},{16,20},{20,24},{24,28},{28,32},{32,36}... | collective-permute-start | bytes 3080 | tf_op jit(solution)/shard_map/ppermute | solution.py:16
  40.2 19.2 %copy-start.1 = (bf16[1280,640]{0,1:T(8,128)(2,1)S(1)}, bf16[1280,640]{0,1:T(8,128)(2,1)}, u32[]{:S(2)}) copy-start(bf16[1280,640]{0,1:T(8,128)(2,1)} %get-tuple-element.24) | copy-start | bytes 4915204
  42.6 4.7 %collective-permute-start.5 = (s32[256]{0:T(256)S(1)}, s32[256]{0:T(256)S(1)}, u32[]{:S(2)}, u32[]{:S(2)}) collective-permute-start(s32[256]{0:T(256)S(1)} %get-tuple-element.20), channel_id=1, source_target_pairs={{0,8},{4,12},{8,16},{12,20},{16,24},{20,28},{24,32},{28,36},{32,40... | collective-permute-start | bytes 3080 | tf_op jit(solution)/shard_map/ppermute | solution.py:16
  47.3 6.0 %collective-permute-start.6 = (s32[256]{0:T(256)S(1)}, s32[256]{0:T(256)S(1)}, u32[]{:S(2)}, u32[]{:S(2)}) collective-permute-start(s32[256]{0:T(256)S(1)} %get-tuple-element.20), channel_id=1, source_target_pairs={{4,0},{8,4},{12,8},{16,12},{20,16},{24,20},{28,24},{32,28},{36,32}... | collective-permute-start | bytes 3080 | tf_op jit(solution)/shard_map/ppermute | solution.py:16
  53.3 5.1 %collective-permute-start.7 = (s32[256]{0:T(256)S(1)}, s32[256]{0:T(256)S(1)}, u32[]{:S(2)}, u32[]{:S(2)}) collective-permute-start(s32[256]{0:T(256)S(1)} %get-tuple-element.20), channel_id=1, source_target_pairs={{8,0},{12,4},{16,8},{20,12},{24,16},{28,20},{32,24},{36,28},{40,32... | collective-permute-start | bytes 3080 | tf_op jit(solution)/shard_map/ppermute | solution.py:16
  60.5 1.0 copy-start.3
  68.6 2.3 %copy-start.2 = (bf16[320,1280]{1,0:T(8,128)(2,1)S(1)}, bf16[320,1280]{1,0:T(8,128)(2,1)}, u32[]{:S(2)}) copy-start(bf16[320,1280]{1,0:T(8,128)(2,1)} %param.19) | copy-start | bytes 2457604
  72.3 1.1 copy-start.11
  72.3 38.4 %copy-start.4 = (f32[1280]{0:T(1024)S(1)}, f32[1280]{0:T(1024)}, u32[]{:S(2)}) copy-start(f32[1280]{0:T(1024)} %param.22) | copy-start | bytes 15364
  72.3 66.1 %reduce-scatter.7.cloned.1.call-start = ((), (), s32[]{:S(2)}) async-start(), calls=%async_computation.4 | async-start | bytes 204800
Sparse Core Ops, SparseCore 0:
  72.4 35.8 reduce-scatter.4
  113.0 25.2 reduce-scatter.6

commit v2 on v1

--- a/solution.py
+++ b/solution.py
@@ -13,6 +13,12 @@
 def from_behind(shard, axis, by):
     length = lax.axis_size(axis)
     pairs = [(i, i + by) for i in range(length) if 0 <= i + by < length]
+    return lax.ppermute(shard, axis, pairs)
+
+
+def around(shard, axis, by):
+    length = lax.axis_size(axis)
+    pairs = [(i, (i + by) % length) for i in range(length)]
     return lax.ppermute(shard, axis, pairs)
 
 
@@ -43,22 +49,31 @@
     heads_here = local_width // HD
     tp_size = lax.axis_size("tp")
     seq_size = lax.axis_size("seq")
-    gathered = lax.all_gather(tokens, "tp", axis=1, tiled=True)
+    position = lax.axis_index("tp")
+    seq_index = lax.axis_index("seq")
+
+    blocks = [tokens] + [around(tokens, "tp", -k) for k in range(1, tp_size)]
+    rotated = jnp.concatenate(blocks + blocks, axis=1)
+    start = ((tp_size - position) % tp_size) * tokens.shape[1]
+    gathered = lax.dynamic_slice_in_dim(rotated, start, tp_size * tokens.shape[1], 1)
+
     normed = layer_norm(gathered, first_gain).astype(jnp.bfloat16)
     queries = jnp.dot(normed, w_query, preferred_element_type=jnp.float32).astype(jnp.bfloat16)
     key_rows = jnp.dot(normed, w_key, preferred_element_type=jnp.float32).astype(jnp.bfloat16)
     value_rows = jnp.dot(normed, w_value, preferred_element_type=jnp.float32).astype(jnp.bfloat16)
-    paired = jnp.concatenate([key_rows, value_rows], axis=1)
     code_query = segment_ids + 1
     code_key = jnp.where(keep_mask > 0, code_query, 0)
+    pair_width = 2 * local_width
+    code_block = jnp.zeros((8, pair_width), jnp.bfloat16)
+    code_block = code_block.at[0, :row_count].set(code_key.astype(jnp.bfloat16))
+    paired = jnp.concatenate([jnp.concatenate([key_rows, value_rows], axis=1), code_block], axis=0)
     pair_list = [paired]
-    code_list = [code_key]
     for offset in (1, 2, -1, -2):
-        moved_pair, moved_code = from_behind((paired, code_key), "seq", offset)
-        pair_list.append(moved_pair)
-        code_list.append(moved_code)
-    all_pairs = jnp.concatenate(pair_list, axis=0)
-    all_codes = jnp.concatenate(code_list, axis=0)
+        pair_list.append(from_behind(paired, "seq", offset))
+    all_pairs = jnp.concatenate([p[:row_count] for p in pair_list], axis=0)
+    all_codes = jnp.concatenate(
+        [code_key] + [p[row_count, :row_count].astype(jnp.int32) for p in pair_list[1:]], axis=0
+    )
     window = all_pairs.shape[0]
     key_heads = all_pairs[:, :local_width].reshape(window, heads_here, HD)
     value_heads = all_pairs[:, local_width:].reshape(window, heads_here, HD)
@@ -79,25 +94,31 @@
     attended = jnp.einsum("hqk,khd->qhd", weights, value_heads, preferred_element_type=jnp.float32)
     attended = attended.reshape(row_count, local_width).astype(jnp.bfloat16)
 
-    position = lax.axis_index("tp")
-    seq_index = lax.axis_index("seq")
     local_index = merge_index - seq_index * row_count
-    order = local_index.T.reshape(row_count)
+    rotated_index = jnp.concatenate([local_index, local_index], axis=1)
+    rotated_index = lax.dynamic_slice_in_dim(rotated_index, position, tp_size, 1)
+    order = rotated_index.T.reshape(row_count)
     attended_sorted = jnp.take(attended, order, axis=0)
     partial_sum = jnp.dot(attended_sorted, w_out, preferred_element_type=jnp.float32)
-    mixed_sum = lax.psum_scatter(
-        partial_sum.astype(jnp.bfloat16), "tp", scatter_dimension=0, tiled=True
-    ).astype(jnp.float32)
-    column = lax.dynamic_slice_in_dim(local_index, position, 1, 1)[:, 0]
+    partial_sum = partial_sum.astype(jnp.bfloat16)
+    chunk = row_count // tp_size
+    mixed_sum = partial_sum[:chunk].astype(jnp.float32)
+    for k in range(1, tp_size):
+        mixed_sum = mixed_sum + around(partial_sum[k * chunk:(k + 1) * chunk], "tp", k).astype(jnp.float32)
+    column = rotated_index[:, 0]
     residual = jnp.take(gathered, column, axis=0)
     updated = residual.astype(jnp.float32) + mixed_sum
     picked = layer_norm(updated, merge_gain).astype(jnp.bfloat16)
     partial_proj = jnp.dot(picked, w_merge, preferred_element_type=jnp.float32)
-    projected = lax.psum_scatter(
-        partial_proj.astype(jnp.bfloat16), "tp", scatter_dimension=1, tiled=True
-    )
+    partial_proj = partial_proj.astype(jnp.bfloat16)
+    width = partial_proj.shape[1] // tp_size
+    doubled = jnp.concatenate([partial_proj, partial_proj], axis=1)
+    projected = lax.dynamic_slice_in_dim(doubled, position * width, width, 1).astype(jnp.float32)
+    for k in range(1, tp_size):
+        piece = lax.dynamic_slice_in_dim(doubled, (position + k) * width, width, 1)
+        projected = projected + around(piece, "tp", k).astype(jnp.float32)
+    projected = projected.astype(jnp.bfloat16)
     slot_count = projected.shape[0]
-    width = projected.shape[1]
 
     owner = destination // slot_count
     slot = destination - owner * slot_count

time: 178 us -> 131 us (0.74)
  waiting for transfers between devices: 68.4 us -> 20.3 us
  starting transfers between devices: 26.1 us -> 44.6 us
  between operations: 13.8 us -> 0.58 us
  blocking collectives: 40.5 us -> 34.3 us
  local copies, waits for them, and re-layouts: 7.86 us -> 10.8 us
  matrix products: 15.1 us -> 12.7 us
    reduce_scatter x1 -> x0, waiting for transfers between devices: 34.7 us -> none  [body(): lax.psum_scatter(partial_sum.astype(jnp.bfloat16), 'tp', scatter_dimensio...]
    ppermute x0 -> x9, starting transfers between devices: none -> 29.7 us  [around(): return lax.ppermute(shard, axis, pairs)]
    unnamed x3 -> x0, waiting for transfers between devices: 25.1 us -> none
    all_gather x1 -> x0, blocking collectives: 11.7 us -> none  [body(): gathered = lax.all_gather(tokens, 'tp', axis=1, tiled=True)]
    ppermute x8 -> x4, starting transfers between devices: 26.1 us -> 14.9 us  [from_behind(): return lax.ppermute(shard, axis, pairs)]
    ppermute x0 -> x9, waiting for transfers between devices: none -> 7.27 us  [around(): return lax.ppermute(shard, axis, pairs)]
    all_to_all x1, blocking collectives: 28.9 us -> 34.3 us  [body(): lax.all_to_all(send_buf, 'seq', 0, 0, tiled=True)]
    ppermute x8 -> x4, waiting for transfers between devices: 8.52 us -> 13.1 us  [from_behind(): return lax.ppermute(shard, axis, pairs)]
  transfers between devices with their start and end apart: 10 -> 13, of which waited for: 5 -> 5; matrix products, arithmetic and copies ran while one was open for 4% -> 4% of each run, Pallas kernels for 0% -> 0%
where the time goes in v2:
time: 131 us; the launch traced here: 130 us
  starting transfers between devices  44.6 us (34%)
  blocking collectives  34.3 us (26%)
  waiting for transfers between devices  20.3 us (15%)
  matrix products  12.7 us (10%)
  local copies, waits for them, and re-layouts  10.8 us (8%)
  other arithmetic  7.12 us (5%)
    all_to_all x1, blocking collectives, body(): lax.all_to_all(send_buf, 'seq', 0, 0, tiled=True)  34.3 us
    ppermute x9, starting transfers between devices, around(): return lax.ppermute(shard, axis, pairs)  29.7 us
    ppermute x4, starting transfers between devices, from_behind(): return lax.ppermute(shard, axis, pairs)  14.9 us
    ppermute x4, waiting for transfers between devices, from_behind(): return lax.ppermute(shard, axis, pairs)  13.1 us
    ppermute x9, waiting for transfers between devices, around(): return lax.ppermute(shard, axis, pairs)  7.27 us
    dot_general x1, matrix products, body(): jnp.einsum('hqk,khd->qhd', weights, value_heads, preferred_element_type=j...  4.15 us
    concatenate x1, local copies, waits for them, and re-layouts, body(): rotated = jnp.concatenate(blocks + blocks, axis=1)  3.04 us
    sub x1, matrix products, body(): exponent = jnp.exp(scores - row_max)  2.95 us
  transfers between devices with their start and end apart: 13, of which 5 were waited for; matrix products, arithmetic and copies ran while one was open for 4% of the time, Pallas kernels for 0%

profile of v2, /device:TPU:1, one launch (start us, length us, event | category | flops | bytes accessed | tf_op | source)
XLA Modules:
  0.0 130.4 jit_solution(4113502374236818088)
XLA Ops:
  0.0 1.2 copy.54
  1.2 3.9 %collective-permute-start.2 = (bf16[256,320]{1,0:T(8,128)(2,1)S(1)}, bf16[256,320]{1,0:T(8,128)(2,1)S(1)}, u32[]{:S(2)}, u32[]{:S(2)}) collective-permute-start(bf16[256,320]{1,0:T(8,128)(2,1)S(1)} %copy.54), channel_id=1, source_target_pairs={{0,1},{1,2},{2,3},{3,0},{4,5},{5,6},{6,7},{7,4},{8,9},{9,10},{10,1... | collective-permute-start | bytes 491528 | tf_op jit(solution)/shard_map/ppermute | solution.py:22
  5.2 4.4 %collective-permute-start.1 = (bf16[256,320]{1,0:T(8,128)(2,1)S(1)}, bf16[256,320]{1,0:T(8,128)(2,1)S(1)}, u32[]{:S(2)}, u32[]{:S(2)}) collective-permute-start(bf16[256,320]{1,0:T(8,128)(2,1)S(1)} %copy.54), channel_id=1, source_target_pairs={{0,2},{1,3},{2,0},{3,1},{4,6},{5,7},{6,4},{7,5},{8,10},{9,11},{10,... | collective-permute-start | bytes 491528 | tf_op jit(solution)/shard_map/ppermute | solution.py:22
  9.5 3.1 %collective-permute-start = (bf16[256,320]{1,0:T(8,128)(2,1)S(1)}, bf16[256,320]{1,0:T(8,128)(2,1)S(1)}, u32[]{:S(2)}, u32[]{:S(2)}) collective-permute-start(bf16[256,320]{1,0:T(8,128)(2,1)S(1)} %copy.54), channel_id=1, source_target_pairs={{0,3},{1,0},{2,1},{3,2},{4,7},{5,4},{6,5},{7,6},{8,11},{9,8},{10,9... | collective-permute-start | bytes 491528 | tf_op jit(solution)/shard_map/ppermute | solution.py:22
  16.2 3.0 %concatenate.29 = bf16[256,2560]{1,0:T(8,128)(2,1)} concatenate(bf16[256,320]{1,0:T(8,128)(2,1)S(1)} %copy.54, bf16[256,320]{1,0:T(8,128)(2,1)S(1)} %collective-permute-done, bf16[256,320]{1,0:T(8,128)(2,1)S(1)} %collective-permute-done.1, bf16[256,320]{1,0:T(8,128)(2,1)S(1)} %collective-permute-done.2, bf16[256,320]{1,0:T(8,128)(2,1)S(1)} %copy.54, ...), dimensions={1} | concatenate | bytes 2621440 | tf_op jit(solution)/shard_map/concatenate | solution.py:56
  19.3 1.7 %convert_reduce_fusion = (f32[256]{0:T(256)S(1)}, bf16[256,1280]{1,0:T(8,128)(2,1)S(1)}) fusion(bf16[256,2560]{1,0:T(8,128)(2,1)} %concatenate.29, s32[]{:T(128)S(6)} %select_n.77), kind=kLoop, calls=%fused_computation.10 | loop fusion | flops 655104 | bytes 1311748 | tf_op jit(solution)/shard_map/reduce_sum | solution.py:27
  22.7 1.3 collective-permute-start.6
  24.0 7.4 %collective-permute-start.5 = (bf16[264,640]{0,1:T(8,128)(2,1)S(1)}, bf16[264,640]{0,1:T(8,128)(2,1)S(1)}, u32[]{:S(2)}, u32[]{:S(2)}) collective-permute-start(bf16[264,640]{0,1:T(8,128)(2,1)S(1)} %fusion.12), channel_id=1, source_target_pairs={{4,0},{8,4},{12,8},{16,12},{20,16},{24,20},{28,24},{32,28},{36,32}... | collective-permute-start | bytes 1013768 | tf_op jit(solution)/shard_map/ppermute | solution.py:16
  31.3 4.3 %collective-permute-start.4 = (bf16[264,640]{0,1:T(8,128)(2,1)S(1)}, bf16[264,640]{0,1:T(8,128)(2,1)S(1)}, u32[]{:S(2)}, u32[]{:S(2)}) collective-permute-start(bf16[264,640]{0,1:T(8,128)(2,1)S(1)} %fusion.12), channel_id=1, source_target_pairs={{0,8},{4,12},{8,16},{12,20},{16,24},{20,28},{24,32},{28,36},{32,40... | collective-permute-start | bytes 1013768 | tf_op jit(solution)/shard_map/ppermute | solution.py:16
  35.7 2.0 %collective-permute-start.3 = (bf16[264,640]{0,1:T(8,128)(2,1)S(1)}, bf16[264,640]{0,1:T(8,128)(2,1)S(1)}, u32[]{:S(2)}, u32[]{:S(2)}) collective-permute-start(bf16[264,640]{0,1:T(8,128)(2,1)S(1)} %fusion.12), channel_id=1, source_target_pairs={{0,4},{4,8},{8,12},{12,16},{16,20},{20,24},{24,28},{28,32},{32,36}... | collective-permute-start | bytes 1013768 | tf_op jit(solution)/shard_map/ppermute | solution.py:16
  38.8 13.1 %collective-permute-done.3 = bf16[264,640]{0,1:T(8,128)(2,1)S(1)} collective-permute-done((bf16[264,640]{0,1:T(8,128)(2,1)S(1)}, bf16[264,640]{0,1:T(8,128)(2,1)S(1)}, u32[]{:S(2)}, u32[]{:S(2)}) %collective-permute-start.3) | collective-permute-done | bytes 337952 | tf_op jit(solution)/shard_map/ppermute | solution.py:16
  53.8 2.9 %exponential_reduce_fusion = f32[4,256]{1,0:T(4,128)S(1)} fusion(bf16[256,4,80]{0,2,1:T(8,128)(2,1)} %bitcast.33, bf16[1280,4,80]{0,2,1:T(8,128)(2,1)S(1)} %bitcast.28, pred[256,1280]{1,0:T(8,128)(4,1)S(1)} %fusion.8), kind=kOutput, calls=%fused_computation.6 | convolution fusion | flops 214959360 | bytes 1314816 | tf_op jit(solution)/shard_map/sub | solution.py:91
  56.8 4.1 %fusion.9 = bf16[4,80,256]{2,1,0:T(8,128)(2,1)} fusion(bf16[1280,4,80]{0,2,1:T(8,128)(2,1)} %bitcast.30, f32[4,256]{1,0:T(4,128)S(1)} %exponential_reduce_fusion, bf16[256,4,80]{0,2,1:T(8,128)(2,1)} %bitcast.34, bf16[1280,4,80]{0,2,1:T(8,128)(2,1)S(1)} %bitcast.29, pred[256,1280]{1,0:T(8,128)(4,1)S(1)} %fusion.8), kind=kOutput, calls=%fused_computation.18 | convolution fusion | flops 426068224 | bytes 2297856 | tf_op jit(solution)/shard_map/hqk,khd->qhd/dot_general | solution.py:94
  63.2 1.7 %convolution_convert_fusion = bf16[256,1280]{1,0:T(8,128)(2,1)S(1)} fusion(bf16[320,1280]{1,0:T(8,128)(2,1)} %param.21, bf16[256,320]{1,0:T(8,128)(2,1)S(1)} %gather_fusion.1, pred[256]{0:T(512)(128)(4,1)S(1)} %compare_and_fusion), kind=kOutput, calls=%fused_computation.8 | convolution fusion | flops 210124800 | bytes 1638656 | tf_op jit(solution)/shard_map/dot_general | solution.py:102
  65.7 3.6 %collective-permute-start.7 = (bf16[64,1280]{1,0:T(8,128)(2,1)}, bf16[64,1280]{1,0:T(8,128)(2,1)S(1)}, u32[]{:S(2)}, u32[]{:S(2)}) collective-permute-start(bf16[64,1280]{1,0:T(8,128)(2,1)} %get-tuple-element.35), channel_id=1, source_target_pairs={{0,1},{1,2},{2,3},{3,0},{4,5},{5,6},{6,7},{7,4},{8,9},{9,10},{10,1... | collective-permute-start | bytes 491528 | tf_op jit(solution)/shard_map/ppermute | solution.py:22
  69.3 3.0 %collective-permute-start.9 = (bf16[64,1280]{1,0:T(8,128)(2,1)}, bf16[64,1280]{1,0:T(8,128)(2,1)S(1)}, u32[]{:S(2)}, u32[]{:S(2)}) collective-permute-start(bf16[64,1280]{1,0:T(8,128)(2,1)} %get-tuple-element.36), channel_id=1, source_target_pairs={{0,3},{1,0},{2,1},{3,2},{4,7},{5,4},{6,5},{7,6},{8,11},{9,8},{10,9... | collective-permute-start | bytes 491528 | tf_op jit(solution)/shard_map/ppermute | solution.py:22
  72.3 2.8 %collective-permute-start.8 = (bf16[64,1280]{1,0:T(8,128)(2,1)}, bf16[64,1280]{1,0:T(8,128)(2,1)}, u32[]{:S(2)}, u32[]{:S(2)}) collective-permute-start(bf16[64,1280]{1,0:T(8,128)(2,1)} %get-tuple-element.37), channel_id=1, source_target_pairs={{0,2},{1,3},{2,0},{3,1},{4,6},{5,7},{6,4},{7,5},{8,10},{9,11},{10,... | collective-permute-start | bytes 491528 | tf_op jit(solution)/shard_map/ppermute | solution.py:22
  75.9 1.3 collective-permute-done.9
  77.2 3.0 %collective-permute-done.8 = bf16[64,1280]{1,0:T(8,128)(2,1)} collective-permute-done((bf16[64,1280]{1,0:T(8,128)(2,1)}, bf16[64,1280]{1,0:T(8,128)(2,1)}, u32[]{:S(2)}, u32[]{:S(2)}) %collective-permute-start.8) | collective-permute-done | bytes 163872 | tf_op jit(solution)/shard_map/ppermute | solution.py:22
  82.3 2.3 %collective-permute-start.10 = (bf16[64,160]{1,0:T(8,128)(2,1)S(1)}, bf16[64,160]{1,0:T(8,128)(2,1)S(1)}, u32[]{:S(2)}, u32[]{:S(2)}) collective-permute-start(bf16[64,160]{1,0:T(8,128)(2,1)S(1)} %get-tuple-element.38), channel_id=1, source_target_pairs={{0,1},{1,2},{2,3},{3,0},{4,5},{5,6},{6,7},{7,4},{8,9},{9,10},{10,1... | collective-permute-start | bytes 61448 | tf_op jit(solution)/shard_map/ppermute | solution.py:22
  84.5 4.0 %collective-permute-start.11 = (bf16[64,160]{1,0:T(8,128)(2,1)S(1)}, bf16[64,160]{1,0:T(8,128)(2,1)S(1)}, u32[]{:S(2)}, u32[]{:S(2)}) collective-permute-start(bf16[64,160]{1,0:T(8,128)(2,1)S(1)} %get-tuple-element.39), channel_id=1, source_target_pairs={{0,2},{1,3},{2,0},{3,1},{4,6},{5,7},{6,4},{7,5},{8,10},{9,11},{10,... | collective-permute-start | bytes 61448 | tf_op jit(solution)/shard_map/ppermute | solution.py:22
  88.5 2.6 %collective-permute-start.12 = (bf16[64,160]{1,0:T(8,128)(2,1)S(1)}, bf16[64,160]{1,0:T(8,128)(2,1)S(1)}, u32[]{:S(2)}, u32[]{:S(2)}) collective-permute-start(bf16[64,160]{1,0:T(8,128)(2,1)S(1)} %get-tuple-element.40), channel_id=1, source_target_pairs={{0,3},{1,0},{2,1},{3,2},{4,7},{5,4},{6,5},{7,6},{8,11},{9,8},{10,9... | collective-permute-start | bytes 61448 | tf_op jit(solution)/shard_map/ppermute | solution.py:22
  91.5 2.0 %collective-permute-done.12 = bf16[64,160]{1,0:T(8,128)(2,1)S(1)} collective-permute-done((bf16[64,160]{1,0:T(8,128)(2,1)S(1)}, bf16[64,160]{1,0:T(8,128)(2,1)S(1)}, u32[]{:S(2)}, u32[]{:S(2)}) %collective-permute-start.12) | collective-permute-done | bytes 20512 | tf_op jit(solution)/shard_map/ppermute | solution.py:22
  94.5 34.3 %all_to_all.6 = bf16[128,2,240]{2,1,0:T(2,128)(2,1)S(1)} all-to-all(bf16[128,2,240]{2,1,0:T(2,128)(2,1)S(1)} %reshape.270), channel_id=1, replica_groups=mesh['seq'=128,'tp'=4] {'seq'}, dimensions={0} | all-to-all | bytes 245760 | tf_op jit(solution)/shard_map/all_to_all | solution.py:139
  (87 shorter events, 16.9 us)
Async XLA Ops:
  0.0 81.6 %copy-start = (bf16[1280,640]{1,0:T(8,128)(2,1)S(1)}, bf16[1280,640]{1,0:T(8,128)(2,1)}, u32[]{:S(2)}) copy-start(bf16[1280,640]{1,0:T(8,128)(2,1)} %param.25) | copy-start | bytes 4915204
  1.2 14.0 %collective-permute-start.2 = (bf16[256,320]{1,0:T(8,128)(2,1)S(1)}, bf16[256,320]{1,0:T(8,128)(2,1)S(1)}, u32[]{:S(2)}, u32[]{:S(2)}) collective-permute-start(bf16[256,320]{1,0:T(8,128)(2,1)S(1)} %copy.54), channel_id=1, source_target_pairs={{0,1},{1,2},{2,3},{3,0},{4,5},{5,6},{6,7},{7,4},{8,9},{9,10},{10,1... | collective-permute-start | bytes 491528 | tf_op jit(solution)/shard_map/ppermute | solution.py:22
  5.2 10.1 %collective-permute-start.1 = (bf16[256,320]{1,0:T(8,128)(2,1)S(1)}, bf16[256,320]{1,0:T(8,128)(2,1)S(1)}, u32[]{:S(2)}, u32[]{:S(2)}) collective-permute-start(bf16[256,320]{1,0:T(8,128)(2,1)S(1)} %copy.54), channel_id=1, source_target_pairs={{0,2},{1,3},{2,0},{3,1},{4,6},{5,7},{6,4},{7,5},{8,10},{9,11},{10,... | collective-permute-start | bytes 491528 | tf_op jit(solution)/shard_map/ppermute | solution.py:22
  9.5 6.7 %collective-permute-start = (bf16[256,320]{1,0:T(8,128)(2,1)S(1)}, bf16[256,320]{1,0:T(8,128)(2,1)S(1)}, u32[]{:S(2)}, u32[]{:S(2)}) collective-permute-start(bf16[256,320]{1,0:T(8,128)(2,1)S(1)} %copy.54), channel_id=1, source_target_pairs={{0,3},{1,0},{2,1},{3,2},{4,7},{5,4},{6,5},{7,6},{8,11},{9,8},{10,9... | collective-permute-start | bytes 491528 | tf_op jit(solution)/shard_map/ppermute | solution.py:22
  19.3 2.0 %copy-start.2 = (bf16[1280,320]{0,1:T(8,128)(2,1)S(1)}, bf16[1280,320]{0,1:T(8,128)(2,1)}, u32[]{:S(2)}) copy-start(bf16[1280,320]{0,1:T(8,128)(2,1)} %param.20) | copy-start | bytes 2457604
  19.3 2.0 %copy-start.5 = (f32[1280]{0:T(1024)S(1)}, f32[1280]{0:T(1024)}, u32[]{:S(2)}) copy-start(f32[1280]{0:T(1024)} %param.17) | copy-start | bytes 15364
  20.9 1.2 copy-start.3
  22.1 15.5 %copy-start.4 = (bf16[1280,320]{0,1:T(8,128)(2,1)S(1)}, bf16[1280,320]{0,1:T(8,128)(2,1)}, u32[]{:S(2)}) copy-start(bf16[1280,320]{0,1:T(8,128)(2,1)} %param.18) | copy-start | bytes 2457604
  22.7 29.4 %collective-permute-start.6 = (bf16[264,640]{0,1:T(8,128)(2,1)S(1)}, bf16[264,640]{0,1:T(8,128)(2,1)S(1)}, u32[]{:S(2)}, u32[]{:S(2)}) collective-permute-start(bf16[264,640]{0,1:T(8,128)(2,1)S(1)} %fusion.12), channel_id=1, source_target_pairs={{8,0},{12,4},{16,8},{20,12},{24,16},{28,20},{32,24},{36,28},{40,32... | collective-permute-start | bytes 1013768 | tf_op jit(solution)/shard_map/ppermute | solution.py:16
  24.0 28.0 %collective-permute-start.5 = (bf16[264,640]{0,1:T(8,128)(2,1)S(1)}, bf16[264,640]{0,1:T(8,128)(2,1)S(1)}, u32[]{:S(2)}, u32[]{:S(2)}) collective-permute-start(bf16[264,640]{0,1:T(8,128)(2,1)S(1)} %fusion.12), channel_id=1, source_target_pairs={{4,0},{8,4},{12,8},{16,12},{20,16},{24,20},{28,24},{32,28},{36,32}... | collective-permute-start | bytes 1013768 | tf_op jit(solution)/shard_map/ppermute | solution.py:16
  31.3 20.6 %collective-permute-start.4 = (bf16[264,640]{0,1:T(8,128)(2,1)S(1)}, bf16[264,640]{0,1:T(8,128)(2,1)S(1)}, u32[]{:S(2)}, u32[]{:S(2)}) collective-permute-start(bf16[264,640]{0,1:T(8,128)(2,1)S(1)} %fusion.12), channel_id=1, source_target_pairs={{0,8},{4,12},{8,16},{12,20},{16,24},{20,28},{24,32},{28,36},{32,40... | collective-permute-start | bytes 1013768 | tf_op jit(solution)/shard_map/ppermute | solution.py:16
  35.7 16.3 %collective-permute-start.3 = (bf16[264,640]{0,1:T(8,128)(2,1)S(1)}, bf16[264,640]{0,1:T(8,128)(2,1)S(1)}, u32[]{:S(2)}, u32[]{:S(2)}) collective-permute-start(bf16[264,640]{0,1:T(8,128)(2,1)S(1)} %fusion.12), channel_id=1, source_target_pairs={{0,4},{4,8},{8,12},{12,16},{16,20},{20,24},{24,28},{28,32},{32,36}... | collective-permute-start | bytes 1013768 | tf_op jit(solution)/shard_map/ppermute | solution.py:16
  63.2 12.0 %copy-start.6 = (s32[64]{0:T(128)S(1)}, s32[64]{0:T(128)}, u32[]{:S(2)}) copy-start(s32[64]{0:T(128)} %param.27) | copy-start | bytes 772
  65.7 15.9 %copy-start.1 = (f32[1280]{0:T(1024)S(1)}, f32[1280]{0:T(1024)}, u32[]{:S(2)}) copy-start(f32[1280]{0:T(1024)} %param.24) | copy-start | bytes 15364
  65.7 10.2 %collective-permute-start.7 = (bf16[64,1280]{1,0:T(8,128)(2,1)}, bf16[64,1280]{1,0:T(8,128)(2,1)S(1)}, u32[]{:S(2)}, u32[]{:S(2)}) collective-permute-start(bf16[64,1280]{1,0:T(8,128)(2,1)} %get-tuple-element.35), channel_id=1, source_target_pairs={{0,1},{1,2},{2,3},{3,0},{4,5},{5,6},{6,7},{7,4},{8,9},{9,10},{10,1... | collective-permute-start | bytes 491528 | tf_op jit(solution)/shard_map/ppermute | solution.py:22
  69.3 7.9 %collective-permute-start.9 = (bf16[64,1280]{1,0:T(8,128)(2,1)}, bf16[64,1280]{1,0:T(8,128)(2,1)S(1)}, u32[]{:S(2)}, u32[]{:S(2)}) collective-permute-start(bf16[64,1280]{1,0:T(8,128)(2,1)} %get-tuple-element.36), channel_id=1, source_target_pairs={{0,3},{1,0},{2,1},{3,2},{4,7},{5,4},{6,5},{7,6},{8,11},{9,8},{10,9... | collective-permute-start | bytes 491528 | tf_op jit(solution)/shard_map/ppermute | solution.py:22
  72.3 7.9 %collective-permute-start.8 = (bf16[64,1280]{1,0:T(8,128)(2,1)}, bf16[64,1280]{1,0:T(8,128)(2,1)}, u32[]{:S(2)}, u32[]{:S(2)}) collective-permute-start(bf16[64,1280]{1,0:T(8,128)(2,1)} %get-tuple-element.37), channel_id=1, source_target_pairs={{0,2},{1,3},{2,0},{3,1},{4,6},{5,7},{6,4},{7,5},{8,10},{9,11},{10,... | collective-permute-start | bytes 491528 | tf_op jit(solution)/shard_map/ppermute | solution.py:22
  82.3 9.3 %collective-permute-start.10 = (bf16[64,160]{1,0:T(8,128)(2,1)S(1)}, bf16[64,160]{1,0:T(8,128)(2,1)S(1)}, u32[]{:S(2)}, u32[]{:S(2)}) collective-permute-start(bf16[64,160]{1,0:T(8,128)(2,1)S(1)} %get-tuple-element.38), channel_id=1, source_target_pairs={{0,1},{1,2},{2,3},{3,0},{4,5},{5,6},{6,7},{7,4},{8,9},{9,10},{10,1... | collective-permute-start | bytes 61448 | tf_op jit(solution)/shard_map/ppermute | solution.py:22
  84.5 7.0 %collective-permute-start.11 = (bf16[64,160]{1,0:T(8,128)(2,1)S(1)}, bf16[64,160]{1,0:T(8,128)(2,1)S(1)}, u32[]{:S(2)}, u32[]{:S(2)}) collective-permute-start(bf16[64,160]{1,0:T(8,128)(2,1)S(1)} %get-tuple-element.39), channel_id=1, source_target_pairs={{0,2},{1,3},{2,0},{3,1},{4,6},{5,7},{6,4},{7,5},{8,10},{9,11},{10,... | collective-permute-start | bytes 61448 | tf_op jit(solution)/shard_map/ppermute | solution.py:22
  88.5 5.0 %collective-permute-start.12 = (bf16[64,160]{1,0:T(8,128)(2,1)S(1)}, bf16[64,160]{1,0:T(8,128)(2,1)S(1)}, u32[]{:S(2)}, u32[]{:S(2)}) collective-permute-start(bf16[64,160]{1,0:T(8,128)(2,1)S(1)} %get-tuple-element.40), channel_id=1, source_target_pairs={{0,3},{1,0},{2,1},{3,2},{4,7},{5,4},{6,5},{7,6},{8,11},{9,8},{10,9... | collective-permute-start | bytes 61448 | tf_op jit(solution)/shard_map/ppermute | solution.py:22

commit v3 on v2

--- a/solution.py
+++ b/solution.py
@@ -13,12 +13,6 @@
 def from_behind(shard, axis, by):
     length = lax.axis_size(axis)
     pairs = [(i, i + by) for i in range(length) if 0 <= i + by < length]
-    return lax.ppermute(shard, axis, pairs)
-
-
-def around(shard, axis, by):
-    length = lax.axis_size(axis)
-    pairs = [(i, (i + by) % length) for i in range(length)]
     return lax.ppermute(shard, axis, pairs)
 
 
@@ -52,10 +46,9 @@
     position = lax.axis_index("tp")
     seq_index = lax.axis_index("seq")
 
-    blocks = [tokens] + [around(tokens, "tp", -k) for k in range(1, tp_size)]
-    rotated = jnp.concatenate(blocks + blocks, axis=1)
-    start = ((tp_size - position) % tp_size) * tokens.shape[1]
-    gathered = lax.dynamic_slice_in_dim(rotated, start, tp_size * tokens.shape[1], 1)
+    gathered = lax.all_to_all(
+        jnp.concatenate([tokens] * tp_size, axis=1), "tp", 1, 1, tiled=True
+    )
 
     normed = layer_norm(gathered, first_gain).astype(jnp.bfloat16)
     queries = jnp.dot(normed, w_query, preferred_element_type=jnp.float32).astype(jnp.bfloat16)
@@ -95,28 +88,22 @@
     attended = attended.reshape(row_count, local_width).astype(jnp.bfloat16)
 
     local_index = merge_index - seq_index * row_count
-    rotated_index = jnp.concatenate([local_index, local_index], axis=1)
-    rotated_index = lax.dynamic_slice_in_dim(rotated_index, position, tp_size, 1)
-    order = rotated_index.T.reshape(row_count)
+    order = local_index.T.reshape(row_count)
     attended_sorted = jnp.take(attended, order, axis=0)
     partial_sum = jnp.dot(attended_sorted, w_out, preferred_element_type=jnp.float32)
     partial_sum = partial_sum.astype(jnp.bfloat16)
     chunk = row_count // tp_size
-    mixed_sum = partial_sum[:chunk].astype(jnp.float32)
-    for k in range(1, tp_size):
-        mixed_sum = mixed_sum + around(partial_sum[k * chunk:(k + 1) * chunk], "tp", k).astype(jnp.float32)
-    column = rotated_index[:, 0]
+    pieces = lax.all_to_all(partial_sum, "tp", 0, 0, tiled=True)
+    mixed_sum = jnp.sum(pieces.reshape(tp_size, chunk, -1).astype(jnp.float32), axis=0)
+    column = lax.dynamic_slice_in_dim(local_index, position, 1, 1)[:, 0]
     residual = jnp.take(gathered, column, axis=0)
     updated = residual.astype(jnp.float32) + mixed_sum
     picked = layer_norm(updated, merge_gain).astype(jnp.bfloat16)
     partial_proj = jnp.dot(picked, w_merge, preferred_element_type=jnp.float32)
     partial_proj = partial_proj.astype(jnp.bfloat16)
     width = partial_proj.shape[1] // tp_size
-    doubled = jnp.concatenate([partial_proj, partial_proj], axis=1)
-    projected = lax.dynamic_slice_in_dim(doubled, position * width, width, 1).astype(jnp.float32)
-    for k in range(1, tp_size):
-        piece = lax.dynamic_slice_in_dim(doubled, (position + k) * width, width, 1)
-        projected = projected + around(piece, "tp", k).astype(jnp.float32)
+    proj_pieces = lax.all_to_all(partial_proj, "tp", 1, 0, tiled=True)
+    projected = jnp.sum(proj_pieces.reshape(tp_size, chunk, width).astype(jnp.float32), axis=0)
     projected = projected.astype(jnp.bfloat16)
     slot_count = projected.shape[0]
 

time: 131 us -> 120 us (0.916)
  starting transfers between devices: 44.6 us -> 28.5 us
  waiting for transfers between devices: 20.3 us -> 31.2 us
  local copies, waits for them, and re-layouts: 10.8 us -> 7.06 us
    ppermute x9 -> x0, starting transfers between devices: 29.7 us -> none  [around(): return lax.ppermute(shard, axis, pairs)]
    all_to_all x0 -> x3, waiting for transfers between devices: none -> 18.2 us  [the longest x1 7.26 us: body(): lax.all_to_all(jnp.concatenate([tokens] * tp_size, axis=1), 'tp', 1, 1, t...]
    all_to_all x0 -> x3, starting transfers between devices: none -> 12.3 us  [the longest x1 4.83 us: body(): lax.all_to_all(jnp.concatenate([tokens] * tp_size, axis=1), 'tp', 1, 1, t...]
    ppermute x9 -> x0, waiting for transfers between devices: 7.27 us -> none  [around(): return lax.ppermute(shard, axis, pairs)]
    concatenate x1 -> x0, local copies, waits for them, and re-layouts: 3.04 us -> none  [body(): rotated = jnp.concatenate(blocks + blocks, axis=1)]
    reduce_sum x2, other arithmetic: 2.81 us -> 0.4 us  [layer_norm(): row_mean = jnp.mean(activations, axis=-1, keepdims=True)]
    concatenate x2 -> x1, other arithmetic: 0.2 us -> 2.14 us  [body(): jnp.concatenate([tokens] * tp_size, axis=1)]
  transfers between devices with their start and end apart: 13 -> 7, of which waited for: 5 -> 4; matrix products, arithmetic and copies ran while one was open for 4% -> 3% of each run, Pallas kernels for 0% -> 0%
where the time goes in v3:
time: 120 us; the launch traced here: 119 us
  blocking collectives  33.8 us (28%)
  waiting for transfers between devices  31.2 us (26%)
  starting transfers between devices  28.5 us (24%)
  matrix products  11.9 us (10%)
  local copies, waits for them, and re-layouts  7.06 us (6%)
  other arithmetic  6.07 us (5%)
    all_to_all x1, blocking collectives, body(): lax.all_to_all(send_buf, 'seq', 0, 0, tiled=True)  33.8 us
    ppermute x4, starting transfers between devices, from_behind(): return lax.ppermute(shard, axis, pairs)  16.2 us
    ppermute x4, waiting for transfers between devices, from_behind(): return lax.ppermute(shard, axis, pairs)  13.1 us
    all_to_all x1, waiting for transfers between devices, body(): lax.all_to_all(jnp.concatenate([tokens] * tp_size, axis=1), 'tp', 1, 1, t...  7.26 us
    all_to_all x1, waiting for transfers between devices, body(): pieces = lax.all_to_all(partial_sum, 'tp', 0, 0, tiled=True)  6.48 us
    all_to_all x1, starting transfers between devices, body(): lax.all_to_all(jnp.concatenate([tokens] * tp_size, axis=1), 'tp', 1, 1, t...  4.83 us
    all_to_all x1, waiting for transfers between devices, body(): proj_pieces = lax.all_to_all(partial_proj, 'tp', 1, 0, tiled=True)  4.42 us
    all_to_all x1, starting transfers between devices, body(): pieces = lax.all_to_all(partial_sum, 'tp', 0, 0, tiled=True)  4.15 us
  transfers between devices with their start and end apart: 7, of which 4 were waited for; matrix products, arithmetic and copies ran while one was open for 3% of the time, Pallas kernels for 0%

profile of v3, /device:TPU:1, one launch (start us, length us, event | category | flops | bytes accessed | tf_op | source)
XLA Modules:
  0.0 119.0 jit_solution(5586977528392365858)
XLA Ops:
  0.0 2.1 %pad_maximum_fusion = bf16[256,1280]{0,1:T(8,128)(2,1)} fusion(bf16[256,320]{0,1:T(8,128)(2,1)} %param.16), kind=kLoop, calls=%fused_computation.26 | loop fusion | flops 2621440 | bytes 819200 | tf_op jit(solution)/shard_map/concatenate | solution.py:50
  2.2 4.8 %all-to-all-start = ((bf16[256,4,320]{0,2,1:T(8,128)(2,1)}), bf16[256,4,320]{0,2,1:T(8,128)(2,1)S(1)}, u32[]{:S(2)}, u32[]{:S(2)}) async-start(bf16[256,4,320]{0,2,1:T(8,128)(2,1)} %bitcast.1), calls=%async_computation | async-start | bytes 1310720 | tf_op jit(solution)/shard_map/all_to_all | solution.py:49
  7.4 7.3 %all-to-all-done = bf16[256,4,320]{0,2,1:T(8,128)(2,1)S(1)} async-done(((bf16[256,4,320]{0,2,1:T(8,128)(2,1)}), bf16[256,4,320]{0,2,1:T(8,128)(2,1)S(1)}, u32[]{:S(2)}, u32[]{:S(2)}) %all-to-all-start) | async-done | bytes 655392 | tf_op jit(solution)/shard_map/all_to_all | solution.py:49
  16.7 1.3 %collective-permute-start.3 = (bf16[264,640]{0,1:T(8,128)(2,1)S(1)}, bf16[264,640]{0,1:T(8,128)(2,1)S(1)}, u32[]{:S(2)}, u32[]{:S(2)}) collective-permute-start(bf16[264,640]{0,1:T(8,128)(2,1)S(1)} %fusion.9), channel_id=1, source_target_pairs={{8,0},{12,4},{16,8},{20,12},{24,16},{28,20},{32,24},{36,28},{40,32... | collective-permute-start | bytes 1013768 | tf_op jit(solution)/shard_map/ppermute | solution.py:16
  18.0 8.5 %collective-permute-start.2 = (bf16[264,640]{0,1:T(8,128)(2,1)S(1)}, bf16[264,640]{0,1:T(8,128)(2,1)S(1)}, u32[]{:S(2)}, u32[]{:S(2)}) collective-permute-start(bf16[264,640]{0,1:T(8,128)(2,1)S(1)} %fusion.9), channel_id=1, source_target_pairs={{4,0},{8,4},{12,8},{16,12},{20,16},{24,20},{28,24},{32,28},{36,32}... | collective-permute-start | bytes 1013768 | tf_op jit(solution)/shard_map/ppermute | solution.py:16
  26.5 4.3 %collective-permute-start.1 = (bf16[264,640]{0,1:T(8,128)(2,1)S(1)}, bf16[264,640]{0,1:T(8,128)(2,1)S(1)}, u32[]{:S(2)}, u32[]{:S(2)}) collective-permute-start(bf16[264,640]{0,1:T(8,128)(2,1)S(1)} %fusion.9), channel_id=1, source_target_pairs={{0,8},{4,12},{8,16},{12,20},{16,24},{20,28},{24,32},{28,36},{32,40... | collective-permute-start | bytes 1013768 | tf_op jit(solution)/shard_map/ppermute | solution.py:16
  30.8 2.1 %collective-permute-start = (bf16[264,640]{0,1:T(8,128)(2,1)S(1)}, bf16[264,640]{0,1:T(8,128)(2,1)S(1)}, u32[]{:S(2)}, u32[]{:S(2)}) collective-permute-start(bf16[264,640]{0,1:T(8,128)(2,1)S(1)} %fusion.9), channel_id=1, source_target_pairs={{0,4},{4,8},{8,12},{12,16},{16,20},{20,24},{24,28},{28,32},{32,36}... | collective-permute-start | bytes 1013768 | tf_op jit(solution)/shard_map/ppermute | solution.py:16
  32.9 1.1 convolution_convert_fusion.1
  34.0 13.1 %collective-permute-done = bf16[264,640]{0,1:T(8,128)(2,1)S(1)} collective-permute-done((bf16[264,640]{0,1:T(8,128)(2,1)S(1)}, bf16[264,640]{0,1:T(8,128)(2,1)S(1)}, u32[]{:S(2)}, u32[]{:S(2)}) %collective-permute-start) | collective-permute-done | bytes 337952 | tf_op jit(solution)/shard_map/ppermute | solution.py:16
  47.2 1.0 fusion.44
  49.0 2.9 %exponential_reduce_fusion = f32[4,256]{1,0:T(4,128)S(1)} fusion(bf16[256,4,80]{0,2,1:T(8,128)(2,1)} %bitcast.39, bf16[1280,4,80]{0,2,1:T(8,128)(2,1)S(1)} %bitcast.36, pred[256,1280]{1,0:T(8,128)(4,1)S(1)} %fusion.5), kind=kOutput, calls=%fused_computation.6 | convolution fusion | flops 214959360 | bytes 1314816 | tf_op jit(solution)/shard_map/sub | solution.py:84
  51.9 4.1 %fusion.6 = bf16[4,80,256]{2,1,0:T(8,128)(2,1)} fusion(bf16[1280,4,80]{0,2,1:T(8,128)(2,1)} %bitcast.38, f32[4,256]{1,0:T(4,128)S(1)} %exponential_reduce_fusion, bf16[256,4,80]{0,2,1:T(8,128)(2,1)} %bitcast.40, bf16[1280,4,80]{0,2,1:T(8,128)(2,1)S(1)} %bitcast.37, pred[256,1280]{1,0:T(8,128)(4,1)S(1)} %fusion.5), kind=kOutput, calls=%fused_computation.17 | convolution fusion | flops 426068224 | bytes 2297856 | tf_op jit(solution)/shard_map/hqk,khd->qhd/dot_general | solution.py:87
  56.1 1.2 copy.39
  57.2 1.2 gather_fusion.1
  58.4 1.4 %convolution_convert_fusion = bf16[256,1280]{1,0:T(8,128)(2,1)} fusion(bf16[320,1280]{1,0:T(8,128)(2,1)S(1)} %copy-done.4, bf16[256,320]{1,0:T(8,128)(2,1)S(1)} %gather_fusion.1, pred[256]{0:T(512)(128)(4,1)S(1)} %compare_and_fusion), kind=kOutput, calls=%fused_computation.8 | convolution fusion | flops 210124800 | bytes 1638656 | tf_op jit(solution)/shard_map/dot_general | solution.py:93
  59.8 4.2 %all-to-all-start.1 = ((bf16[4,64,1280]{2,1,0:T(8,128)(2,1)}), bf16[4,64,1280]{2,1,0:T(8,128)(2,1)}, u32[]{:S(2)}, u32[]{:S(2)}) async-start(bf16[4,64,1280]{2,1,0:T(8,128)(2,1)} %bitcast.11), calls=%async_computation.1 | async-start | bytes 1310720 | tf_op jit(solution)/shard_map/all_to_all | solution.py:96
  64.5 0.7 gather_fusion
  65.2 6.5 %all-to-all-done.1 = bf16[4,64,1280]{2,1,0:T(8,128)(2,1)} async-done(((bf16[4,64,1280]{2,1,0:T(8,128)(2,1)}), bf16[4,64,1280]{2,1,0:T(8,128)(2,1)}, u32[]{:S(2)}, u32[]{:S(2)}) %all-to-all-start.1) | async-done | bytes 655392 | tf_op jit(solution)/shard_map/all_to_all | solution.py:96
  71.7 1.2 %convert_reduce_fusion.1 = f32[64,1280]{1,0:T(8,128)S(1)} fusion(bf16[4,64,1280]{2,1,0:T(8,128)(2,1)} %all-to-all-done.1), kind=kLoop, calls=%fused_computation.13 | loop fusion | flops 573440 | bytes 983040 | tf_op jit(solution)/shard_map/reduce_sum | solution.py:97
  74.0 0.7 copy.40
  74.6 3.3 %all-to-all-start.2 = ((bf16[64,4,160]{2,0,1:T(8,128)(2,1)}), bf16[64,4,160]{2,0,1:T(8,128)(2,1)S(1)}, u32[]{:S(2)}, u32[]{:S(2)}) async-start(bf16[64,4,160]{2,0,1:T(8,128)(2,1)} %copy.40), calls=%async_computation.2 | async-start | bytes 262144 | tf_op jit(solution)/shard_map/all_to_all | solution.py:105
  78.3 4.4 %all-to-all-done.2 = bf16[64,4,160]{2,0,1:T(8,128)(2,1)S(1)} async-done(((bf16[64,4,160]{2,0,1:T(8,128)(2,1)}), bf16[64,4,160]{2,0,1:T(8,128)(2,1)S(1)}, u32[]{:S(2)}, u32[]{:S(2)}) %all-to-all-start.2) | async-done | bytes 81952 | tf_op jit(solution)/shard_map/all_to_all | solution.py:105
  83.6 33.8 %all_to_all.40 = bf16[128,2,240]{2,1,0:T(2,128)(2,1)S(1)} all-to-all(bf16[128,2,240]{2,1,0:T(2,128)(2,1)S(1)} %reshape.286), channel_id=1, replica_groups=mesh['seq'=128,'tp'=4] {'seq'}, dimensions={0} | all-to-all | bytes 245760 | tf_op jit(solution)/shard_map/all_to_all | solution.py:126
  118.2 0.8 convolution_convert_fusion.6
  (83 shorter events, 6.7 us)
Async XLA Ops:
  0.0 73.4 %copy-start = (bf16[1280,640]{1,0:T(8,128)(2,1)S(1)}, bf16[1280,640]{1,0:T(8,128)(2,1)}, u32[]{:S(2)}) copy-start(bf16[1280,640]{1,0:T(8,128)(2,1)} %param.25) | copy-start | bytes 4915204
  0.0 7.0 %copy-start.10 = (s32[64]{0:T(128)S(1)}, s32[64]{0:T(128)}, u32[]{:S(2)}) copy-start(s32[64]{0:T(128)} %param.27) | copy-start | bytes 772
  0.0 7.0 %copy-start.7 = (s32[64,4]{0,1:T(4,128)S(1)}, s32[64,4]{0,1:T(4,128)}, u32[]{:S(2)}) copy-start(s32[64,4]{0,1:T(4,128)} %param.26) | copy-start | bytes 3076
  0.0 7.1 %copy-start.8 = (s32[256]{0:T(256)S(1)}, s32[256]{0:T(256)}, u32[]{:S(2)}) copy-start(s32[256]{0:T(256)} %param.23) | copy-start | bytes 3076
  0.0 7.1 %copy-start.9 = (s32[256]{0:T(256)S(1)}, s32[256]{0:T(256)}, u32[]{:S(2)}) copy-start(s32[256]{0:T(256)} %param.22) | copy-start | bytes 3076
  0.0 15.1 %copy-start.5 = (f32[1280]{0:T(1024)S(1)}, f32[1280]{0:T(1024)}, u32[]{:S(2)}) copy-start(f32[1280]{0:T(1024)} %param.17) | copy-start | bytes 15364
  2.2 12.5 %all-to-all-start = ((bf16[256,4,320]{0,2,1:T(8,128)(2,1)}), bf16[256,4,320]{0,2,1:T(8,128)(2,1)S(1)}, u32[]{:S(2)}, u32[]{:S(2)}) async-start(bf16[256,4,320]{0,2,1:T(8,128)(2,1)} %bitcast.1), calls=%async_computation | async-start | bytes 1310720 | tf_op jit(solution)/shard_map/all_to_all | solution.py:49
  7.0 8.3 %copy-start.1 = (bf16[1280,320]{0,1:T(8,128)(2,1)S(1)}, bf16[1280,320]{0,1:T(8,128)(2,1)}, u32[]{:S(2)}) copy-start(bf16[1280,320]{0,1:T(8,128)(2,1)} %param.19) | copy-start | bytes 2457604
  15.1 1.1 copy-start.2
  16.2 16.7 %copy-start.3 = (bf16[1280,320]{0,1:T(8,128)(2,1)S(1)}, bf16[1280,320]{0,1:T(8,128)(2,1)}, u32[]{:S(2)}) copy-start(bf16[1280,320]{0,1:T(8,128)(2,1)} %param.18) | copy-start | bytes 2457604
  16.7 30.5 %collective-permute-start.3 = (bf16[264,640]{0,1:T(8,128)(2,1)S(1)}, bf16[264,640]{0,1:T(8,128)(2,1)S(1)}, u32[]{:S(2)}, u32[]{:S(2)}) collective-permute-start(bf16[264,640]{0,1:T(8,128)(2,1)S(1)} %fusion.9), channel_id=1, source_target_pairs={{8,0},{12,4},{16,8},{20,12},{24,16},{28,20},{32,24},{36,28},{40,32... | collective-permute-start | bytes 1013768 | tf_op jit(solution)/shard_map/ppermute | solution.py:16
  18.0 29.2 %collective-permute-start.2 = (bf16[264,640]{0,1:T(8,128)(2,1)S(1)}, bf16[264,640]{0,1:T(8,128)(2,1)S(1)}, u32[]{:S(2)}, u32[]{:S(2)}) collective-permute-start(bf16[264,640]{0,1:T(8,128)(2,1)S(1)} %fusion.9), channel_id=1, source_target_pairs={{4,0},{8,4},{12,8},{16,12},{20,16},{24,20},{28,24},{32,28},{36,32}... | collective-permute-start | bytes 1013768 | tf_op jit(solution)/shard_map/ppermute | solution.py:16
  26.5 20.6 %collective-permute-start.1 = (bf16[264,640]{0,1:T(8,128)(2,1)S(1)}, bf16[264,640]{0,1:T(8,128)(2,1)S(1)}, u32[]{:S(2)}, u32[]{:S(2)}) collective-permute-start(bf16[264,640]{0,1:T(8,128)(2,1)S(1)} %fusion.9), channel_id=1, source_target_pairs={{0,8},{4,12},{8,16},{12,20},{16,24},{20,28},{24,32},{28,36},{32,40... | collective-permute-start | bytes 1013768 | tf_op jit(solution)/shard_map/ppermute | solution.py:16
  30.8 16.3 %collective-permute-start = (bf16[264,640]{0,1:T(8,128)(2,1)S(1)}, bf16[264,640]{0,1:T(8,128)(2,1)S(1)}, u32[]{:S(2)}, u32[]{:S(2)}) collective-permute-start(bf16[264,640]{0,1:T(8,128)(2,1)S(1)} %fusion.9), channel_id=1, source_target_pairs={{0,4},{4,8},{8,12},{12,16},{16,20},{20,24},{24,28},{28,32},{32,36}... | collective-permute-start | bytes 1013768 | tf_op jit(solution)/shard_map/ppermute | solution.py:16
  56.1 2.3 %copy-start.4 = (bf16[320,1280]{1,0:T(8,128)(2,1)S(1)}, bf16[320,1280]{1,0:T(8,128)(2,1)}, u32[]{:S(2)}) copy-start(bf16[320,1280]{1,0:T(8,128)(2,1)} %param.21) | copy-start | bytes 2457604
  59.8 11.9 %all-to-all-start.1 = ((bf16[4,64,1280]{2,1,0:T(8,128)(2,1)}), bf16[4,64,1280]{2,1,0:T(8,128)(2,1)}, u32[]{:S(2)}, u32[]{:S(2)}) async-start(bf16[4,64,1280]{2,1,0:T(8,128)(2,1)} %bitcast.11), calls=%async_computation.1 | async-start | bytes 1310720 | tf_op jit(solution)/shard_map/all_to_all | solution.py:96
  64.5 8.9 %copy-start.6 = (f32[1280]{0:T(1024)S(1)}, f32[1280]{0:T(1024)}, u32[]{:S(2)}) copy-start(f32[1280]{0:T(1024)} %param.24) | copy-start | bytes 15364
  74.6 8.1 %all-to-all-start.2 = ((bf16[64,4,160]{2,0,1:T(8,128)(2,1)}), bf16[64,4,160]{2,0,1:T(8,128)(2,1)S(1)}, u32[]{:S(2)}, u32[]{:S(2)}) async-start(bf16[64,4,160]{2,0,1:T(8,128)(2,1)} %copy.40), calls=%async_computation.2 | async-start | bytes 262144 | tf_op jit(solution)/shard_map/all_to_all | solution.py:105

commit v4 on v3

--- a/solution.py
+++ b/solution.py
@@ -102,10 +102,7 @@
     partial_proj = jnp.dot(picked, w_merge, preferred_element_type=jnp.float32)
     partial_proj = partial_proj.astype(jnp.bfloat16)
     width = partial_proj.shape[1] // tp_size
-    proj_pieces = lax.all_to_all(partial_proj, "tp", 1, 0, tiled=True)
-    projected = jnp.sum(proj_pieces.reshape(tp_size, chunk, width).astype(jnp.float32), axis=0)
-    projected = projected.astype(jnp.bfloat16)
-    slot_count = projected.shape[0]
+    slot_count = partial_proj.shape[0]
 
     owner = destination // slot_count
     slot = destination - owner * slot_count
@@ -116,16 +113,21 @@
     send_pos = owner * CAP + rank
     target = jnp.arange(seq_size * CAP)
     send_hot = (send_pos[None, :] == target[:, None]).astype(jnp.bfloat16)
-    send_rows = jnp.dot(send_hot, projected, preferred_element_type=jnp.float32)
-    send_rows = send_rows.astype(jnp.bfloat16).reshape(seq_size, CAP, width)
+    send_rows = jnp.dot(send_hot, partial_proj, preferred_element_type=jnp.float32)
+    send_rows = send_rows.astype(jnp.bfloat16).reshape(seq_size, CAP, tp_size, width)
+    send_rows = jnp.transpose(send_rows, (0, 2, 1, 3))
     slot_code = (slot + 1).astype(jnp.float32)
     send_slot = jnp.dot(send_hot.astype(jnp.float32), slot_code, precision=lax.Precision.HIGHEST)
     slot_row = jnp.zeros((seq_size, 1, width), jnp.bfloat16)
     slot_row = slot_row.at[:, 0, :CAP].set(send_slot.reshape(seq_size, CAP).astype(jnp.bfloat16))
-    send_buf = jnp.concatenate([send_rows, slot_row], axis=1).reshape(seq_size * (CAP + 1), width)
-    recv = lax.all_to_all(send_buf, "seq", 0, 0, tiled=True).reshape(seq_size, CAP + 1, width)
-    recv_rows = recv[:, :CAP, :].reshape(seq_size * CAP, width)
-    recv_slot = recv[:, CAP, :CAP].reshape(seq_size * CAP).astype(jnp.int32) - 1
+    slot_row = jnp.broadcast_to(slot_row[:, None], (seq_size, tp_size, 1, width))
+    send_buf = jnp.concatenate([send_rows, slot_row], axis=2)
+    send_buf = send_buf.reshape(seq_size * tp_size * (CAP + 1), width)
+    recv = lax.all_to_all(send_buf, ("seq", "tp"), 0, 0, tiled=True)
+    recv = recv.reshape(seq_size, tp_size, CAP + 1, width)
+    recv_rows = jnp.sum(recv[:, :, :CAP, :].astype(jnp.float32), axis=1)
+    recv_rows = recv_rows.astype(jnp.bfloat16).reshape(seq_size * CAP, width)
+    recv_slot = recv[:, 0, CAP, :CAP].reshape(seq_size * CAP).astype(jnp.int32) - 1
     recv_hot = (recv_slot[None, :] == lane[:, None]).astype(jnp.bfloat16)
     delivered = jnp.dot(recv_hot, recv_rows, preferred_element_type=jnp.float32)
     return delivered.astype(jnp.bfloat16)

time: 120 us -> 126 us (1.050)
  blocking collectives: 33.8 us -> 44 us
  waiting for transfers between devices: 31.2 us -> 26.4 us
  starting transfers between devices: 28.5 us -> 25.2 us
  local copies, waits for them, and re-layouts: 7.06 us -> 10.1 us
    all_to_all x1, blocking collectives: 33.8 us -> 44 us  [body(): recv = lax.all_to_all(send_buf, ('seq', 'tp'), 0, 0, tiled=True)]
    all_to_all x1 -> x0, waiting for transfers between devices: 4.42 us -> none  [body(): proj_pieces = lax.all_to_all(partial_proj, 'tp', 1, 0, tiled=True)]
    all_to_all x1 -> x0, starting transfers between devices: 3.32 us -> none  [body(): proj_pieces = lax.all_to_all(partial_proj, 'tp', 1, 0, tiled=True)]
    unnamed x30, local copies, waits for them, and re-layouts: 0.96 us -> 4.18 us
  transfers between devices with their start and end apart: 7 -> 6, of which waited for: 4 -> 3; matrix products, arithmetic and copies ran while one was open for 3% -> 2% of each run, Pallas kernels for 0% -> 0%
where the time goes in v4:
time: 126 us; the launch traced here: 125 us
  blocking collectives  44 us (35%)
  waiting for transfers between devices  26.4 us (21%)
  starting transfers between devices  25.2 us (20%)
  matrix products  11.9 us (9%)
  local copies, waits for them, and re-layouts  10.1 us (8%)
  other arithmetic  7.1 us (6%)
    all_to_all x1, blocking collectives, body(): recv = lax.all_to_all(send_buf, ('seq', 'tp'), 0, 0, tiled=True)  44 us
    ppermute x4, starting transfers between devices, from_behind(): return lax.ppermute(shard, axis, pairs)  16.2 us
    ppermute x4, waiting for transfers between devices, from_behind(): return lax.ppermute(shard, axis, pairs)  13.1 us
    all_to_all x1, waiting for transfers between devices, body(): lax.all_to_all(jnp.concatenate([tokens] * tp_size, axis=1), 'tp', 1, 1, t...  6.71 us
    all_to_all x1, waiting for transfers between devices, body(): pieces = lax.all_to_all(partial_sum, 'tp', 0, 0, tiled=True)  6.64 us
    all_to_all x1, starting transfers between devices, body(): lax.all_to_all(jnp.concatenate([tokens] * tp_size, axis=1), 'tp', 1, 1, t...  4.83 us
    unnamed x30, local copies, waits for them, and re-layouts  4.18 us
    all_to_all x1, starting transfers between devices, body(): pieces = lax.all_to_all(partial_sum, 'tp', 0, 0, tiled=True)  4.15 us
  transfers between devices with their start and end apart: 6, of which 3 were waited for; matrix products, arithmetic and copies ran while one was open for 2% of the time, Pallas kernels for 0%

profile of v4, /device:TPU:1, one launch (start us, length us, event | category | flops | bytes accessed | tf_op | source)
XLA Modules:
  0.0 125.1 jit_solution(8909314533098550864)
XLA Ops:
  0.0 2.1 %pad_maximum_fusion.1 = bf16[256,1280]{0,1:T(8,128)(2,1)} fusion(bf16[256,320]{0,1:T(8,128)(2,1)} %param.16), kind=kLoop, calls=%fused_computation.27 | loop fusion | flops 2621440 | bytes 819200 | tf_op jit(solution)/shard_map/concatenate | solution.py:50
  2.2 4.8 %all-to-all-start = ((bf16[256,4,320]{0,2,1:T(8,128)(2,1)}), bf16[256,4,320]{0,2,1:T(8,128)(2,1)S(1)}, u32[]{:S(2)}, u32[]{:S(2)}) async-start(bf16[256,4,320]{0,2,1:T(8,128)(2,1)} %bitcast.1), calls=%async_computation | async-start | bytes 1310720 | tf_op jit(solution)/shard_map/all_to_all | solution.py:49
  7.9 6.7 %all-to-all-done = bf16[256,4,320]{0,2,1:T(8,128)(2,1)S(1)} async-done(((bf16[256,4,320]{0,2,1:T(8,128)(2,1)}), bf16[256,4,320]{0,2,1:T(8,128)(2,1)S(1)}, u32[]{:S(2)}, u32[]{:S(2)}) %all-to-all-start) | async-done | bytes 655392 | tf_op jit(solution)/shard_map/all_to_all | solution.py:49
  16.7 1.3 %collective-permute-start.3 = (bf16[264,640]{0,1:T(8,128)(2,1)S(1)}, bf16[264,640]{0,1:T(8,128)(2,1)S(1)}, u32[]{:S(2)}, u32[]{:S(2)}) collective-permute-start(bf16[264,640]{0,1:T(8,128)(2,1)S(1)} %fusion.8), channel_id=1, source_target_pairs={{8,0},{12,4},{16,8},{20,12},{24,16},{28,20},{32,24},{36,28},{40,32... | collective-permute-start | bytes 1013768 | tf_op jit(solution)/shard_map/ppermute | solution.py:16
  18.0 8.5 %collective-permute-start.2 = (bf16[264,640]{0,1:T(8,128)(2,1)S(1)}, bf16[264,640]{0,1:T(8,128)(2,1)S(1)}, u32[]{:S(2)}, u32[]{:S(2)}) collective-permute-start(bf16[264,640]{0,1:T(8,128)(2,1)S(1)} %fusion.8), channel_id=1, source_target_pairs={{4,0},{8,4},{12,8},{16,12},{20,16},{24,20},{28,24},{32,28},{36,32}... | collective-permute-start | bytes 1013768 | tf_op jit(solution)/shard_map/ppermute | solution.py:16
  26.5 4.3 %collective-permute-start.1 = (bf16[264,640]{0,1:T(8,128)(2,1)S(1)}, bf16[264,640]{0,1:T(8,128)(2,1)S(1)}, u32[]{:S(2)}, u32[]{:S(2)}) collective-permute-start(bf16[264,640]{0,1:T(8,128)(2,1)S(1)} %fusion.8), channel_id=1, source_target_pairs={{0,8},{4,12},{8,16},{12,20},{16,24},{20,28},{24,32},{28,36},{32,40... | collective-permute-start | bytes 1013768 | tf_op jit(solution)/shard_map/ppermute | solution.py:16
  30.8 2.1 %collective-permute-start = (bf16[264,640]{0,1:T(8,128)(2,1)S(1)}, bf16[264,640]{0,1:T(8,128)(2,1)S(1)}, u32[]{:S(2)}, u32[]{:S(2)}) collective-permute-start(bf16[264,640]{0,1:T(8,128)(2,1)S(1)} %fusion.8), channel_id=1, source_target_pairs={{0,4},{4,8},{8,12},{12,16},{16,20},{20,24},{24,28},{28,32},{32,36}... | collective-permute-start | bytes 1013768 | tf_op jit(solution)/shard_map/ppermute | solution.py:16
  32.9 1.1 convolution_convert_fusion.2
  34.0 13.1 %collective-permute-done = bf16[264,640]{0,1:T(8,128)(2,1)S(1)} collective-permute-done((bf16[264,640]{0,1:T(8,128)(2,1)S(1)}, bf16[264,640]{0,1:T(8,128)(2,1)S(1)}, u32[]{:S(2)}, u32[]{:S(2)}) %collective-permute-start) | collective-permute-done | bytes 337952 | tf_op jit(solution)/shard_map/ppermute | solution.py:16
  47.2 1.0 fusion.46
  49.0 3.0 %exponential_reduce_fusion = f32[4,256]{1,0:T(4,128)S(1)} fusion(bf16[256,4,80]{0,2,1:T(8,128)(2,1)} %bitcast.55, bf16[1280,4,80]{0,2,1:T(8,128)(2,1)S(1)} %bitcast.52, pred[256,1280]{1,0:T(8,128)(4,1)S(1)} %fusion.5), kind=kOutput, calls=%fused_computation.6 | convolution fusion | flops 214959360 | bytes 1314816 | tf_op jit(solution)/shard_map/sub | solution.py:84
  51.9 4.1 %fusion.6 = bf16[4,80,256]{2,1,0:T(8,128)(2,1)} fusion(bf16[1280,4,80]{0,2,1:T(8,128)(2,1)} %bitcast.54, f32[4,256]{1,0:T(4,128)S(1)} %exponential_reduce_fusion, bf16[256,4,80]{0,2,1:T(8,128)(2,1)} %bitcast.56, bf16[1280,4,80]{0,2,1:T(8,128)(2,1)S(1)} %bitcast.53, pred[256,1280]{1,0:T(8,128)(4,1)S(1)} %fusion.5), kind=kOutput, calls=%fused_computation.18 | convolution fusion | flops 426068224 | bytes 2297856 | tf_op jit(solution)/shard_map/hqk,khd->qhd/dot_general | solution.py:87
  56.1 1.2 copy.33
  57.2 1.2 gather_fusion.1
  58.4 1.4 %convolution_convert_fusion = bf16[256,1280]{1,0:T(8,128)(2,1)} fusion(bf16[320,1280]{1,0:T(8,128)(2,1)S(1)} %copy-done.4, bf16[256,320]{1,0:T(8,128)(2,1)S(1)} %gather_fusion.1, pred[256]{0:T(512)(128)(4,1)S(1)} %compare_and_fusion), kind=kOutput, calls=%fused_computation.8 | convolution fusion | flops 210124800 | bytes 1638656 | tf_op jit(solution)/shard_map/dot_general | solution.py:93
  59.8 4.2 %all-to-all-start.1 = ((bf16[4,64,1280]{2,1,0:T(8,128)(2,1)}), bf16[4,64,1280]{2,1,0:T(8,128)(2,1)}, u32[]{:S(2)}, u32[]{:S(2)}) async-start(bf16[4,64,1280]{2,1,0:T(8,128)(2,1)} %bitcast.11), calls=%async_computation.1 | async-start | bytes 1310720 | tf_op jit(solution)/shard_map/all_to_all | solution.py:96
  64.3 0.7 gather_fusion
  65.0 6.6 %all-to-all-done.1 = bf16[4,64,1280]{2,1,0:T(8,128)(2,1)} async-done(((bf16[4,64,1280]{2,1,0:T(8,128)(2,1)}), bf16[4,64,1280]{2,1,0:T(8,128)(2,1)}, u32[]{:S(2)}, u32[]{:S(2)}) %all-to-all-start.1) | async-done | bytes 655392 | tf_op jit(solution)/shard_map/all_to_all | solution.py:96
  71.7 1.2 convert_reduce_fusion.1
  73.4 0.6 convolution_convert_fusion.1
  76.1 44.0 %all_to_all.30 = bf16[512,2,240]{2,1,0:T(2,128)(2,1)} all-to-all(bf16[512,2,240]{2,1,0:T(2,128)(2,1)S(1)} %reshape.289), channel_id=1, replica_groups=mesh['seq'=128,'tp'=4] {'seq','tp'}, dimensions={0} | all-to-all | bytes 983040 | tf_op jit(solution)/shard_map/all_to_all | solution.py:126
  120.1 3.0 %reshape.290 = bf16[512,3,160]{2,1,0:T(4,128)(2,1)S(1)} reshape(bf16[512,2,240]{2,1,0:T(2,128)(2,1)} %all_to_all.30) | data formatting | bytes 983040
  123.3 0.8 slice_reduce_fusion
  124.4 0.8 convolution_convert_fusion.6
  (79 shorter events, 7.0 us)
Async XLA Ops:
  0.0 73.4 %copy-start = (bf16[1280,640]{1,0:T(8,128)(2,1)S(1)}, bf16[1280,640]{1,0:T(8,128)(2,1)}, u32[]{:S(2)}) copy-start(bf16[1280,640]{1,0:T(8,128)(2,1)} %param.25) | copy-start | bytes 4915204
  0.0 7.0 %copy-start.7 = (s32[64,4]{0,1:T(4,128)S(1)}, s32[64,4]{0,1:T(4,128)}, u32[]{:S(2)}) copy-start(s32[64,4]{0,1:T(4,128)} %param.26) | copy-start | bytes 3076
  0.0 7.2 %copy-start.10 = (s32[64]{0:T(128)S(1)}, s32[64]{0:T(128)}, u32[]{:S(2)}) copy-start(s32[64]{0:T(128)} %param.27) | copy-start | bytes 772
  0.0 7.8 %copy-start.8 = (s32[256]{0:T(256)S(1)}, s32[256]{0:T(256)}, u32[]{:S(2)}) copy-start(s32[256]{0:T(256)} %param.23) | copy-start | bytes 3076
  0.0 7.8 %copy-start.9 = (s32[256]{0:T(256)S(1)}, s32[256]{0:T(256)}, u32[]{:S(2)}) copy-start(s32[256]{0:T(256)} %param.22) | copy-start | bytes 3076
  0.0 15.1 %copy-start.5 = (f32[1280]{0:T(1024)S(1)}, f32[1280]{0:T(1024)}, u32[]{:S(2)}) copy-start(f32[1280]{0:T(1024)} %param.17) | copy-start | bytes 15364
  2.2 12.5 %all-to-all-start = ((bf16[256,4,320]{0,2,1:T(8,128)(2,1)}), bf16[256,4,320]{0,2,1:T(8,128)(2,1)S(1)}, u32[]{:S(2)}, u32[]{:S(2)}) async-start(bf16[256,4,320]{0,2,1:T(8,128)(2,1)} %bitcast.1), calls=%async_computation | async-start | bytes 1310720 | tf_op jit(solution)/shard_map/all_to_all | solution.py:49
  7.0 8.3 %copy-start.1 = (bf16[1280,320]{0,1:T(8,128)(2,1)S(1)}, bf16[1280,320]{0,1:T(8,128)(2,1)}, u32[]{:S(2)}) copy-start(bf16[1280,320]{0,1:T(8,128)(2,1)} %param.19) | copy-start | bytes 2457604
  15.1 1.1 copy-start.2
  16.2 16.7 %copy-start.3 = (bf16[1280,320]{0,1:T(8,128)(2,1)S(1)}, bf16[1280,320]{0,1:T(8,128)(2,1)}, u32[]{:S(2)}) copy-start(bf16[1280,320]{0,1:T(8,128)(2,1)} %param.18) | copy-start | bytes 2457604
  16.7 30.5 %collective-permute-start.3 = (bf16[264,640]{0,1:T(8,128)(2,1)S(1)}, bf16[264,640]{0,1:T(8,128)(2,1)S(1)}, u32[]{:S(2)}, u32[]{:S(2)}) collective-permute-start(bf16[264,640]{0,1:T(8,128)(2,1)S(1)} %fusion.8), channel_id=1, source_target_pairs={{8,0},{12,4},{16,8},{20,12},{24,16},{28,20},{32,24},{36,28},{40,32... | collective-permute-start | bytes 1013768 | tf_op jit(solution)/shard_map/ppermute | solution.py:16
  18.0 29.2 %collective-permute-start.2 = (bf16[264,640]{0,1:T(8,128)(2,1)S(1)}, bf16[264,640]{0,1:T(8,128)(2,1)S(1)}, u32[]{:S(2)}, u32[]{:S(2)}) collective-permute-start(bf16[264,640]{0,1:T(8,128)(2,1)S(1)} %fusion.8), channel_id=1, source_target_pairs={{4,0},{8,4},{12,8},{16,12},{20,16},{24,20},{28,24},{32,28},{36,32}... | collective-permute-start | bytes 1013768 | tf_op jit(solution)/shard_map/ppermute | solution.py:16
  26.5 20.6 %collective-permute-start.1 = (bf16[264,640]{0,1:T(8,128)(2,1)S(1)}, bf16[264,640]{0,1:T(8,128)(2,1)S(1)}, u32[]{:S(2)}, u32[]{:S(2)}) collective-permute-start(bf16[264,640]{0,1:T(8,128)(2,1)S(1)} %fusion.8), channel_id=1, source_target_pairs={{0,8},{4,12},{8,16},{12,20},{16,24},{20,28},{24,32},{28,36},{32,40... | collective-permute-start | bytes 1013768 | tf_op jit(solution)/shard_map/ppermute | solution.py:16
  30.8 16.3 %collective-permute-start = (bf16[264,640]{0,1:T(8,128)(2,1)S(1)}, bf16[264,640]{0,1:T(8,128)(2,1)S(1)}, u32[]{:S(2)}, u32[]{:S(2)}) collective-permute-start(bf16[264,640]{0,1:T(8,128)(2,1)S(1)} %fusion.8), channel_id=1, source_target_pairs={{0,4},{4,8},{8,12},{12,16},{16,20},{20,24},{24,28},{28,32},{32,36}... | collective-permute-start | bytes 1013768 | tf_op jit(solution)/shard_map/ppermute | solution.py:16
  56.1 2.3 %copy-start.4 = (bf16[320,1280]{1,0:T(8,128)(2,1)S(1)}, bf16[320,1280]{1,0:T(8,128)(2,1)}, u32[]{:S(2)}) copy-start(bf16[320,1280]{1,0:T(8,128)(2,1)} %param.21) | copy-start | bytes 2457604
  59.8 11.9 %all-to-all-start.1 = ((bf16[4,64,1280]{2,1,0:T(8,128)(2,1)}), bf16[4,64,1280]{2,1,0:T(8,128)(2,1)}, u32[]{:S(2)}, u32[]{:S(2)}) async-start(bf16[4,64,1280]{2,1,0:T(8,128)(2,1)} %bitcast.11), calls=%async_computation.1 | async-start | bytes 1310720 | tf_op jit(solution)/shard_map/all_to_all | solution.py:96
  64.3 9.1 %copy-start.6 = (f32[1280]{0:T(1024)S(1)}, f32[1280]{0:T(1024)}, u32[]{:S(2)}) copy-start(f32[1280]{0:T(1024)} %param.24) | copy-start | bytes 15364

commit v5 on v3

--- a/solution.py
+++ b/solution.py
@@ -46,6 +46,11 @@
     position = lax.axis_index("tp")
     seq_index = lax.axis_index("seq")
 
+    local_index = merge_index - seq_index * row_count
+    order = local_index.T.reshape(row_count)
+    tokens = jnp.take(tokens, order, axis=0)
+    segment_ids = jnp.take(segment_ids, order, axis=0)
+    keep_mask = jnp.take(keep_mask, order, axis=0)
     gathered = lax.all_to_all(
         jnp.concatenate([tokens] * tp_size, axis=1), "tp", 1, 1, tiled=True
     )
@@ -85,18 +90,14 @@
     row_total = jnp.sum(exponent, axis=-1, keepdims=True)
     weights = (exponent / row_total).astype(jnp.bfloat16)
     attended = jnp.einsum("hqk,khd->qhd", weights, value_heads, preferred_element_type=jnp.float32)
-    attended = attended.reshape(row_count, local_width).astype(jnp.bfloat16)
-
-    local_index = merge_index - seq_index * row_count
-    order = local_index.T.reshape(row_count)
-    attended_sorted = jnp.take(attended, order, axis=0)
-    partial_sum = jnp.dot(attended_sorted, w_out, preferred_element_type=jnp.float32)
+    attended = attended.astype(jnp.bfloat16)
+    out_heads = w_out.reshape(heads_here, HD, w_out.shape[1])
+    partial_sum = jnp.einsum("qhd,hdn->qn", attended, out_heads, preferred_element_type=jnp.float32)
     partial_sum = partial_sum.astype(jnp.bfloat16)
     chunk = row_count // tp_size
     pieces = lax.all_to_all(partial_sum, "tp", 0, 0, tiled=True)
     mixed_sum = jnp.sum(pieces.reshape(tp_size, chunk, -1).astype(jnp.float32), axis=0)
-    column = lax.dynamic_slice_in_dim(local_index, position, 1, 1)[:, 0]
-    residual = jnp.take(gathered, column, axis=0)
+    residual = lax.dynamic_slice_in_dim(gathered, position * chunk, chunk, 0)
     updated = residual.astype(jnp.float32) + mixed_sum
     picked = layer_norm(updated, merge_gain).astype(jnp.bfloat16)
     partial_proj = jnp.dot(picked, w_merge, preferred_element_type=jnp.float32)

time: 120 us -> 122 us (1.017)
  local copies, waits for them, and re-layouts: 7.06 us -> 11.3 us
  other arithmetic: 6.07 us -> 3.59 us
  matrix products: 11.9 us -> 14.2 us
    gather x2 -> x3, local copies, waits for them, and re-layouts: 1.89 us -> 5.1 us  [the longest x1 1.98 us: body(): segment_ids = jnp.take(segment_ids, order, axis=0)]
    sub x1, matrix products: 2.95 us -> 5.56 us  [body(): exponent = jnp.exp(scores - row_max)]
    concatenate x1 -> x0, other arithmetic: 2.14 us -> none  [body(): jnp.concatenate([tokens] * tp_size, axis=1)]
    all_to_all x1, waiting for transfers between devices: 7.26 us -> 5.53 us  [body(): lax.all_to_all(jnp.concatenate([tokens] * tp_size, axis=1), 'tp', 1, 1, t...]
    unnamed x30 -> x26, local copies, waits for them, and re-layouts: 0.96 us -> 2.2 us
    dot_general x2 -> x1, matrix products: 5.56 us -> 5.24 us  [body(): jnp.einsum('qhd,hdn->qn', attended, out_heads, preferred_element_type=jnp...]
where the time goes in v5:
time: 122 us; the launch traced here: 121 us
  blocking collectives  33.8 us (28%)
  waiting for transfers between devices  30 us (25%)
  starting transfers between devices  28 us (23%)
  matrix products  14.2 us (12%)
  local copies, waits for them, and re-layouts  11.3 us (9%)
  other arithmetic  3.59 us (3%)
    all_to_all x1, blocking collectives, body(): lax.all_to_all(send_buf, 'seq', 0, 0, tiled=True)  33.8 us
    ppermute x4, starting transfers between devices, from_behind(): return lax.ppermute(shard, axis, pairs)  16.2 us
    ppermute x4, waiting for transfers between devices, from_behind(): return lax.ppermute(shard, axis, pairs)  13 us
    all_to_all x1, waiting for transfers between devices, body(): pieces = lax.all_to_all(partial_sum, 'tp', 0, 0, tiled=True)  7.05 us
    sub x1, matrix products, body(): exponent = jnp.exp(scores - row_max)  5.56 us
    all_to_all x1, waiting for transfers between devices, body(): lax.all_to_all(jnp.concatenate([tokens] * tp_size, axis=1), 'tp', 1, 1, t...  5.53 us
    dot_general x1, matrix products, body(): jnp.einsum('qhd,hdn->qn', attended, out_heads, preferred_element_type=jnp...  5.24 us
    all_to_all x1, starting transfers between devices, body(): lax.all_to_all(jnp.concatenate([tokens] * tp_size, axis=1), 'tp', 1, 1, t...  4.96 us
  transfers between devices with their start and end apart: 7, of which 4 were waited for; matrix products, arithmetic and copies ran while one was open for 3% of the time, Pallas kernels for 0%

profile of v5, /device:TPU:1, one launch (start us, length us, event | category | flops | bytes accessed | tf_op | source)
XLA Modules:
  0.0 121.3 jit_solution(11979619081100485500)
XLA Ops:
  0.0 0.8 subtract_bitcast_fusion
  1.0 2.0 %gather_fusion.2 = s32[256]{0:T(256)S(1)} fusion(s32[256]{0:T(256)} %param.24, s32[1024]{0:T(1024)S(1)} %get-tuple-element.38), kind=kCustom, calls=%fused_computation.1.clone | custom fusion | bytes 3072 | tf_op jit(solution)/shard_map/jit(_take)/gather | solution.py:52
  3.0 1.1 copy.38
  4.1 1.2 gather_fusion
  5.5 0.9 concatenate.23
  6.4 5.0 %all-to-all-start = ((bf16[256,4,320]{0,2,1:T(8,128)(2,1)}), bf16[256,4,320]{0,2,1:T(8,128)(2,1)S(1)}, u32[]{:S(2)}, u32[]{:S(2)}) async-start(bf16[256,4,320]{0,2,1:T(8,128)(2,1)} %concatenate.23), calls=%async_computation | async-start | bytes 1310720 | tf_op jit(solution)/shard_map/all_to_all | solution.py:54
  11.4 1.9 %gather_fusion.1 = s32[256]{0:T(256)S(1)} fusion(s32[256]{0:T(256)S(1)} %copy-done.1, s32[1024]{0:T(1024)S(1)} %get-tuple-element.38), kind=kCustom, calls=%fused_computation.clone | custom fusion | bytes 3072 | tf_op jit(solution)/shard_map/jit(_take)/gather | solution.py:53
  13.5 5.5 %all-to-all-done = bf16[256,4,320]{0,2,1:T(8,128)(2,1)S(1)} async-done(((bf16[256,4,320]{0,2,1:T(8,128)(2,1)}), bf16[256,4,320]{0,2,1:T(8,128)(2,1)S(1)}, u32[]{:S(2)}, u32[]{:S(2)}) %all-to-all-start) | async-done | bytes 655392 | tf_op jit(solution)/shard_map/all_to_all | solution.py:54
  21.0 1.3 %collective-permute-start.3 = (bf16[264,640]{0,1:T(8,128)(2,1)S(1)}, bf16[264,640]{0,1:T(8,128)(2,1)S(1)}, u32[]{:S(2)}, u32[]{:S(2)}) collective-permute-start(bf16[264,640]{0,1:T(8,128)(2,1)S(1)} %fusion.11), channel_id=1, source_target_pairs={{8,0},{12,4},{16,8},{20,12},{24,16},{28,20},{32,24},{36,28},{40,32... | collective-permute-start | bytes 1013768 | tf_op jit(solution)/shard_map/ppermute | solution.py:16
  22.3 8.5 %collective-permute-start.2 = (bf16[264,640]{0,1:T(8,128)(2,1)S(1)}, bf16[264,640]{0,1:T(8,128)(2,1)S(1)}, u32[]{:S(2)}, u32[]{:S(2)}) collective-permute-start(bf16[264,640]{0,1:T(8,128)(2,1)S(1)} %fusion.11), channel_id=1, source_target_pairs={{4,0},{8,4},{12,8},{16,12},{20,16},{24,20},{28,24},{32,28},{36,32}... | collective-permute-start | bytes 1013768 | tf_op jit(solution)/shard_map/ppermute | solution.py:16
  30.8 4.3 %collective-permute-start.1 = (bf16[264,640]{0,1:T(8,128)(2,1)S(1)}, bf16[264,640]{0,1:T(8,128)(2,1)S(1)}, u32[]{:S(2)}, u32[]{:S(2)}) collective-permute-start(bf16[264,640]{0,1:T(8,128)(2,1)S(1)} %fusion.11), channel_id=1, source_target_pairs={{0,8},{4,12},{8,16},{12,20},{16,24},{20,28},{24,32},{28,36},{32,40... | collective-permute-start | bytes 1013768 | tf_op jit(solution)/shard_map/ppermute | solution.py:16
  35.1 2.1 %collective-permute-start = (bf16[264,640]{0,1:T(8,128)(2,1)S(1)}, bf16[264,640]{0,1:T(8,128)(2,1)S(1)}, u32[]{:S(2)}, u32[]{:S(2)}) collective-permute-start(bf16[264,640]{0,1:T(8,128)(2,1)S(1)} %fusion.11), channel_id=1, source_target_pairs={{0,4},{4,8},{8,12},{12,16},{16,20},{20,24},{24,28},{28,32},{32,36}... | collective-permute-start | bytes 1013768 | tf_op jit(solution)/shard_map/ppermute | solution.py:16
  37.3 1.1 convolution_convert_fusion
  38.4 13.0 %collective-permute-done = bf16[264,640]{0,1:T(8,128)(2,1)S(1)} collective-permute-done((bf16[264,640]{0,1:T(8,128)(2,1)S(1)}, bf16[264,640]{0,1:T(8,128)(2,1)S(1)}, u32[]{:S(2)}, u32[]{:S(2)}) %collective-permute-start) | collective-permute-done | bytes 337952 | tf_op jit(solution)/shard_map/ppermute | solution.py:16
  51.5 1.0 fusion.37
  53.4 5.6 %exponential_reduce_fusion = (f32[4,256]{1,0:T(4,128)S(1)}, f32[4,256,1280]{2,1,0:T(8,128)}) fusion(bf16[256,4,80]{0,2,1:T(8,128)(2,1)} %bitcast.39, bf16[1280,4,80]{0,2,1:T(8,128)(2,1)} %bitcast.37, pred[256,1280]{1,0:T(8,128)(4,1)S(1)} %fusion.6), kind=kOutput, calls=%fused_computation.7 | convolution fusion | flops 214959360 | bytes 6557696 | tf_op jit(solution)/shard_map/sub | solution.py:89
  58.9 5.2 %fusion.3 = bf16[256,1280]{1,0:T(8,128)(2,1)} fusion(bf16[4,80,1280]{2,1,0:T(8,128)(2,1)} %bitcast.41, bf16[1280,4,80]{0,2,1:T(8,128)(2,1)S(1)} %bitcast.36, f32[4,256,1280]{2,1,0:T(8,128)} %get-tuple-element.37, f32[4,256]{1,0:T(4,128)S(1)} %get-tuple-element.36), kind=kOutput, calls=%fused_computation.10 | convolution fusion | flops 422461440 | bytes 7540736 | tf_op jit(solution)/shard_map/qhd,hdn->qn/dot_general | solution.py:95
  64.2 3.5 %all-to-all-start.1 = ((bf16[4,64,1280]{2,1,0:T(8,128)(2,1)}), bf16[4,64,1280]{2,1,0:T(8,128)(2,1)S(1)}, u32[]{:S(2)}, u32[]{:S(2)}) async-start(bf16[4,64,1280]{2,1,0:T(8,128)(2,1)} %bitcast.38), calls=%async_computation.1 | async-start | bytes 1310720 | tf_op jit(solution)/shard_map/all_to_all | solution.py:98
  68.2 7.0 %all-to-all-done.1 = bf16[4,64,1280]{2,1,0:T(8,128)(2,1)S(1)} async-done(((bf16[4,64,1280]{2,1,0:T(8,128)(2,1)}), bf16[4,64,1280]{2,1,0:T(8,128)(2,1)S(1)}, u32[]{:S(2)}, u32[]{:S(2)}) %all-to-all-start.1) | async-done | bytes 655392 | tf_op jit(solution)/shard_map/all_to_all | solution.py:98
  76.3 0.7 copy.42
  77.0 3.3 %all-to-all-start.2 = ((bf16[64,4,160]{2,0,1:T(8,128)(2,1)}), bf16[64,4,160]{2,0,1:T(8,128)(2,1)S(1)}, u32[]{:S(2)}, u32[]{:S(2)}) async-start(bf16[64,4,160]{2,0,1:T(8,128)(2,1)} %copy.42), calls=%async_computation.2 | async-start | bytes 262144 | tf_op jit(solution)/shard_map/all_to_all | solution.py:106
  80.7 4.4 %all-to-all-done.2 = bf16[64,4,160]{2,0,1:T(8,128)(2,1)S(1)} async-done(((bf16[64,4,160]{2,0,1:T(8,128)(2,1)}), bf16[64,4,160]{2,0,1:T(8,128)(2,1)S(1)}, u32[]{:S(2)}, u32[]{:S(2)}) %all-to-all-start.2) | async-done | bytes 81952 | tf_op jit(solution)/shard_map/all_to_all | solution.py:106
  86.0 33.8 %all_to_all.37 = bf16[128,2,240]{2,1,0:T(2,128)(2,1)S(1)} all-to-all(bf16[128,2,240]{2,1,0:T(2,128)(2,1)S(1)} %reshape.336), channel_id=1, replica_groups=mesh['seq'=128,'tp'=4] {'seq'}, dimensions={0} | all-to-all | bytes 245760 | tf_op jit(solution)/shard_map/all_to_all | solution.py:127
  120.6 0.8 convolution_convert_fusion.5
  (78 shorter events, 6.9 us)
Async XLA Ops:
  0.0 75.7 %copy-start = (bf16[1280,640]{1,0:T(8,128)(2,1)S(1)}, bf16[1280,640]{1,0:T(8,128)(2,1)}, u32[]{:S(2)}) copy-start(bf16[1280,640]{1,0:T(8,128)(2,1)} %param.27) | copy-start | bytes 4915204
  5.2 6.1 %copy-start.1 = (s32[256]{0:T(256)S(1)}, s32[256]{0:T(256)}, u32[]{:S(2)}) copy-start(s32[256]{0:T(256)} %param.25) | copy-start | bytes 3076
  5.5 7.9 %copy-start.7 = (s32[64]{0:T(128)S(1)}, s32[64]{0:T(128)}, u32[]{:S(2)}) copy-start(s32[64]{0:T(128)} %param.29) | copy-start | bytes 772
  6.4 13.0 %copy-start.5 = (f32[1280]{0:T(1024)S(1)}, f32[1280]{0:T(1024)}, u32[]{:S(2)}) copy-start(f32[1280]{0:T(1024)} %param.19) | copy-start | bytes 15364
  6.4 12.6 %all-to-all-start = ((bf16[256,4,320]{0,2,1:T(8,128)(2,1)}), bf16[256,4,320]{0,2,1:T(8,128)(2,1)S(1)}, u32[]{:S(2)}, u32[]{:S(2)}) async-start(bf16[256,4,320]{0,2,1:T(8,128)(2,1)} %concatenate.23), calls=%async_computation | async-start | bytes 1310720 | tf_op jit(solution)/shard_map/all_to_all | solution.py:54
  11.4 8.3 %copy-start.2 = (bf16[1280,320]{0,1:T(8,128)(2,1)S(1)}, bf16[1280,320]{0,1:T(8,128)(2,1)}, u32[]{:S(2)}) copy-start(bf16[1280,320]{0,1:T(8,128)(2,1)} %param.21) | copy-start | bytes 2457604
  19.4 1.1 copy-start.3
  20.6 16.7 %copy-start.4 = (bf16[1280,320]{0,1:T(8,128)(2,1)S(1)}, bf16[1280,320]{0,1:T(8,128)(2,1)}, u32[]{:S(2)}) copy-start(bf16[1280,320]{0,1:T(8,128)(2,1)} %param.20) | copy-start | bytes 2457604
  21.0 30.5 %collective-permute-start.3 = (bf16[264,640]{0,1:T(8,128)(2,1)S(1)}, bf16[264,640]{0,1:T(8,128)(2,1)S(1)}, u32[]{:S(2)}, u32[]{:S(2)}) collective-permute-start(bf16[264,640]{0,1:T(8,128)(2,1)S(1)} %fusion.11), channel_id=1, source_target_pairs={{8,0},{12,4},{16,8},{20,12},{24,16},{28,20},{32,24},{36,28},{40,32... | collective-permute-start | bytes 1013768 | tf_op jit(solution)/shard_map/ppermute | solution.py:16
  22.3 29.2 %collective-permute-start.2 = (bf16[264,640]{0,1:T(8,128)(2,1)S(1)}, bf16[264,640]{0,1:T(8,128)(2,1)S(1)}, u32[]{:S(2)}, u32[]{:S(2)}) collective-permute-start(bf16[264,640]{0,1:T(8,128)(2,1)S(1)} %fusion.11), channel_id=1, source_target_pairs={{4,0},{8,4},{12,8},{16,12},{20,16},{24,20},{28,24},{32,28},{36,32}... | collective-permute-start | bytes 1013768 | tf_op jit(solution)/shard_map/ppermute | solution.py:16
  30.8 20.6 %collective-permute-start.1 = (bf16[264,640]{0,1:T(8,128)(2,1)S(1)}, bf16[264,640]{0,1:T(8,128)(2,1)S(1)}, u32[]{:S(2)}, u32[]{:S(2)}) collective-permute-start(bf16[264,640]{0,1:T(8,128)(2,1)S(1)} %fusion.11), channel_id=1, source_target_pairs={{0,8},{4,12},{8,16},{12,20},{16,24},{20,28},{24,32},{28,36},{32,40... | collective-permute-start | bytes 1013768 | tf_op jit(solution)/shard_map/ppermute | solution.py:16
  35.1 16.3 %collective-permute-start = (bf16[264,640]{0,1:T(8,128)(2,1)S(1)}, bf16[264,640]{0,1:T(8,128)(2,1)S(1)}, u32[]{:S(2)}, u32[]{:S(2)}) collective-permute-start(bf16[264,640]{0,1:T(8,128)(2,1)S(1)} %fusion.11), channel_id=1, source_target_pairs={{0,4},{4,8},{8,12},{12,16},{16,20},{20,24},{24,28},{28,32},{32,36}... | collective-permute-start | bytes 1013768 | tf_op jit(solution)/shard_map/ppermute | solution.py:16
  64.2 11.1 %all-to-all-start.1 = ((bf16[4,64,1280]{2,1,0:T(8,128)(2,1)}), bf16[4,64,1280]{2,1,0:T(8,128)(2,1)S(1)}, u32[]{:S(2)}, u32[]{:S(2)}) async-start(bf16[4,64,1280]{2,1,0:T(8,128)(2,1)} %bitcast.38), calls=%async_computation.1 | async-start | bytes 1310720 | tf_op jit(solution)/shard_map/all_to_all | solution.py:98
  67.6 8.1 %copy-start.6 = (f32[1280]{0:T(1024)S(1)}, f32[1280]{0:T(1024)}, u32[]{:S(2)}) copy-start(f32[1280]{0:T(1024)} %param.26) | copy-start | bytes 15364
  77.0 8.1 %all-to-all-start.2 = ((bf16[64,4,160]{2,0,1:T(8,128)(2,1)}), bf16[64,4,160]{2,0,1:T(8,128)(2,1)S(1)}, u32[]{:S(2)}, u32[]{:S(2)}) async-start(bf16[64,4,160]{2,0,1:T(8,128)(2,1)} %copy.42), calls=%async_computation.2 | async-start | bytes 262144 | tf_op jit(solution)/shard_map/all_to_all | solution.py:106

commit v6 on v3

--- a/solution.py
+++ b/solution.py
@@ -1,6 +1,10 @@
+import functools
+
 import jax
 import jax.numpy as jnp
 from jax import lax
+from jax.experimental import pallas as pl
+from jax.experimental.pallas import tpu as pltpu
 from jax.sharding import PartitionSpec as P
 
 HD = 80
@@ -14,6 +18,62 @@
     length = lax.axis_size(axis)
     pairs = [(i, i + by) for i in range(length) if 0 <= i + by < length]
     return lax.ppermute(shard, axis, pairs)
+
+
+def attn_kernel(heads, rows, qcode_ref, q_ref, b0, b1, b2, b3, b4, out_ref):
+    blocks = (b0, b1, b2, b3, b4)
+    scale = HD ** (-0.5)
+    qcode = qcode_ref[...]
+    width = heads * HD
+    row_id = lax.broadcasted_iota(jnp.int32, (rows, rows), 0)
+    col_id = lax.broadcasted_iota(jnp.int32, (rows, rows), 1)
+    diag = row_id == col_id
+    masks = []
+    for b, blk in enumerate(blocks):
+        kcode = blk[rows:rows + 1, 0:rows].astype(jnp.float32)
+        m = qcode == kcode
+        if b == 0:
+            m = m | diag
+        masks.append(m)
+    for h in range(heads):
+        q = q_ref[:, h * HD:(h + 1) * HD]
+        scores = []
+        for b, blk in enumerate(blocks):
+            k = blk[0:rows, h * HD:(h + 1) * HD]
+            s = lax.dot_general(q, k, (((1,), (1,)), ((), ())), preferred_element_type=jnp.float32) * scale
+            scores.append(jnp.where(masks[b], s, -1e30))
+        row_max = scores[0].max(axis=1, keepdims=True)
+        for s in scores[1:]:
+            row_max = jnp.maximum(row_max, s.max(axis=1, keepdims=True))
+        exps = [jnp.exp(s - row_max) for s in scores]
+        total = exps[0].sum(axis=1, keepdims=True)
+        for e in exps[1:]:
+            total = total + e.sum(axis=1, keepdims=True)
+        acc = None
+        for b, blk in enumerate(blocks):
+            w = (exps[b] / total).astype(jnp.bfloat16)
+            v = blk[0:rows, width + h * HD:width + (h + 1) * HD]
+            p = jnp.dot(w, v, preferred_element_type=jnp.float32)
+            acc = p if acc is None else acc + p
+        out_ref[:, h * HD:(h + 1) * HD] = acc.astype(out_ref.dtype)
+
+
+def attention(qcode, q, blocks):
+    rows, width = q.shape
+    heads = width // HD
+    vmem = pl.BlockSpec(memory_space=pltpu.VMEM)
+    flops = 2 * 2 * heads * rows * rows * len(blocks) * HD
+    return pl.pallas_call(
+        functools.partial(attn_kernel, heads, rows),
+        out_shape=jax.ShapeDtypeStruct((rows, width), jnp.bfloat16),
+        in_specs=[vmem] * (2 + len(blocks)),
+        out_specs=vmem,
+        cost_estimate=pl.CostEstimate(
+            flops=flops,
+            transcendentals=heads * rows * rows * len(blocks),
+            bytes_accessed=sum(b.size * 2 for b in blocks) + q.size * 4,
+        ),
+    )(qcode, q, *blocks)
 
 
 def layer_norm(activations, norm_gain):
@@ -63,29 +123,8 @@
     pair_list = [paired]
     for offset in (1, 2, -1, -2):
         pair_list.append(from_behind(paired, "seq", offset))
-    all_pairs = jnp.concatenate([p[:row_count] for p in pair_list], axis=0)
-    all_codes = jnp.concatenate(
-        [code_key] + [p[row_count, :row_count].astype(jnp.int32) for p in pair_list[1:]], axis=0
-    )
-    window = all_pairs.shape[0]
-    key_heads = all_pairs[:, :local_width].reshape(window, heads_here, HD)
-    value_heads = all_pairs[:, local_width:].reshape(window, heads_here, HD)
-    query_heads = queries.reshape(row_count, heads_here, HD)
-    score_scale = HD ** (-0.5)
-    scores = (
-        jnp.einsum("qhd,khd->hqk", query_heads, key_heads, preferred_element_type=jnp.float32)
-        * score_scale
-    )
-    query_pos = jnp.arange(row_count)[:, None]
-    key_pos = jnp.arange(window)[None, :]
-    allowed = (code_query[:, None] == all_codes[None, :]) | (key_pos == query_pos)
-    scores = jnp.where(allowed[None], scores, -1e30)
-    row_max = jnp.max(scores, axis=-1, keepdims=True)
-    exponent = jnp.exp(scores - row_max)
-    row_total = jnp.sum(exponent, axis=-1, keepdims=True)
-    weights = (exponent / row_total).astype(jnp.bfloat16)
-    attended = jnp.einsum("hqk,khd->qhd", weights, value_heads, preferred_element_type=jnp.float32)
-    attended = attended.reshape(row_count, local_width).astype(jnp.bfloat16)
+    query_code = code_query.astype(jnp.float32)[:, None]
+    attended = attention(query_code, queries, pair_list)
 
     local_index = merge_index - seq_index * row_count
     order = local_index.T.reshape(row_count)

time: 120 us -> 114 us (0.950)
  Pallas kernels: 0 us -> 6.35 us
  matrix products: 11.9 us -> 6.42 us
  waiting for transfers between devices: 31.2 us -> 26.3 us
  blocking collectives: 33.8 us -> 31.9 us
    pallas_call x0 -> x1, Pallas kernels: none -> 6.35 us  [attention(): pl.pallas_call(functools.partial(attn_kernel, heads, rows), out_shape=jax...]
    ppermute x4, waiting for transfers between devices: 13.1 us -> 8.48 us  [from_behind(): return lax.ppermute(shard, axis, pairs)]
    dot_general x1 -> x0, matrix products: 4.15 us -> none  [body(): jnp.einsum('hqk,khd->qhd', weights, value_heads, preferred_element_type=j...]
    sub x1 -> x0, matrix products: 2.95 us -> none  [body(): exponent = jnp.exp(scores - row_max)]
    all_to_all x1, blocking collectives: 33.8 us -> 31.9 us  [body(): lax.all_to_all(send_buf, 'seq', 0, 0, tiled=True)]
  transfers between devices with their start and end apart: 7 -> 7, of which waited for: 4 -> 6; matrix products, arithmetic and copies ran while one was open for 3% -> 4% of each run, Pallas kernels for 0% -> 0%
where the time goes in v6:
time: 114 us
  blocking collectives  31.9 us (28%)
  starting transfers between devices  28.5 us (25%)
  waiting for transfers between devices  26.3 us (23%)
  local copies, waits for them, and re-layouts  7.65 us (7%)
  matrix products  6.42 us (6%)
  Pallas kernels  6.35 us (6%)
  other arithmetic  6.13 us (5%)
    all_to_all x1, blocking collectives, body(): lax.all_to_all(send_buf, 'seq', 0, 0, tiled=True)  31.9 us
    ppermute x4, starting transfers between devices, from_behind(): return lax.ppermute(shard, axis, pairs)  16 us
    ppermute x4, waiting for transfers between devices, from_behind(): return lax.ppermute(shard, axis, pairs)  8.48 us
    all_to_all x1, waiting for transfers between devices, body(): pieces = lax.all_to_all(partial_sum, 'tp', 0, 0, tiled=True)  6.86 us
    all_to_all x1, waiting for transfers between devices, body(): lax.all_to_all(jnp.concatenate([tokens] * tp_size, axis=1), 'tp', 1, 1, t...  6.58 us
    pallas_call x1, Pallas kernels, attention(): pl.pallas_call(functools.partial(attn_kernel, heads, rows), out_shape=jax...  6.35 us
    all_to_all x1, starting transfers between devices, body(): lax.all_to_all(jnp.concatenate([tokens] * tp_size, axis=1), 'tp', 1, 1, t...  4.96 us
    all_to_all x1, waiting for transfers between devices, body(): proj_pieces = lax.all_to_all(partial_proj, 'tp', 1, 0, tiled=True)  4.42 us
  transfers between devices with their start and end apart: 7, of which 6 were waited for; matrix products, arithmetic and copies ran while one was open for 4% of the time, Pallas kernels for 0%

profile of v6, /device:TPU:1, one launch (start us, length us, event | category | flops | bytes accessed | tf_op | source)
XLA Modules:
  0.0 113.6 jit_solution(16739718864202738547)
XLA Ops:
  0.0 2.1 %pad_maximum_fusion = bf16[256,1280]{0,1:T(8,128)(2,1)} fusion(bf16[256,320]{0,1:T(8,128)(2,1)} %param.16), kind=kLoop, calls=%fused_computation.17 | loop fusion | flops 2621440 | bytes 819200 | tf_op jit(solution)/shard_map/concatenate | solution.py:110
  2.2 5.0 %all-to-all-start = ((bf16[256,4,320]{0,2,1:T(8,128)(2,1)}), bf16[256,4,320]{0,2,1:T(8,128)(2,1)S(1)}, u32[]{:S(2)}, u32[]{:S(2)}) async-start(bf16[256,4,320]{0,2,1:T(8,128)(2,1)} %bitcast.1), calls=%async_computation | async-start | bytes 1310720 | tf_op jit(solution)/shard_map/all_to_all | solution.py:109
  7.4 0.8 copy.54.qcode_ref
  8.2 6.6 %all-to-all-done = bf16[256,4,320]{0,2,1:T(8,128)(2,1)S(1)} async-done(((bf16[256,4,320]{0,2,1:T(8,128)(2,1)}), bf16[256,4,320]{0,2,1:T(8,128)(2,1)S(1)}, u32[]{:S(2)}, u32[]{:S(2)}) %all-to-all-start) | async-done | bytes 655392 | tf_op jit(solution)/shard_map/all_to_all | solution.py:109
  16.5 1.5 %convolution_convert_fusion.2 = bf16[256,320]{0,1:T(8,128)(2,1)S(1)} fusion(bf16[1280,320]{0,1:T(8,128)(2,1)} %param.19, bf16[256,1280]{0,1:T(8,128)(2,1)S(1)} %multiply_convert_fusion), kind=kOutput, calls=%fused_computation.10 | convolution fusion | flops 209797120 | bytes 1638400 | tf_op jit(solution)/shard_map/dot_general | solution.py:115
  18.2 0.8 fusion.4.b0
  19.0 8.1 %collective-permute-start = (bf16[264,640]{1,0:T(8,128)(2,1)}, bf16[264,640]{1,0:T(8,128)(2,1)}, u32[]{:S(2)}, u32[]{:S(2)}) collective-permute-start(bf16[264,640]{1,0:T(8,128)(2,1)} %fusion.4.b0), channel_id=1, source_target_pairs={{0,4},{4,8},{8,12},{12,16},{16,20},{20,24},{24,28},{28,32},{32,36}... | collective-permute-start | bytes 1013768 | tf_op jit(solution)/shard_map/ppermute | solution.py:20
  27.1 4.7 %collective-permute-start.1 = (bf16[264,640]{1,0:T(8,128)(2,1)}, bf16[264,640]{1,0:T(8,128)(2,1)}, u32[]{:S(2)}, u32[]{:S(2)}) collective-permute-start(bf16[264,640]{1,0:T(8,128)(2,1)} %fusion.4.b0), channel_id=1, source_target_pairs={{0,8},{4,12},{8,16},{12,20},{16,24},{20,28},{24,32},{28,36},{32,40... | collective-permute-start | bytes 1013768 | tf_op jit(solution)/shard_map/ppermute | solution.py:20
  31.8 1.9 %collective-permute-start.2 = (bf16[264,640]{1,0:T(8,128)(2,1)}, bf16[264,640]{1,0:T(8,128)(2,1)}, u32[]{:S(2)}, u32[]{:S(2)}) collective-permute-start(bf16[264,640]{1,0:T(8,128)(2,1)} %fusion.4.b0), channel_id=1, source_target_pairs={{4,0},{8,4},{12,8},{16,12},{20,16},{24,20},{28,24},{32,28},{36,32}... | collective-permute-start | bytes 1013768 | tf_op jit(solution)/shard_map/ppermute | solution.py:20
  33.8 1.3 %collective-permute-start.3 = (bf16[264,640]{1,0:T(8,128)(2,1)}, bf16[264,640]{1,0:T(8,128)(2,1)}, u32[]{:S(2)}, u32[]{:S(2)}) collective-permute-start(bf16[264,640]{1,0:T(8,128)(2,1)} %fusion.4.b0), channel_id=1, source_target_pairs={{8,0},{12,4},{16,8},{20,12},{24,16},{28,20},{32,24},{36,28},{40,32... | collective-permute-start | bytes 1013768 | tf_op jit(solution)/shard_map/ppermute | solution.py:20
  35.1 1.5 %convolution_convert_fusion.3 = bf16[256,320]{0,1:T(8,128)(2,1)S(1)} fusion(bf16[1280,320]{0,1:T(8,128)(2,1)} %param.18, bf16[256,1280]{0,1:T(8,128)(2,1)S(1)} %multiply_convert_fusion), kind=kOutput, calls=%fused_computation.11 | convolution fusion | flops 209797120 | bytes 1638400 | tf_op jit(solution)/shard_map/dot_general | solution.py:114
  36.6 0.8 copy.55.q_ref
  37.4 1.3 %collective-permute-done.1.b2 = bf16[264,640]{1,0:T(8,128)(2,1)} collective-permute-done((bf16[264,640]{1,0:T(8,128)(2,1)}, bf16[264,640]{1,0:T(8,128)(2,1)}, u32[]{:S(2)}, u32[]{:S(2)}) %collective-permute-start.1) | collective-permute-done | bytes 337952 | tf_op jit(solution)/shard_map/ppermute | solution.py:20
  38.8 4.1 %collective-permute-done.2.b3 = bf16[264,640]{1,0:T(8,128)(2,1)} collective-permute-done((bf16[264,640]{1,0:T(8,128)(2,1)}, bf16[264,640]{1,0:T(8,128)(2,1)}, u32[]{:S(2)}, u32[]{:S(2)}) %collective-permute-start.2) | collective-permute-done | bytes 337952 | tf_op jit(solution)/shard_map/ppermute | solution.py:20
  42.9 3.0 %collective-permute-done.3.b4 = bf16[264,640]{1,0:T(8,128)(2,1)} collective-permute-done((bf16[264,640]{1,0:T(8,128)(2,1)}, bf16[264,640]{1,0:T(8,128)(2,1)}, u32[]{:S(2)}, u32[]{:S(2)}) %collective-permute-start.3) | collective-permute-done | bytes 337952 | tf_op jit(solution)/shard_map/ppermute | solution.py:20
  45.9 6.4 %shard_map.118 = bf16[256,320]{1,0:T(8,128)(2,1)} custom-call(f32[256,1]{1,0:T(8,128)} %copy.54.qcode_ref, bf16[256,320]{1,0:T(8,128)(2,1)} %copy.55.q_ref, bf16[264,640]{1,0:T(8,128)(2,1)} %fusion.4.b0, bf16[264,640]{1,0:T(8,128)(2,1)} %collective-permute-done.b1, bf16[264,640]{1,0:T(8,128)(2,1)} %collective-permute-done.1.b2, ...), custom_call_target="tpu_custom_call" | custom-call | flops 419430400 | bytes 2017280 | tf_op jit(solution)/shard_map/pallas_call | solution.py:66
  52.3 2.2 %gather_fusion.1 = bf16[256,320]{1,0:T(8,128)(2,1)S(1)} fusion(bf16[256,320]{1,0:T(8,128)(2,1)} %shard_map.118, s32[1024]{0:T(1024)S(1)} %pad_clamp_fusion), kind=kCustom, calls=%fused_computation.1 | custom fusion | bytes 328704 | tf_op jit(solution)/shard_map/jit(_take)/gather | solution.py:131
  54.4 1.4 %convolution_convert_fusion = bf16[256,1280]{1,0:T(8,128)(2,1)} fusion(bf16[320,1280]{1,0:T(8,128)(2,1)S(1)} %copy-done.2, bf16[256,320]{1,0:T(8,128)(2,1)S(1)} %gather_fusion.1, pred[256]{0:T(512)(128)(4,1)S(1)} %compare_and_fusion), kind=kOutput, calls=%fused_computation.2 | convolution fusion | flops 210124800 | bytes 1638656 | tf_op jit(solution)/shard_map/dot_general | solution.py:132
  55.9 4.2 %all-to-all-start.1 = ((bf16[4,64,1280]{2,1,0:T(8,128)(2,1)}), bf16[4,64,1280]{2,1,0:T(8,128)(2,1)}, u32[]{:S(2)}, u32[]{:S(2)}) async-start(bf16[4,64,1280]{2,1,0:T(8,128)(2,1)} %bitcast.7), calls=%async_computation.1 | async-start | bytes 1310720 | tf_op jit(solution)/shard_map/all_to_all | solution.py:135
  61.2 6.9 %all-to-all-done.1 = bf16[4,64,1280]{2,1,0:T(8,128)(2,1)} async-done(((bf16[4,64,1280]{2,1,0:T(8,128)(2,1)}), bf16[4,64,1280]{2,1,0:T(8,128)(2,1)}, u32[]{:S(2)}, u32[]{:S(2)}) %all-to-all-start.1) | async-done | bytes 655392 | tf_op jit(solution)/shard_map/all_to_all | solution.py:135
  68.1 1.2 %convert_reduce_fusion.1 = f32[64,1280]{1,0:T(8,128)S(1)} fusion(bf16[4,64,1280]{2,1,0:T(8,128)(2,1)} %all-to-all-done.1), kind=kLoop, calls=%fused_computation.7 | loop fusion | flops 573440 | bytes 983040 | tf_op jit(solution)/shard_map/reduce_sum | solution.py:136
  71.0 3.3 %all-to-all-start.2 = ((bf16[64,4,160]{2,0,1:T(8,128)(2,1)}), bf16[64,4,160]{2,0,1:T(8,128)(2,1)S(1)}, u32[]{:S(2)}, u32[]{:S(2)}) async-start(bf16[64,4,160]{2,0,1:T(8,128)(2,1)} %copy.56), calls=%async_computation.2 | async-start | bytes 262144 | tf_op jit(solution)/shard_map/all_to_all | solution.py:144
  74.7 4.4 %all-to-all-done.2 = bf16[64,4,160]{2,0,1:T(8,128)(2,1)S(1)} async-done(((bf16[64,4,160]{2,0,1:T(8,128)(2,1)}), bf16[64,4,160]{2,0,1:T(8,128)(2,1)S(1)}, u32[]{:S(2)}, u32[]{:S(2)}) %all-to-all-start.2) | async-done | bytes 81952 | tf_op jit(solution)/shard_map/all_to_all | solution.py:144
  80.0 31.9 %all_to_all.40 = bf16[128,2,240]{2,1,0:T(2,128)(2,1)S(1)} all-to-all(bf16[128,2,240]{2,1,0:T(2,128)(2,1)S(1)} %reshape.213), channel_id=1, replica_groups=mesh['seq'=128,'tp'=4] {'seq'}, dimensions={0} | all-to-all | bytes 245760 | tf_op jit(solution)/shard_map/all_to_all | solution.py:165
  (65 shorter events, 7.7 us)
Async XLA Ops:
  0.0 69.8 %copy-start = (bf16[1280,640]{1,0:T(8,128)(2,1)S(1)}, bf16[1280,640]{1,0:T(8,128)(2,1)}, u32[]{:S(2)}) copy-start(bf16[1280,640]{1,0:T(8,128)(2,1)} %param.25) | copy-start | bytes 4915204
  0.0 7.1 %copy-start.5 = (s32[64,4]{0,1:T(4,128)S(1)}, s32[64,4]{0,1:T(4,128)}, u32[]{:S(2)}) copy-start(s32[64,4]{0,1:T(4,128)} %param.26) | copy-start | bytes 3076
  0.0 7.2 %copy-start.6 = (s32[256]{0:T(256)S(1)}, s32[256]{0:T(256)}, u32[]{:S(2)}) copy-start(s32[256]{0:T(256)} %param.23) | copy-start | bytes 3076
  0.0 7.2 %copy-start.7 = (s32[256]{0:T(256)S(1)}, s32[256]{0:T(256)}, u32[]{:S(2)}) copy-start(s32[256]{0:T(256)} %param.22) | copy-start | bytes 3076
  0.0 7.2 %copy-start.8 = (s32[64]{0:T(128)S(1)}, s32[64]{0:T(128)}, u32[]{:S(2)}) copy-start(s32[64]{0:T(128)} %param.27) | copy-start | bytes 772
  2.2 13.0 %copy-start.3 = (f32[1280]{0:T(1024)S(1)}, f32[1280]{0:T(1024)}, u32[]{:S(2)}) copy-start(f32[1280]{0:T(1024)} %param.17) | copy-start | bytes 15364
  2.2 12.6 %all-to-all-start = ((bf16[256,4,320]{0,2,1:T(8,128)(2,1)}), bf16[256,4,320]{0,2,1:T(8,128)(2,1)S(1)}, u32[]{:S(2)}, u32[]{:S(2)}) async-start(bf16[256,4,320]{0,2,1:T(8,128)(2,1)} %bitcast.1), calls=%async_computation | async-start | bytes 1310720 | tf_op jit(solution)/shard_map/all_to_all | solution.py:109
  14.8 1.1 %copy-start.1 = (bf16[1280,320]{0,1:T(8,128)(2,1)S(1)}, bf16[1280,320]{0,1:T(8,128)(2,1)}, u32[]{:S(2)}) copy-start(bf16[1280,320]{0,1:T(8,128)(2,1)} %param.20) | copy-start | bytes 2457604
  19.0 18.4 %collective-permute-start = (bf16[264,640]{1,0:T(8,128)(2,1)}, bf16[264,640]{1,0:T(8,128)(2,1)}, u32[]{:S(2)}, u32[]{:S(2)}) collective-permute-start(bf16[264,640]{1,0:T(8,128)(2,1)} %fusion.4.b0), channel_id=1, source_target_pairs={{0,4},{4,8},{8,12},{12,16},{16,20},{20,24},{24,28},{28,32},{32,36}... | collective-permute-start | bytes 1013768 | tf_op jit(solution)/shard_map/ppermute | solution.py:20
  27.1 11.7 %collective-permute-start.1 = (bf16[264,640]{1,0:T(8,128)(2,1)}, bf16[264,640]{1,0:T(8,128)(2,1)}, u32[]{:S(2)}, u32[]{:S(2)}) collective-permute-start(bf16[264,640]{1,0:T(8,128)(2,1)} %fusion.4.b0), channel_id=1, source_target_pairs={{0,8},{4,12},{8,16},{12,20},{16,24},{20,28},{24,32},{28,36},{32,40... | collective-permute-start | bytes 1013768 | tf_op jit(solution)/shard_map/ppermute | solution.py:20
  31.8 11.1 %collective-permute-start.2 = (bf16[264,640]{1,0:T(8,128)(2,1)}, bf16[264,640]{1,0:T(8,128)(2,1)}, u32[]{:S(2)}, u32[]{:S(2)}) collective-permute-start(bf16[264,640]{1,0:T(8,128)(2,1)} %fusion.4.b0), channel_id=1, source_target_pairs={{4,0},{8,4},{12,8},{16,12},{20,16},{24,20},{28,24},{32,28},{36,32}... | collective-permute-start | bytes 1013768 | tf_op jit(solution)/shard_map/ppermute | solution.py:20
  33.8 12.2 %collective-permute-start.3 = (bf16[264,640]{1,0:T(8,128)(2,1)}, bf16[264,640]{1,0:T(8,128)(2,1)}, u32[]{:S(2)}, u32[]{:S(2)}) collective-permute-start(bf16[264,640]{1,0:T(8,128)(2,1)} %fusion.4.b0), channel_id=1, source_target_pairs={{8,0},{12,4},{16,8},{20,12},{24,16},{28,20},{32,24},{36,28},{40,32... | collective-permute-start | bytes 1013768 | tf_op jit(solution)/shard_map/ppermute | solution.py:20
  52.3 2.2 %copy-start.2 = (bf16[320,1280]{1,0:T(8,128)(2,1)S(1)}, bf16[320,1280]{1,0:T(8,128)(2,1)}, u32[]{:S(2)}) copy-start(bf16[320,1280]{1,0:T(8,128)(2,1)} %param.21) | copy-start | bytes 2457604
  55.9 12.2 %all-to-all-start.1 = ((bf16[4,64,1280]{2,1,0:T(8,128)(2,1)}), bf16[4,64,1280]{2,1,0:T(8,128)(2,1)}, u32[]{:S(2)}, u32[]{:S(2)}) async-start(bf16[4,64,1280]{2,1,0:T(8,128)(2,1)} %bitcast.7), calls=%async_computation.1 | async-start | bytes 1310720 | tf_op jit(solution)/shard_map/all_to_all | solution.py:135
  61.2 8.6 %copy-start.4 = (f32[1280]{0:T(1024)S(1)}, f32[1280]{0:T(1024)}, u32[]{:S(2)}) copy-start(f32[1280]{0:T(1024)} %param.24) | copy-start | bytes 15364
  71.0 8.1 %all-to-all-start.2 = ((bf16[64,4,160]{2,0,1:T(8,128)(2,1)}), bf16[64,4,160]{2,0,1:T(8,128)(2,1)S(1)}, u32[]{:S(2)}, u32[]{:S(2)}) async-start(bf16[64,4,160]{2,0,1:T(8,128)(2,1)} %copy.56), calls=%async_computation.2 | async-start | bytes 262144 | tf_op jit(solution)/shard_map/all_to_all | solution.py:144

commit v7 on v6

--- a/solution.py
+++ b/solution.py
@@ -20,7 +20,7 @@
     return lax.ppermute(shard, axis, pairs)
 
 
-def attn_kernel(heads, rows, qcode_ref, q_ref, b0, b1, b2, b3, b4, out_ref):
+def attn_kernel(heads, rows, qcode_ref, order_ref, q_ref, w_ref, b0, b1, b2, b3, b4, out_ref):
     blocks = (b0, b1, b2, b3, b4)
     scale = HD ** (-0.5)
     qcode = qcode_ref[...]
@@ -35,6 +35,8 @@
         if b == 0:
             m = m | diag
         masks.append(m)
+    pick = (order_ref[...] == col_id).astype(jnp.bfloat16)
+    mixed = None
     for h in range(heads):
         q = q_ref[:, h * HD:(h + 1) * HD]
         scores = []
@@ -55,25 +57,33 @@
             v = blk[0:rows, width + h * HD:width + (h + 1) * HD]
             p = jnp.dot(w, v, preferred_element_type=jnp.float32)
             acc = p if acc is None else acc + p
-        out_ref[:, h * HD:(h + 1) * HD] = acc.astype(out_ref.dtype)
+        ordered = jnp.dot(pick, acc.astype(jnp.bfloat16), preferred_element_type=jnp.float32)
+        part = jnp.dot(
+            ordered.astype(jnp.bfloat16), w_ref[h * HD:(h + 1) * HD, :],
+            preferred_element_type=jnp.float32,
+        )
+        mixed = part if mixed is None else mixed + part
+    out_ref[...] = mixed.astype(out_ref.dtype)
 
 
-def attention(qcode, q, blocks):
+def attention(qcode, order, q, w_out, blocks):
     rows, width = q.shape
     heads = width // HD
+    out_width = w_out.shape[1]
     vmem = pl.BlockSpec(memory_space=pltpu.VMEM)
     flops = 2 * 2 * heads * rows * rows * len(blocks) * HD
+    flops += 2 * rows * rows * width + 2 * rows * width * out_width
     return pl.pallas_call(
         functools.partial(attn_kernel, heads, rows),
-        out_shape=jax.ShapeDtypeStruct((rows, width), jnp.bfloat16),
-        in_specs=[vmem] * (2 + len(blocks)),
+        out_shape=jax.ShapeDtypeStruct((rows, out_width), jnp.bfloat16),
+        in_specs=[vmem] * (4 + len(blocks)),
         out_specs=vmem,
         cost_estimate=pl.CostEstimate(
             flops=flops,
             transcendentals=heads * rows * rows * len(blocks),
-            bytes_accessed=sum(b.size * 2 for b in blocks) + q.size * 4,
+            bytes_accessed=sum(b.size * 2 for b in blocks) + q.size * 2 + w_out.size * 2 + rows * out_width * 2,
         ),
-    )(qcode, q, *blocks)
+    )(qcode, order, q, w_out, *blocks)
 
 
 def layer_norm(activations, norm_gain):
@@ -124,13 +134,9 @@
     for offset in (1, 2, -1, -2):
         pair_list.append(from_behind(paired, "seq", offset))
     query_code = code_query.astype(jnp.float32)[:, None]
-    attended = attention(query_code, queries, pair_list)
-
     local_index = merge_index - seq_index * row_count
     order = local_index.T.reshape(row_count)
-    attended_sorted = jnp.take(attended, order, axis=0)
-    partial_sum = jnp.dot(attended_sorted, w_out, preferred_element_type=jnp.float32)
-    partial_sum = partial_sum.astype(jnp.bfloat16)
+    partial_sum = attention(query_code, order[:, None], queries, w_out, pair_list)
     chunk = row_count // tp_size
     pieces = lax.all_to_all(partial_sum, "tp", 0, 0, tiled=True)
     mixed_sum = jnp.sum(pieces.reshape(tp_size, chunk, -1).astype(jnp.float32), axis=0)

time: 114 us -> 114 us (level)
  Pallas kernels: 6.35 us -> 9.17 us
  matrix products: 6.42 us -> 5.02 us
    pallas_call x1, Pallas kernels: 6.35 us -> 9.17 us  [attention(): pl.pallas_call(functools.partial(attn_kernel, heads, rows), out_shape=jax...]
    gather x1 -> x0, local copies, waits for them, and re-layouts: 2.17 us -> none  [body(): attended_sorted = jnp.take(attended, order, axis=0)]
    ppermute x4, waiting for transfers between devices: 8.48 us -> 6.69 us  [from_behind(): return lax.ppermute(shard, axis, pairs)]
    dot_general x1 -> x0, matrix products: 1.41 us -> none  [body(): jnp.dot(attended_sorted, w_out, preferred_element_type=jnp.float32)]
    dot_general x1, matrix products: 0.38 us -> 1.54 us  [body(): jnp.dot(normed, w_value, preferred_element_type=jnp.float32)]
    dot_general x1, matrix products: 1.53 us -> 0.38 us  [body(): jnp.dot(normed, w_key, preferred_element_type=jnp.float32)]
  transfers between devices with their start and end apart: 7 -> 7, of which waited for: 6 -> 5; matrix products, arithmetic and copies ran while one was open for 4% -> 5% of each run, Pallas kernels for 0% -> 0%
where the time goes in v7:
time: 114 us; the launch traced here: 113 us
  blocking collectives  31.9 us (28%)
  starting transfers between devices  28.5 us (25%)
  waiting for transfers between devices  25.5 us (22%)
  Pallas kernels  9.17 us (8%)
  local copies, waits for them, and re-layouts  6.72 us (6%)
  other arithmetic  6.34 us (6%)
  matrix products  5.02 us (4%)
    all_to_all x1, blocking collectives, body(): lax.all_to_all(send_buf, 'seq', 0, 0, tiled=True)  31.9 us
    ppermute x4, starting transfers between devices, from_behind(): return lax.ppermute(shard, axis, pairs)  16 us
    pallas_call x1, Pallas kernels, attention(): pl.pallas_call(functools.partial(attn_kernel, heads, rows), out_shape=jax...  9.17 us
    all_to_all x1, waiting for transfers between devices, body(): lax.all_to_all(jnp.concatenate([tokens] * tp_size, axis=1), 'tp', 1, 1, t...  7.56 us
    all_to_all x1, waiting for transfers between devices, body(): pieces = lax.all_to_all(partial_sum, 'tp', 0, 0, tiled=True)  6.88 us
    ppermute x4, waiting for transfers between devices, from_behind(): return lax.ppermute(shard, axis, pairs)  6.69 us
    all_to_all x1, starting transfers between devices, body(): lax.all_to_all(jnp.concatenate([tokens] * tp_size, axis=1), 'tp', 1, 1, t...  4.96 us
    all_to_all x1, waiting for transfers between devices, body(): proj_pieces = lax.all_to_all(partial_proj, 'tp', 1, 0, tiled=True)  4.42 us
  transfers between devices with their start and end apart: 7, of which 5 were waited for; matrix products, arithmetic and copies ran while one was open for 5% of the time, Pallas kernels for 0%

profile of v7, /device:TPU:1, one launch (start us, length us, event | category | flops | bytes accessed | tf_op | source)
XLA Modules:
  0.0 113.5 jit_solution(39280919694136714)
XLA Ops:
  0.0 2.1 %pad_maximum_fusion = bf16[256,1280]{0,1:T(8,128)(2,1)} fusion(bf16[256,320]{0,1:T(8,128)(2,1)} %param.16), kind=kLoop, calls=%fused_computation.15 | loop fusion | flops 2621440 | bytes 819200 | tf_op jit(solution)/shard_map/concatenate | solution.py:120
  2.2 5.0 %all-to-all-start = ((bf16[256,4,320]{0,2,1:T(8,128)(2,1)}), bf16[256,4,320]{0,2,1:T(8,128)(2,1)S(1)}, u32[]{:S(2)}, u32[]{:S(2)}) async-start(bf16[256,4,320]{0,2,1:T(8,128)(2,1)} %bitcast.1), calls=%async_computation | async-start | bytes 1310720 | tf_op jit(solution)/shard_map/all_to_all | solution.py:119
  7.2 7.6 %all-to-all-done = bf16[256,4,320]{0,2,1:T(8,128)(2,1)S(1)} async-done(((bf16[256,4,320]{0,2,1:T(8,128)(2,1)}), bf16[256,4,320]{0,2,1:T(8,128)(2,1)S(1)}, u32[]{:S(2)}, u32[]{:S(2)}) %all-to-all-start) | async-done | bytes 655392 | tf_op jit(solution)/shard_map/all_to_all | solution.py:119
  16.5 1.5 %convolution_convert_fusion = bf16[256,320]{0,1:T(8,128)(2,1)S(1)} fusion(bf16[1280,320]{0,1:T(8,128)(2,1)} %param.20, bf16[256,1280]{0,1:T(8,128)(2,1)S(1)} %multiply_convert_fusion), kind=kOutput, calls=%fused_computation.7 | convolution fusion | flops 209797120 | bytes 1638400 | tf_op jit(solution)/shard_map/dot_general | solution.py:126
  18.0 0.8 copy.59
  18.8 1.1 fusion.4.b0
  19.9 8.1 %collective-permute-start = (bf16[264,640]{1,0:T(8,128)(2,1)S(1)}, bf16[264,640]{1,0:T(8,128)(2,1)}, u32[]{:S(2)}, u32[]{:S(2)}) collective-permute-start(bf16[264,640]{1,0:T(8,128)(2,1)S(1)} %fusion.4.b0), channel_id=1, source_target_pairs={{0,4},{4,8},{8,12},{12,16},{16,20},{20,24},{24,28},{28,32},{32,36}... | collective-permute-start | bytes 1013768 | tf_op jit(solution)/shard_map/ppermute | solution.py:20
  28.0 4.7 %collective-permute-start.1 = (bf16[264,640]{1,0:T(8,128)(2,1)S(1)}, bf16[264,640]{1,0:T(8,128)(2,1)}, u32[]{:S(2)}, u32[]{:S(2)}) collective-permute-start(bf16[264,640]{1,0:T(8,128)(2,1)S(1)} %fusion.4.b0), channel_id=1, source_target_pairs={{0,8},{4,12},{8,16},{12,20},{16,24},{20,28},{24,32},{28,36},{32,40... | collective-permute-start | bytes 1013768 | tf_op jit(solution)/shard_map/ppermute | solution.py:20
  32.7 1.9 %collective-permute-start.2 = (bf16[264,640]{1,0:T(8,128)(2,1)S(1)}, bf16[264,640]{1,0:T(8,128)(2,1)}, u32[]{:S(2)}, u32[]{:S(2)}) collective-permute-start(bf16[264,640]{1,0:T(8,128)(2,1)S(1)} %fusion.4.b0), channel_id=1, source_target_pairs={{4,0},{8,4},{12,8},{16,12},{20,16},{24,20},{28,24},{32,28},{36,32}... | collective-permute-start | bytes 1013768 | tf_op jit(solution)/shard_map/ppermute | solution.py:20
  34.7 1.3 %collective-permute-start.3 = (bf16[264,640]{1,0:T(8,128)(2,1)S(1)}, bf16[264,640]{1,0:T(8,128)(2,1)}, u32[]{:S(2)}, u32[]{:S(2)}) collective-permute-start(bf16[264,640]{1,0:T(8,128)(2,1)S(1)} %fusion.4.b0), channel_id=1, source_target_pairs={{8,0},{12,4},{16,8},{20,12},{24,16},{28,20},{32,24},{36,28},{40,32... | collective-permute-start | bytes 1013768 | tf_op jit(solution)/shard_map/ppermute | solution.py:20
  36.0 0.8 broadcast_in_dim_reshape.4.order_ref
  36.8 0.8 copy.60.qcode_ref
  37.6 1.5 %convolution_convert_fusion.2 = bf16[256,320]{0,1:T(8,128)(2,1)S(1)} fusion(bf16[1280,320]{0,1:T(8,128)(2,1)} %param.18, bf16[256,1280]{0,1:T(8,128)(2,1)S(1)} %multiply_convert_fusion), kind=kOutput, calls=%fused_computation.9 | convolution fusion | flops 209797120 | bytes 1638400 | tf_op jit(solution)/shard_map/dot_general | solution.py:124
  39.1 0.8 copy.62.q_ref
  39.9 3.7 %collective-permute-done.2.b3 = bf16[264,640]{1,0:T(8,128)(2,1)} collective-permute-done((bf16[264,640]{1,0:T(8,128)(2,1)S(1)}, bf16[264,640]{1,0:T(8,128)(2,1)}, u32[]{:S(2)}, u32[]{:S(2)}) %collective-permute-start.2) | collective-permute-done | bytes 337952 | tf_op jit(solution)/shard_map/ppermute | solution.py:20
  43.6 3.0 %collective-permute-done.3.b4 = bf16[264,640]{1,0:T(8,128)(2,1)} collective-permute-done((bf16[264,640]{1,0:T(8,128)(2,1)S(1)}, bf16[264,640]{1,0:T(8,128)(2,1)}, u32[]{:S(2)}, u32[]{:S(2)}) %collective-permute-start.3) | collective-permute-done | bytes 337952 | tf_op jit(solution)/shard_map/ppermute | solution.py:20
  46.6 9.2 %shard_map.118 = bf16[256,1280]{1,0:T(8,128)(2,1)} custom-call(f32[256,1]{1,0:T(8,128)} %copy.60.qcode_ref, s32[256,1]{1,0:T(8,128)} %broadcast_in_dim_reshape.4.order_ref, bf16[256,320]{1,0:T(8,128)(2,1)} %copy.62.q_ref, bf16[320,1280]{1,0:T(8,128)(2,1)} %w_ref.1, bf16[264,640]{1,0:T(8,128)(2,1)} %copy-done.1, bf16[264,640]{1,0:T(8,128)(2,1)} %collective-permute-done.b1, ...), custom_call_target="tpu_custom_call" | custom-call | flops 671088640 | bytes 3328000 | tf_op jit(solution)/shard_map/pallas_call | solution.py:76
  55.8 4.2 %all-to-all-start.1 = ((bf16[4,64,1280]{2,1,0:T(8,128)(2,1)}), bf16[4,64,1280]{2,1,0:T(8,128)(2,1)}, u32[]{:S(2)}, u32[]{:S(2)}) async-start(bf16[4,64,1280]{2,1,0:T(8,128)(2,1)} %bitcast.24), calls=%async_computation.1 | async-start | bytes 1310720 | tf_op jit(solution)/shard_map/all_to_all | solution.py:141
  61.2 6.9 %all-to-all-done.1 = bf16[4,64,1280]{2,1,0:T(8,128)(2,1)} async-done(((bf16[4,64,1280]{2,1,0:T(8,128)(2,1)}), bf16[4,64,1280]{2,1,0:T(8,128)(2,1)}, u32[]{:S(2)}, u32[]{:S(2)}) %all-to-all-start.1) | async-done | bytes 655392 | tf_op jit(solution)/shard_map/all_to_all | solution.py:141
  68.0 1.2 %convert_reduce_fusion.1 = f32[64,1280]{1,0:T(8,128)S(1)} fusion(bf16[4,64,1280]{2,1,0:T(8,128)(2,1)} %all-to-all-done.1), kind=kLoop, calls=%fused_computation.5 | loop fusion | flops 573440 | bytes 983040 | tf_op jit(solution)/shard_map/reduce_sum | solution.py:142
  71.0 3.3 %all-to-all-start.2 = ((bf16[64,4,160]{2,0,1:T(8,128)(2,1)}), bf16[64,4,160]{2,0,1:T(8,128)(2,1)S(1)}, u32[]{:S(2)}, u32[]{:S(2)}) async-start(bf16[64,4,160]{2,0,1:T(8,128)(2,1)} %copy.63), calls=%async_computation.2 | async-start | bytes 262144 | tf_op jit(solution)/shard_map/all_to_all | solution.py:150
  74.7 4.4 %all-to-all-done.2 = bf16[64,4,160]{2,0,1:T(8,128)(2,1)S(1)} async-done(((bf16[64,4,160]{2,0,1:T(8,128)(2,1)}), bf16[64,4,160]{2,0,1:T(8,128)(2,1)S(1)}, u32[]{:S(2)}, u32[]{:S(2)}) %all-to-all-start.2) | async-done | bytes 81952 | tf_op jit(solution)/shard_map/all_to_all | solution.py:150
  80.0 31.9 %all_to_all.40 = bf16[128,2,240]{2,1,0:T(2,128)(2,1)S(1)} all-to-all(bf16[128,2,240]{2,1,0:T(2,128)(2,1)S(1)} %reshape.164), channel_id=1, replica_groups=mesh['seq'=128,'tp'=4] {'seq'}, dimensions={0} | all-to-all | bytes 245760 | tf_op jit(solution)/shard_map/all_to_all | solution.py:171
  112.7 0.8 convolution_convert_fusion.5
  (59 shorter events, 6.6 us)
Async XLA Ops:
  0.0 69.7 %copy-start = (bf16[1280,640]{1,0:T(8,128)(2,1)S(1)}, bf16[1280,640]{1,0:T(8,128)(2,1)}, u32[]{:S(2)}) copy-start(bf16[1280,640]{1,0:T(8,128)(2,1)} %param.25) | copy-start | bytes 4915204
  0.0 7.1 %copy-start.7 = (s32[256]{0:T(256)S(1)}, s32[256]{0:T(256)}, u32[]{:S(2)}) copy-start(s32[256]{0:T(256)} %param.22) | copy-start | bytes 3076
  0.0 7.1 %copy-start.6 = (s32[256]{0:T(256)S(1)}, s32[256]{0:T(256)}, u32[]{:S(2)}) copy-start(s32[256]{0:T(256)} %param.23) | copy-start | bytes 3076
  0.0 7.2 %copy-start.5 = (s32[64,4]{0,1:T(4,128)S(1)}, s32[64,4]{0,1:T(4,128)}, u32[]{:S(2)}) copy-start(s32[64,4]{0,1:T(4,128)} %param.26) | copy-start | bytes 3076
  2.2 13.0 %copy-start.3 = (f32[1280]{0:T(1024)S(1)}, f32[1280]{0:T(1024)}, u32[]{:S(2)}) copy-start(f32[1280]{0:T(1024)} %param.17) | copy-start | bytes 15364
  2.2 12.6 %all-to-all-start = ((bf16[256,4,320]{0,2,1:T(8,128)(2,1)}), bf16[256,4,320]{0,2,1:T(8,128)(2,1)S(1)}, u32[]{:S(2)}, u32[]{:S(2)}) async-start(bf16[256,4,320]{0,2,1:T(8,128)(2,1)} %bitcast.1), calls=%async_computation | async-start | bytes 1310720 | tf_op jit(solution)/shard_map/all_to_all | solution.py:119
  14.8 1.1 %copy-start.2 = (bf16[1280,320]{0,1:T(8,128)(2,1)S(1)}, bf16[1280,320]{0,1:T(8,128)(2,1)}, u32[]{:S(2)}) copy-start(bf16[1280,320]{0,1:T(8,128)(2,1)} %param.19) | copy-start | bytes 2457604
  16.5 19.5 %copy-start.8 = (s32[64]{0:T(128)S(1)}, s32[64]{0:T(128)}, u32[]{:S(2)}) copy-start(s32[64]{0:T(128)} %param.27) | copy-start | bytes 772
  19.9 26.7 %copy-start.1 = (bf16[264,640]{1,0:T(8,128)(2,1)}, bf16[264,640]{1,0:T(8,128)(2,1)S(1)}, u32[]{:S(2)}) copy-start(bf16[264,640]{1,0:T(8,128)(2,1)S(1)} %fusion.4.b0) | copy-start | bytes 1013764
  19.9 20.0 %collective-permute-start = (bf16[264,640]{1,0:T(8,128)(2,1)S(1)}, bf16[264,640]{1,0:T(8,128)(2,1)}, u32[]{:S(2)}, u32[]{:S(2)}) collective-permute-start(bf16[264,640]{1,0:T(8,128)(2,1)S(1)} %fusion.4.b0), channel_id=1, source_target_pairs={{0,4},{4,8},{8,12},{12,16},{16,20},{20,24},{24,28},{28,32},{32,36}... | collective-permute-start | bytes 1013768 | tf_op jit(solution)/shard_map/ppermute | solution.py:20
  28.0 11.9 %collective-permute-start.1 = (bf16[264,640]{1,0:T(8,128)(2,1)S(1)}, bf16[264,640]{1,0:T(8,128)(2,1)}, u32[]{:S(2)}, u32[]{:S(2)}) collective-permute-start(bf16[264,640]{1,0:T(8,128)(2,1)S(1)} %fusion.4.b0), channel_id=1, source_target_pairs={{0,8},{4,12},{8,16},{12,20},{16,24},{20,28},{24,32},{28,36},{32,40... | collective-permute-start | bytes 1013768 | tf_op jit(solution)/shard_map/ppermute | solution.py:20
  32.7 10.9 %collective-permute-start.2 = (bf16[264,640]{1,0:T(8,128)(2,1)S(1)}, bf16[264,640]{1,0:T(8,128)(2,1)}, u32[]{:S(2)}, u32[]{:S(2)}) collective-permute-start(bf16[264,640]{1,0:T(8,128)(2,1)S(1)} %fusion.4.b0), channel_id=1, source_target_pairs={{4,0},{8,4},{12,8},{16,12},{20,16},{24,20},{28,24},{32,28},{36,32}... | collective-permute-start | bytes 1013768 | tf_op jit(solution)/shard_map/ppermute | solution.py:20
  34.7 11.9 %collective-permute-start.3 = (bf16[264,640]{1,0:T(8,128)(2,1)S(1)}, bf16[264,640]{1,0:T(8,128)(2,1)}, u32[]{:S(2)}, u32[]{:S(2)}) collective-permute-start(bf16[264,640]{1,0:T(8,128)(2,1)S(1)} %fusion.4.b0), channel_id=1, source_target_pairs={{8,0},{12,4},{16,8},{20,12},{24,16},{28,20},{32,24},{36,28},{40,32... | collective-permute-start | bytes 1013768 | tf_op jit(solution)/shard_map/ppermute | solution.py:20
  55.8 12.3 %all-to-all-start.1 = ((bf16[4,64,1280]{2,1,0:T(8,128)(2,1)}), bf16[4,64,1280]{2,1,0:T(8,128)(2,1)}, u32[]{:S(2)}, u32[]{:S(2)}) async-start(bf16[4,64,1280]{2,1,0:T(8,128)(2,1)} %bitcast.24), calls=%async_computation.1 | async-start | bytes 1310720 | tf_op jit(solution)/shard_map/all_to_all | solution.py:141
  61.1 8.6 %copy-start.4 = (f32[1280]{0:T(1024)S(1)}, f32[1280]{0:T(1024)}, u32[]{:S(2)}) copy-start(f32[1280]{0:T(1024)} %param.24) | copy-start | bytes 15364
  71.0 8.1 %all-to-all-start.2 = ((bf16[64,4,160]{2,0,1:T(8,128)(2,1)}), bf16[64,4,160]{2,0,1:T(8,128)(2,1)S(1)}, u32[]{:S(2)}, u32[]{:S(2)}) async-start(bf16[64,4,160]{2,0,1:T(8,128)(2,1)} %copy.63), calls=%async_computation.2 | async-start | bytes 262144 | tf_op jit(solution)/shard_map/all_to_all | solution.py:150

commit v8 on v7

--- a/solution.py
+++ b/solution.py
@@ -20,11 +20,13 @@
     return lax.ppermute(shard, axis, pairs)
 
 
-def attn_kernel(heads, rows, qcode_ref, order_ref, q_ref, w_ref, b0, b1, b2, b3, b4, out_ref):
+def attn_kernel(heads, rows, q_ref, w_ref, b0, b1, b2, b3, b4, out_ref, att_ref):
     blocks = (b0, b1, b2, b3, b4)
     scale = HD ** (-0.5)
-    qcode = qcode_ref[...]
     width = heads * HD
+    side = jnp.transpose(b0[rows:rows + 8, 0:rows].astype(jnp.float32))
+    qcode = side[:, 1:2]
+    order = side[:, 2:3]
     row_id = lax.broadcasted_iota(jnp.int32, (rows, rows), 0)
     col_id = lax.broadcasted_iota(jnp.int32, (rows, rows), 1)
     diag = row_id == col_id
@@ -35,8 +37,6 @@
         if b == 0:
             m = m | diag
         masks.append(m)
-    pick = (order_ref[...] == col_id).astype(jnp.bfloat16)
-    mixed = None
     for h in range(heads):
         q = q_ref[:, h * HD:(h + 1) * HD]
         scores = []
@@ -57,16 +57,14 @@
             v = blk[0:rows, width + h * HD:width + (h + 1) * HD]
             p = jnp.dot(w, v, preferred_element_type=jnp.float32)
             acc = p if acc is None else acc + p
-        ordered = jnp.dot(pick, acc.astype(jnp.bfloat16), preferred_element_type=jnp.float32)
-        part = jnp.dot(
-            ordered.astype(jnp.bfloat16), w_ref[h * HD:(h + 1) * HD, :],
-            preferred_element_type=jnp.float32,
-        )
-        mixed = part if mixed is None else mixed + part
+        att_ref[:, h * HD:(h + 1) * HD] = acc.astype(jnp.bfloat16)
+    pick = (order == col_id.astype(jnp.float32)).astype(jnp.bfloat16)
+    ordered = jnp.dot(pick, att_ref[...], preferred_element_type=jnp.float32)
+    mixed = jnp.dot(ordered.astype(jnp.bfloat16), w_ref[...], preferred_element_type=jnp.float32)
     out_ref[...] = mixed.astype(out_ref.dtype)
 
 
-def attention(qcode, order, q, w_out, blocks):
+def attention(q, w_out, blocks):
     rows, width = q.shape
     heads = width // HD
     out_width = w_out.shape[1]
@@ -76,14 +74,15 @@
     return pl.pallas_call(
         functools.partial(attn_kernel, heads, rows),
         out_shape=jax.ShapeDtypeStruct((rows, out_width), jnp.bfloat16),
-        in_specs=[vmem] * (4 + len(blocks)),
+        in_specs=[vmem] * (2 + len(blocks)),
         out_specs=vmem,
+        scratch_shapes=[pltpu.VMEM((rows, width), jnp.bfloat16)],
         cost_estimate=pl.CostEstimate(
             flops=flops,
             transcendentals=heads * rows * rows * len(blocks),
             bytes_accessed=sum(b.size * 2 for b in blocks) + q.size * 2 + w_out.size * 2 + rows * out_width * 2,
         ),
-    )(qcode, order, q, w_out, *blocks)
+    )(q, w_out, *blocks)
 
 
 def layer_norm(activations, norm_gain):
@@ -127,16 +126,16 @@
     code_query = segment_ids + 1
     code_key = jnp.where(keep_mask > 0, code_query, 0)
     pair_width = 2 * local_width
+    local_index = merge_index - seq_index * row_count
+    order = local_index.T.reshape(row_count)
+    code_rows = jnp.stack([code_key, code_query, order]).astype(jnp.bfloat16)
     code_block = jnp.zeros((8, pair_width), jnp.bfloat16)
-    code_block = code_block.at[0, :row_count].set(code_key.astype(jnp.bfloat16))
+    code_block = code_block.at[0:3, :row_count].set(code_rows)
     paired = jnp.concatenate([jnp.concatenate([key_rows, value_rows], axis=1), code_block], axis=0)
     pair_list = [paired]
     for offset in (1, 2, -1, -2):
         pair_list.append(from_behind(paired, "seq", offset))
-    query_code = code_query.astype(jnp.float32)[:, None]
-    local_index = merge_index - seq_index * row_count
-    order = local_index.T.reshape(row_count)
-    partial_sum = attention(query_code, order[:, None], queries, w_out, pair_list)
+    partial_sum = attention(queries, w_out, pair_list)
     chunk = row_count // tp_size
     pieces = lax.all_to_all(partial_sum, "tp", 0, 0, tiled=True)
     mixed_sum = jnp.sum(pieces.reshape(tp_size, chunk, -1).astype(jnp.float32), axis=0)

time: 114 us -> 114 us (level)
  local copies, waits for them, and re-layouts: 6.72 us -> 5.22 us
  waiting for transfers between devices: 25.5 us -> 27 us
    ppermute x4, waiting for transfers between devices: 6.69 us -> 8.27 us  [from_behind(): return lax.ppermute(shard, axis, pairs)]
  transfers between devices with their start and end apart: 7 -> 7, of which waited for: 5 -> 6; matrix products, arithmetic and copies ran while one was open for 5% -> 4% of each run, Pallas kernels for 0% -> 0%
where the time goes in v8:
time: 114 us; the launch traced here: 113 us
  blocking collectives  31.9 us (28%)
  starting transfers between devices  28.5 us (25%)
  waiting for transfers between devices  27 us (24%)
  Pallas kernels  9.05 us (8%)
  other arithmetic  6.34 us (6%)
  local copies, waits for them, and re-layouts  5.22 us (5%)
  matrix products  5.02 us (4%)
    all_to_all x1, blocking collectives, body(): lax.all_to_all(send_buf, 'seq', 0, 0, tiled=True)  31.9 us
    ppermute x4, starting transfers between devices, from_behind(): return lax.ppermute(shard, axis, pairs)  16 us
    pallas_call x1, Pallas kernels, attention(): pl.pallas_call(functools.partial(attn_kernel, heads, rows), out_shape=jax...  9.05 us
    ppermute x4, waiting for transfers between devices, from_behind(): return lax.ppermute(shard, axis, pairs)  8.27 us
    all_to_all x1, waiting for transfers between devices, body(): lax.all_to_all(jnp.concatenate([tokens] * tp_size, axis=1), 'tp', 1, 1, t...  7.48 us
    all_to_all x1, waiting for transfers between devices, body(): pieces = lax.all_to_all(partial_sum, 'tp', 0, 0, tiled=True)  6.86 us
    all_to_all x1, starting transfers between devices, body(): lax.all_to_all(jnp.concatenate([tokens] * tp_size, axis=1), 'tp', 1, 1, t...  4.96 us
    all_to_all x1, waiting for transfers between devices, body(): proj_pieces = lax.all_to_all(partial_proj, 'tp', 1, 0, tiled=True)  4.42 us
  transfers between devices with their start and end apart: 7, of which 6 were waited for; matrix products, arithmetic and copies ran while one was open for 4% of the time, Pallas kernels for 0%

profile of v8, /device:TPU:1, one launch (start us, length us, event | category | flops | bytes accessed | tf_op | source)
XLA Modules:
  0.0 113.4 jit_solution(11843415908825773904)
XLA Ops:
  0.0 2.1 %pad_maximum_fusion = bf16[256,1280]{0,1:T(8,128)(2,1)} fusion(bf16[256,320]{0,1:T(8,128)(2,1)} %param.16), kind=kLoop, calls=%fused_computation.13 | loop fusion | flops 2621440 | bytes 819200 | tf_op jit(solution)/shard_map/concatenate | solution.py:119
  2.2 5.0 %all-to-all-start = ((bf16[256,4,320]{0,2,1:T(8,128)(2,1)}), bf16[256,4,320]{0,2,1:T(8,128)(2,1)S(1)}, u32[]{:S(2)}, u32[]{:S(2)}) async-start(bf16[256,4,320]{0,2,1:T(8,128)(2,1)} %bitcast.1), calls=%async_computation | async-start | bytes 1310720 | tf_op jit(solution)/shard_map/all_to_all | solution.py:118
  7.3 7.5 %all-to-all-done = bf16[256,4,320]{0,2,1:T(8,128)(2,1)S(1)} async-done(((bf16[256,4,320]{0,2,1:T(8,128)(2,1)}), bf16[256,4,320]{0,2,1:T(8,128)(2,1)S(1)}, u32[]{:S(2)}, u32[]{:S(2)}) %all-to-all-start) | async-done | bytes 655392 | tf_op jit(solution)/shard_map/all_to_all | solution.py:118
  16.5 1.5 %convolution_convert_fusion = bf16[256,320]{0,1:T(8,128)(2,1)S(1)} fusion(bf16[1280,320]{0,1:T(8,128)(2,1)} %param.20, bf16[256,1280]{0,1:T(8,128)(2,1)S(1)} %multiply_convert_fusion), kind=kOutput, calls=%fused_computation.7 | convolution fusion | flops 209797120 | bytes 1638400 | tf_op jit(solution)/shard_map/dot_general | solution.py:125
  18.0 0.8 copy.51
  18.8 1.1 pad_maximum_fusion.1.b0
  19.9 8.1 %collective-permute-start = (bf16[264,640]{1,0:T(8,128)(2,1)S(1)}, bf16[264,640]{1,0:T(8,128)(2,1)}, u32[]{:S(2)}, u32[]{:S(2)}) collective-permute-start(bf16[264,640]{1,0:T(8,128)(2,1)S(1)} %pad_maximum_fusion.1.b0), channel_id=1, source_target_pairs={{0,4},{4,8},{8,12},{12,16},{16,20},{20,24},{24,28},{28,32},{32,36}... | collective-permute-start | bytes 1013768 | tf_op jit(solution)/shard_map/ppermute | solution.py:20
  28.0 4.7 %collective-permute-start.1 = (bf16[264,640]{1,0:T(8,128)(2,1)S(1)}, bf16[264,640]{1,0:T(8,128)(2,1)}, u32[]{:S(2)}, u32[]{:S(2)}) collective-permute-start(bf16[264,640]{1,0:T(8,128)(2,1)S(1)} %pad_maximum_fusion.1.b0), channel_id=1, source_target_pairs={{0,8},{4,12},{8,16},{12,20},{16,24},{20,28},{24,32},{28,36},{32,40... | collective-permute-start | bytes 1013768 | tf_op jit(solution)/shard_map/ppermute | solution.py:20
  32.7 1.9 %collective-permute-start.2 = (bf16[264,640]{1,0:T(8,128)(2,1)S(1)}, bf16[264,640]{1,0:T(8,128)(2,1)}, u32[]{:S(2)}, u32[]{:S(2)}) collective-permute-start(bf16[264,640]{1,0:T(8,128)(2,1)S(1)} %pad_maximum_fusion.1.b0), channel_id=1, source_target_pairs={{4,0},{8,4},{12,8},{16,12},{20,16},{24,20},{28,24},{32,28},{36,32}... | collective-permute-start | bytes 1013768 | tf_op jit(solution)/shard_map/ppermute | solution.py:20
  34.7 1.3 %collective-permute-start.3 = (bf16[264,640]{1,0:T(8,128)(2,1)S(1)}, bf16[264,640]{1,0:T(8,128)(2,1)}, u32[]{:S(2)}, u32[]{:S(2)}) collective-permute-start(bf16[264,640]{1,0:T(8,128)(2,1)S(1)} %pad_maximum_fusion.1.b0), channel_id=1, source_target_pairs={{8,0},{12,4},{16,8},{20,12},{24,16},{28,20},{32,24},{36,28},{40,32... | collective-permute-start | bytes 1013768 | tf_op jit(solution)/shard_map/ppermute | solution.py:20
  36.0 1.5 %convolution_convert_fusion.2 = bf16[256,320]{0,1:T(8,128)(2,1)S(1)} fusion(bf16[1280,320]{0,1:T(8,128)(2,1)} %param.18, bf16[256,1280]{0,1:T(8,128)(2,1)S(1)} %multiply_convert_fusion), kind=kOutput, calls=%fused_computation.9 | convolution fusion | flops 209797120 | bytes 1638400 | tf_op jit(solution)/shard_map/dot_general | solution.py:123
  37.5 0.8 copy.52.q_ref
  38.3 1.0 collective-permute-done.1.b2
  39.3 4.3 %collective-permute-done.2.b3 = bf16[264,640]{1,0:T(8,128)(2,1)} collective-permute-done((bf16[264,640]{1,0:T(8,128)(2,1)S(1)}, bf16[264,640]{1,0:T(8,128)(2,1)}, u32[]{:S(2)}, u32[]{:S(2)}) %collective-permute-start.2) | collective-permute-done | bytes 337952 | tf_op jit(solution)/shard_map/ppermute | solution.py:20
  43.6 3.0 %collective-permute-done.3.b4 = bf16[264,640]{1,0:T(8,128)(2,1)} collective-permute-done((bf16[264,640]{1,0:T(8,128)(2,1)S(1)}, bf16[264,640]{1,0:T(8,128)(2,1)}, u32[]{:S(2)}, u32[]{:S(2)}) %collective-permute-start.3) | collective-permute-done | bytes 337952 | tf_op jit(solution)/shard_map/ppermute | solution.py:20
  46.6 9.0 %shard_map.118 = bf16[256,1280]{1,0:T(8,128)(2,1)} custom-call(bf16[256,320]{1,0:T(8,128)(2,1)} %copy.52.q_ref, bf16[320,1280]{1,0:T(8,128)(2,1)} %w_ref.1, bf16[264,640]{1,0:T(8,128)(2,1)} %copy-done.1, bf16[264,640]{1,0:T(8,128)(2,1)} %collective-permute-done.b1, bf16[264,640]{1,0:T(8,128)(2,1)} %collective-permute-done.1.b2, ...), custom_call_target="tpu_custom_call" | custom-call | flops 671088640 | bytes 3328000 | tf_op jit(solution)/shard_map/pallas_call | solution.py:74
  55.6 4.2 %all-to-all-start.1 = ((bf16[4,64,1280]{2,1,0:T(8,128)(2,1)}), bf16[4,64,1280]{2,1,0:T(8,128)(2,1)}, u32[]{:S(2)}, u32[]{:S(2)}) async-start(bf16[4,64,1280]{2,1,0:T(8,128)(2,1)} %bitcast.23), calls=%async_computation.1 | async-start | bytes 1310720 | tf_op jit(solution)/shard_map/all_to_all | solution.py:140
  60.3 0.7 gather_fusion
  61.0 6.9 %all-to-all-done.1 = bf16[4,64,1280]{2,1,0:T(8,128)(2,1)} async-done(((bf16[4,64,1280]{2,1,0:T(8,128)(2,1)}), bf16[4,64,1280]{2,1,0:T(8,128)(2,1)}, u32[]{:S(2)}, u32[]{:S(2)}) %all-to-all-start.1) | async-done | bytes 655392 | tf_op jit(solution)/shard_map/all_to_all | solution.py:140
  67.9 1.2 %convert_reduce_fusion.1 = f32[64,1280]{1,0:T(8,128)S(1)} fusion(bf16[4,64,1280]{2,1,0:T(8,128)(2,1)} %all-to-all-done.1), kind=kLoop, calls=%fused_computation.5 | loop fusion | flops 573440 | bytes 983040 | tf_op jit(solution)/shard_map/reduce_sum | solution.py:141
  70.8 3.3 %all-to-all-start.2 = ((bf16[64,4,160]{2,0,1:T(8,128)(2,1)}), bf16[64,4,160]{2,0,1:T(8,128)(2,1)S(1)}, u32[]{:S(2)}, u32[]{:S(2)}) async-start(bf16[64,4,160]{2,0,1:T(8,128)(2,1)} %copy.53), calls=%async_computation.2 | async-start | bytes 262144 | tf_op jit(solution)/shard_map/all_to_all | solution.py:149
  74.5 4.4 %all-to-all-done.2 = bf16[64,4,160]{2,0,1:T(8,128)(2,1)S(1)} async-done(((bf16[64,4,160]{2,0,1:T(8,128)(2,1)}), bf16[64,4,160]{2,0,1:T(8,128)(2,1)S(1)}, u32[]{:S(2)}, u32[]{:S(2)}) %all-to-all-start.2) | async-done | bytes 81952 | tf_op jit(solution)/shard_map/all_to_all | solution.py:149
  79.8 31.9 %all_to_all.40 = bf16[128,2,240]{2,1,0:T(2,128)(2,1)S(1)} all-to-all(bf16[128,2,240]{2,1,0:T(2,128)(2,1)S(1)} %reshape.163), channel_id=1, replica_groups=mesh['seq'=128,'tp'=4] {'seq'}, dimensions={0} | all-to-all | bytes 245760 | tf_op jit(solution)/shard_map/all_to_all | solution.py:170
  112.6 0.8 convolution_convert_fusion.5
  (59 shorter events, 6.0 us)
Async XLA Ops:
  0.0 69.6 %copy-start = (bf16[1280,640]{1,0:T(8,128)(2,1)S(1)}, bf16[1280,640]{1,0:T(8,128)(2,1)}, u32[]{:S(2)}) copy-start(bf16[1280,640]{1,0:T(8,128)(2,1)} %param.25) | copy-start | bytes 4915204
  0.0 7.1 %copy-start.5 = (s32[64,4]{0,1:T(4,128)S(1)}, s32[64,4]{0,1:T(4,128)}, u32[]{:S(2)}) copy-start(s32[64,4]{0,1:T(4,128)} %param.26) | copy-start | bytes 3076
  0.0 7.2 %copy-start.7 = (s32[256]{0:T(256)S(1)}, s32[256]{0:T(256)}, u32[]{:S(2)}) copy-start(s32[256]{0:T(256)} %param.22) | copy-start | bytes 3076
  0.0 7.2 %copy-start.6 = (s32[256]{0:T(256)S(1)}, s32[256]{0:T(256)}, u32[]{:S(2)}) copy-start(s32[256]{0:T(256)} %param.23) | copy-start | bytes 3076
  2.2 13.0 %copy-start.3 = (f32[1280]{0:T(1024)S(1)}, f32[1280]{0:T(1024)}, u32[]{:S(2)}) copy-start(f32[1280]{0:T(1024)} %param.17) | copy-start | bytes 15364
  2.2 12.6 %all-to-all-start = ((bf16[256,4,320]{0,2,1:T(8,128)(2,1)}), bf16[256,4,320]{0,2,1:T(8,128)(2,1)S(1)}, u32[]{:S(2)}, u32[]{:S(2)}) async-start(bf16[256,4,320]{0,2,1:T(8,128)(2,1)} %bitcast.1), calls=%async_computation | async-start | bytes 1310720 | tf_op jit(solution)/shard_map/all_to_all | solution.py:118
  14.8 1.1 %copy-start.2 = (bf16[1280,320]{0,1:T(8,128)(2,1)S(1)}, bf16[1280,320]{0,1:T(8,128)(2,1)}, u32[]{:S(2)}) copy-start(bf16[1280,320]{0,1:T(8,128)(2,1)} %param.19) | copy-start | bytes 2457604
  16.5 19.5 %copy-start.8 = (s32[64]{0:T(128)S(1)}, s32[64]{0:T(128)}, u32[]{:S(2)}) copy-start(s32[64]{0:T(128)} %param.27) | copy-start | bytes 772
  19.9 26.7 %copy-start.1 = (bf16[264,640]{1,0:T(8,128)(2,1)}, bf16[264,640]{1,0:T(8,128)(2,1)S(1)}, u32[]{:S(2)}) copy-start(bf16[264,640]{1,0:T(8,128)(2,1)S(1)} %pad_maximum_fusion.1.b0) | copy-start | bytes 1013764
  19.9 18.4 %collective-permute-start = (bf16[264,640]{1,0:T(8,128)(2,1)S(1)}, bf16[264,640]{1,0:T(8,128)(2,1)}, u32[]{:S(2)}, u32[]{:S(2)}) collective-permute-start(bf16[264,640]{1,0:T(8,128)(2,1)S(1)} %pad_maximum_fusion.1.b0), channel_id=1, source_target_pairs={{0,4},{4,8},{8,12},{12,16},{16,20},{20,24},{24,28},{28,32},{32,36}... | collective-permute-start | bytes 1013768 | tf_op jit(solution)/shard_map/ppermute | solution.py:20
  28.0 11.3 %collective-permute-start.1 = (bf16[264,640]{1,0:T(8,128)(2,1)S(1)}, bf16[264,640]{1,0:T(8,128)(2,1)}, u32[]{:S(2)}, u32[]{:S(2)}) collective-permute-start(bf16[264,640]{1,0:T(8,128)(2,1)S(1)} %pad_maximum_fusion.1.b0), channel_id=1, source_target_pairs={{0,8},{4,12},{8,16},{12,20},{16,24},{20,28},{24,32},{28,36},{32,40... | collective-permute-start | bytes 1013768 | tf_op jit(solution)/shard_map/ppermute | solution.py:20
  32.7 10.9 %collective-permute-start.2 = (bf16[264,640]{1,0:T(8,128)(2,1)S(1)}, bf16[264,640]{1,0:T(8,128)(2,1)}, u32[]{:S(2)}, u32[]{:S(2)}) collective-permute-start(bf16[264,640]{1,0:T(8,128)(2,1)S(1)} %pad_maximum_fusion.1.b0), channel_id=1, source_target_pairs={{4,0},{8,4},{12,8},{16,12},{20,16},{24,20},{28,24},{32,28},{36,32}... | collective-permute-start | bytes 1013768 | tf_op jit(solution)/shard_map/ppermute | solution.py:20
  34.7 11.9 %collective-permute-start.3 = (bf16[264,640]{1,0:T(8,128)(2,1)S(1)}, bf16[264,640]{1,0:T(8,128)(2,1)}, u32[]{:S(2)}, u32[]{:S(2)}) collective-permute-start(bf16[264,640]{1,0:T(8,128)(2,1)S(1)} %pad_maximum_fusion.1.b0), channel_id=1, source_target_pairs={{8,0},{12,4},{16,8},{20,12},{24,16},{28,20},{32,24},{36,28},{40,32... | collective-permute-start | bytes 1013768 | tf_op jit(solution)/shard_map/ppermute | solution.py:20
  55.6 12.2 %all-to-all-start.1 = ((bf16[4,64,1280]{2,1,0:T(8,128)(2,1)}), bf16[4,64,1280]{2,1,0:T(8,128)(2,1)}, u32[]{:S(2)}, u32[]{:S(2)}) async-start(bf16[4,64,1280]{2,1,0:T(8,128)(2,1)} %bitcast.23), calls=%async_computation.1 | async-start | bytes 1310720 | tf_op jit(solution)/shard_map/all_to_all | solution.py:140
  61.0 8.6 %copy-start.4 = (f32[1280]{0:T(1024)S(1)}, f32[1280]{0:T(1024)}, u32[]{:S(2)}) copy-start(f32[1280]{0:T(1024)} %param.24) | copy-start | bytes 15364
  70.8 8.1 %all-to-all-start.2 = ((bf16[64,4,160]{2,0,1:T(8,128)(2,1)}), bf16[64,4,160]{2,0,1:T(8,128)(2,1)S(1)}, u32[]{:S(2)}, u32[]{:S(2)}) async-start(bf16[64,4,160]{2,0,1:T(8,128)(2,1)} %copy.53), calls=%async_computation.2 | async-start | bytes 262144 | tf_op jit(solution)/shard_map/all_to_all | solution.py:149

commit v9 on v8

--- a/solution.py
+++ b/solution.py
@@ -20,19 +20,19 @@
     return lax.ppermute(shard, axis, pairs)
 
 
-def attn_kernel(heads, rows, q_ref, w_ref, b0, b1, b2, b3, b4, out_ref, att_ref):
-    blocks = (b0, b1, b2, b3, b4)
+def attn_kernel(heads, rows, span, q_ref, w_ref, b0, b1, b2, b3, out_ref, att_ref):
+    blocks = ((b0, 0), (b1, 0), (b2, 0), (b3, 0), (b3, span))
     scale = HD ** (-0.5)
     width = heads * HD
-    side = jnp.transpose(b0[rows:rows + 8, 0:rows].astype(jnp.float32))
+    side = jnp.transpose(b0[rows:rows + 16, 0:rows].astype(jnp.float32))
     qcode = side[:, 1:2]
     order = side[:, 2:3]
     row_id = lax.broadcasted_iota(jnp.int32, (rows, rows), 0)
     col_id = lax.broadcasted_iota(jnp.int32, (rows, rows), 1)
     diag = row_id == col_id
     masks = []
-    for b, blk in enumerate(blocks):
-        kcode = blk[rows:rows + 1, 0:rows].astype(jnp.float32)
+    for b, (blk, at) in enumerate(blocks):
+        kcode = blk[at + rows:at + rows + 1, 0:rows].astype(jnp.float32)
         m = qcode == kcode
         if b == 0:
             m = m | diag
@@ -40,8 +40,8 @@
     for h in range(heads):
         q = q_ref[:, h * HD:(h + 1) * HD]
         scores = []
-        for b, blk in enumerate(blocks):
-            k = blk[0:rows, h * HD:(h + 1) * HD]
+        for b, (blk, at) in enumerate(blocks):
+            k = blk[at:at + rows, h * HD:(h + 1) * HD]
             s = lax.dot_general(q, k, (((1,), (1,)), ((), ())), preferred_element_type=jnp.float32) * scale
             scores.append(jnp.where(masks[b], s, -1e30))
         row_max = scores[0].max(axis=1, keepdims=True)
@@ -52,9 +52,9 @@
         for e in exps[1:]:
             total = total + e.sum(axis=1, keepdims=True)
         acc = None
-        for b, blk in enumerate(blocks):
+        for b, (blk, at) in enumerate(blocks):
             w = (exps[b] / total).astype(jnp.bfloat16)
-            v = blk[0:rows, width + h * HD:width + (h + 1) * HD]
+            v = blk[at:at + rows, width + h * HD:width + (h + 1) * HD]
             p = jnp.dot(w, v, preferred_element_type=jnp.float32)
             acc = p if acc is None else acc + p
         att_ref[:, h * HD:(h + 1) * HD] = acc.astype(jnp.bfloat16)
@@ -69,17 +69,18 @@
     heads = width // HD
     out_width = w_out.shape[1]
     vmem = pl.BlockSpec(memory_space=pltpu.VMEM)
-    flops = 2 * 2 * heads * rows * rows * len(blocks) * HD
+    span = blocks[0].shape[0]
+    flops = 2 * 2 * heads * rows * rows * 5 * HD
     flops += 2 * rows * rows * width + 2 * rows * width * out_width
     return pl.pallas_call(
-        functools.partial(attn_kernel, heads, rows),
+        functools.partial(attn_kernel, heads, rows, span),
         out_shape=jax.ShapeDtypeStruct((rows, out_width), jnp.bfloat16),
         in_specs=[vmem] * (2 + len(blocks)),
         out_specs=vmem,
         scratch_shapes=[pltpu.VMEM((rows, width), jnp.bfloat16)],
         cost_estimate=pl.CostEstimate(
             flops=flops,
-            transcendentals=heads * rows * rows * len(blocks),
+            transcendentals=heads * rows * rows * 5,
             bytes_accessed=sum(b.size * 2 for b in blocks) + q.size * 2 + w_out.size * 2 + rows * out_width * 2,
         ),
     )(q, w_out, *blocks)
@@ -129,12 +130,16 @@
     local_index = merge_index - seq_index * row_count
     order = local_index.T.reshape(row_count)
     code_rows = jnp.stack([code_key, code_query, order]).astype(jnp.bfloat16)
-    code_block = jnp.zeros((8, pair_width), jnp.bfloat16)
+    code_block = jnp.zeros((16, pair_width), jnp.bfloat16)
     code_block = code_block.at[0:3, :row_count].set(code_rows)
     paired = jnp.concatenate([jnp.concatenate([key_rows, value_rows], axis=1), code_block], axis=0)
-    pair_list = [paired]
-    for offset in (1, 2, -1, -2):
-        pair_list.append(from_behind(paired, "seq", offset))
+    from_left = from_behind(paired, "seq", 2)
+    from_right = from_behind(paired, "seq", -2)
+    core = seq_index % 2
+    forward = jnp.where(core == 0, from_right, from_left)
+    swap_pairs = [(i, i ^ 1) for i in range(seq_size)]
+    swapped = lax.ppermute(jnp.concatenate([paired, forward], axis=0), "seq", swap_pairs)
+    pair_list = [paired, from_left, from_right, swapped]
     partial_sum = attention(queries, w_out, pair_list)
     chunk = row_count // tp_size
     pieces = lax.all_to_all(partial_sum, "tp", 0, 0, tiled=True)

time: 114 us -> 114 us (level)
  waiting for transfers between devices: 27 us -> 30.1 us
  starting transfers between devices: 28.5 us -> 25.8 us
  other arithmetic: 6.34 us -> 8.16 us
  blocking collectives: 31.9 us -> 30.6 us
    ppermute x4 -> x2, starting transfers between devices: 16 us -> 8.53 us  [from_behind(): return lax.ppermute(shard, axis, pairs)]
    ppermute x0 -> x1, starting transfers between devices: none -> 4.84 us  [body(): lax.ppermute(jnp.concatenate([paired, forward], axis=0), 'seq', swap_pairs)]
    all_to_all x1, waiting for transfers between devices: 6.86 us -> 9.72 us  [body(): pieces = lax.all_to_all(partial_sum, 'tp', 0, 0, tiled=True)]
    all_to_all x1, blocking collectives: 31.9 us -> 30.6 us  [body(): lax.all_to_all(send_buf, 'seq', 0, 0, tiled=True)]
    dot_general x1, matrix products: 1.54 us -> 0.38 us  [body(): jnp.dot(normed, w_value, preferred_element_type=jnp.float32)]
    dot_general x1, matrix products: 0.38 us -> 1.53 us  [body(): jnp.dot(normed, w_key, preferred_element_type=jnp.float32)]
    ppermute x4 -> x2, waiting for transfers between devices: 8.27 us -> 8.52 us  [from_behind(): return lax.ppermute(shard, axis, pairs)]
  transfers between devices with their start and end apart: 7 -> 6, of which waited for: 6 -> 5; matrix products, arithmetic and copies ran while one was open for 4% -> 4% of each run, Pallas kernels for 0% -> 0%
where the time goes in v9:
time: 114 us
  blocking collectives  30.6 us (27%)
  waiting for transfers between devices  30.1 us (26%)
  starting transfers between devices  25.8 us (23%)
  Pallas kernels  9.11 us (8%)
  other arithmetic  8.16 us (7%)
  matrix products  5.01 us (4%)
  local copies, waits for them, and re-layouts  4.57 us (4%)
    all_to_all x1, blocking collectives, body(): lax.all_to_all(send_buf, 'seq', 0, 0, tiled=True)  30.6 us
    all_to_all x1, waiting for transfers between devices, body(): pieces = lax.all_to_all(partial_sum, 'tp', 0, 0, tiled=True)  9.72 us
    pallas_call x1, Pallas kernels, attention(): pl.pallas_call(functools.partial(attn_kernel, heads, rows, span), out_sha...  9.11 us
    ppermute x2, starting transfers between devices, from_behind(): return lax.ppermute(shard, axis, pairs)  8.53 us
    ppermute x2, waiting for transfers between devices, from_behind(): return lax.ppermute(shard, axis, pairs)  8.52 us
    all_to_all x1, waiting for transfers between devices, body(): lax.all_to_all(jnp.concatenate([tokens] * tp_size, axis=1), 'tp', 1, 1, t...  7.48 us
    all_to_all x1, starting transfers between devices, body(): lax.all_to_all(jnp.concatenate([tokens] * tp_size, axis=1), 'tp', 1, 1, t...  4.96 us
    ppermute x1, starting transfers between devices, body(): lax.ppermute(jnp.concatenate([paired, forward], axis=0), 'seq', swap_pairs)  4.84 us
  transfers between devices with their start and end apart: 6, of which 5 were waited for; matrix products, arithmetic and copies ran while one was open for 4% of the time, Pallas kernels for 0%

profile of v9, /device:TPU:1, one launch (start us, length us, event | category | flops | bytes accessed | tf_op | source)
XLA Modules:
  0.0 113.7 jit_solution(12291489756400620365)
XLA Ops:
  0.0 2.1 %pad_maximum_fusion.1 = bf16[256,1280]{0,1:T(8,128)(2,1)} fusion(bf16[256,320]{0,1:T(8,128)(2,1)} %param.16), kind=kLoop, calls=%fused_computation.14 | loop fusion | flops 2621440 | bytes 819200 | tf_op jit(solution)/shard_map/concatenate | solution.py:120
  2.2 5.0 %all-to-all-start = ((bf16[256,4,320]{0,2,1:T(8,128)(2,1)}), bf16[256,4,320]{0,2,1:T(8,128)(2,1)S(1)}, u32[]{:S(2)}, u32[]{:S(2)}) async-start(bf16[256,4,320]{0,2,1:T(8,128)(2,1)} %bitcast.1), calls=%async_computation | async-start | bytes 1310720 | tf_op jit(solution)/shard_map/all_to_all | solution.py:119
  7.3 7.5 %all-to-all-done = bf16[256,4,320]{0,2,1:T(8,128)(2,1)S(1)} async-done(((bf16[256,4,320]{0,2,1:T(8,128)(2,1)}), bf16[256,4,320]{0,2,1:T(8,128)(2,1)S(1)}, u32[]{:S(2)}, u32[]{:S(2)}) %all-to-all-start) | async-done | bytes 655392 | tf_op jit(solution)/shard_map/all_to_all | solution.py:119
  16.5 1.5 %convolution_convert_fusion.1 = bf16[256,320]{0,1:T(8,128)(2,1)S(1)} fusion(bf16[1280,320]{0,1:T(8,128)(2,1)} %param.19, bf16[256,1280]{0,1:T(8,128)(2,1)S(1)} %multiply_convert_fusion), kind=kOutput, calls=%fused_computation.8 | convolution fusion | flops 209797120 | bytes 1638400 | tf_op jit(solution)/shard_map/dot_general | solution.py:125
  18.2 0.9 pad_maximum_fusion.2.b0
  19.0 7.3 %collective-permute-start = (bf16[272,640]{1,0:T(8,128)(2,1)}, bf16[272,640]{1,0:T(8,128)(2,1)}, u32[]{:S(2)}, u32[]{:S(2)}) collective-permute-start(bf16[272,640]{1,0:T(8,128)(2,1)} %pad_maximum_fusion.2.b0), channel_id=1, source_target_pairs={{0,8},{4,12},{8,16},{12,20},{16,24},{20,28},{24,32},{28,36},{32,40... | collective-permute-start | bytes 1044488 | tf_op jit(solution)/shard_map/ppermute | solution.py:20
  26.3 1.3 %collective-permute-start.1 = (bf16[272,640]{1,0:T(8,128)(2,1)}, bf16[272,640]{1,0:T(8,128)(2,1)}, u32[]{:S(2)}, u32[]{:S(2)}) collective-permute-start(bf16[272,640]{1,0:T(8,128)(2,1)} %pad_maximum_fusion.2.b0), channel_id=1, source_target_pairs={{8,0},{12,4},{16,8},{20,12},{24,16},{28,20},{32,24},{36,28},{40,32... | collective-permute-start | bytes 1044488 | tf_op jit(solution)/shard_map/ppermute | solution.py:20
  27.6 4.0 %collective-permute-done.b1 = bf16[272,640]{1,0:T(8,128)(2,1)} collective-permute-done((bf16[272,640]{1,0:T(8,128)(2,1)}, bf16[272,640]{1,0:T(8,128)(2,1)}, u32[]{:S(2)}, u32[]{:S(2)}) %collective-permute-start) | collective-permute-done | bytes 348192 | tf_op jit(solution)/shard_map/ppermute | solution.py:20
  31.6 4.6 %collective-permute-done.1.b2 = bf16[272,640]{1,0:T(8,128)(2,1)} collective-permute-done((bf16[272,640]{1,0:T(8,128)(2,1)}, bf16[272,640]{1,0:T(8,128)(2,1)}, u32[]{:S(2)}, u32[]{:S(2)}) %collective-permute-start.1) | collective-permute-done | bytes 348192 | tf_op jit(solution)/shard_map/ppermute | solution.py:20
  36.1 1.0 broadcast_select_fusion
  37.1 1.0 pad_maximum_fusion
  38.1 4.8 %collective-permute-start.2 = (bf16[544,640]{1,0:T(8,128)(2,1)}, bf16[544,640]{1,0:T(8,128)(2,1)}, u32[]{:S(2)}, u32[]{:S(2)}) collective-permute-start(bf16[544,640]{1,0:T(8,128)(2,1)} %pad_maximum_fusion), channel_id=1, source_target_pairs={{0,4},{4,0},{8,12},{12,8},{16,20},{20,16},{24,28},{28,24},{32,36},... | collective-permute-start | bytes 2088968 | tf_op jit(solution)/shard_map/ppermute | solution.py:141
  43.0 1.5 %convolution_convert_fusion.2 = bf16[256,320]{0,1:T(8,128)(2,1)S(1)} fusion(bf16[1280,320]{0,1:T(8,128)(2,1)} %param.18, bf16[256,1280]{0,1:T(8,128)(2,1)S(1)} %multiply_convert_fusion), kind=kOutput, calls=%fused_computation.9 | convolution fusion | flops 209797120 | bytes 1638400 | tf_op jit(solution)/shard_map/dot_general | solution.py:124
  44.5 0.8 copy.52.q_ref
  45.3 9.1 %shard_map.118 = bf16[256,1280]{1,0:T(8,128)(2,1)} custom-call(bf16[256,320]{1,0:T(8,128)(2,1)} %copy.52.q_ref, bf16[320,1280]{1,0:T(8,128)(2,1)} %w_ref.1, bf16[272,640]{1,0:T(8,128)(2,1)} %pad_maximum_fusion.2.b0, bf16[272,640]{1,0:T(8,128)(2,1)} %collective-permute-done.b1, bf16[272,640]{1,0:T(8,128)(2,1)} %collective-permute-done.1.b2, ...), custom_call_target="tpu_custom_call" | custom-call | flops 671088640 | bytes 3379200 | tf_op jit(solution)/shard_map/pallas_call | solution.py:75
  54.5 4.2 %all-to-all-start.1 = ((bf16[4,64,1280]{2,1,0:T(8,128)(2,1)}), bf16[4,64,1280]{2,1,0:T(8,128)(2,1)}, u32[]{:S(2)}, u32[]{:S(2)}) async-start(bf16[4,64,1280]{2,1,0:T(8,128)(2,1)} %bitcast.23), calls=%async_computation.1 | async-start | bytes 1310720 | tf_op jit(solution)/shard_map/all_to_all | solution.py:145
  59.1 0.7 gather_fusion
  59.8 9.7 %all-to-all-done.1 = bf16[4,64,1280]{2,1,0:T(8,128)(2,1)} async-done(((bf16[4,64,1280]{2,1,0:T(8,128)(2,1)}), bf16[4,64,1280]{2,1,0:T(8,128)(2,1)}, u32[]{:S(2)}, u32[]{:S(2)}) %all-to-all-start.1) | async-done | bytes 655392 | tf_op jit(solution)/shard_map/all_to_all | solution.py:145
  69.6 1.2 %convert_reduce_fusion.1 = f32[64,1280]{1,0:T(8,128)S(1)} fusion(bf16[4,64,1280]{2,1,0:T(8,128)(2,1)} %all-to-all-done.1), kind=kLoop, calls=%fused_computation.5 | loop fusion | flops 573440 | bytes 983040 | tf_op jit(solution)/shard_map/reduce_sum | solution.py:146
  71.8 0.7 copy.53
  72.5 3.3 %all-to-all-start.2 = ((bf16[64,4,160]{2,0,1:T(8,128)(2,1)}), bf16[64,4,160]{2,0,1:T(8,128)(2,1)S(1)}, u32[]{:S(2)}, u32[]{:S(2)}) async-start(bf16[64,4,160]{2,0,1:T(8,128)(2,1)} %copy.53), calls=%async_computation.2 | async-start | bytes 262144 | tf_op jit(solution)/shard_map/all_to_all | solution.py:154
  76.2 4.4 %all-to-all-done.2 = bf16[64,4,160]{2,0,1:T(8,128)(2,1)S(1)} async-done(((bf16[64,4,160]{2,0,1:T(8,128)(2,1)}), bf16[64,4,160]{2,0,1:T(8,128)(2,1)S(1)}, u32[]{:S(2)}, u32[]{:S(2)}) %all-to-all-start.2) | async-done | bytes 81952 | tf_op jit(solution)/shard_map/all_to_all | solution.py:154
  81.5 30.6 %all_to_all.40 = bf16[128,2,240]{2,1,0:T(2,128)(2,1)S(1)} all-to-all(bf16[128,2,240]{2,1,0:T(2,128)(2,1)S(1)} %reshape.163), channel_id=1, replica_groups=mesh['seq'=128,'tp'=4] {'seq'}, dimensions={0} | all-to-all | bytes 245760 | tf_op jit(solution)/shard_map/all_to_all | solution.py:175
  112.9 0.8 convolution_convert_fusion.5
  (57 shorter events, 5.5 us)
Async XLA Ops:
  0.0 71.2 %copy-start = (bf16[1280,640]{1,0:T(8,128)(2,1)S(1)}, bf16[1280,640]{1,0:T(8,128)(2,1)}, u32[]{:S(2)}) copy-start(bf16[1280,640]{1,0:T(8,128)(2,1)} %param.25) | copy-start | bytes 4915204
  0.0 7.1 %copy-start.4 = (s32[64,4]{0,1:T(4,128)S(1)}, s32[64,4]{0,1:T(4,128)}, u32[]{:S(2)}) copy-start(s32[64,4]{0,1:T(4,128)} %param.26) | copy-start | bytes 3076
  0.0 7.2 %copy-start.5 = (s32[256]{0:T(256)S(1)}, s32[256]{0:T(256)}, u32[]{:S(2)}) copy-start(s32[256]{0:T(256)} %param.23) | copy-start | bytes 3076
  0.0 7.2 %copy-start.6 = (s32[256]{0:T(256)S(1)}, s32[256]{0:T(256)}, u32[]{:S(2)}) copy-start(s32[256]{0:T(256)} %param.22) | copy-start | bytes 3076
  2.2 13.0 %copy-start.2 = (f32[1280]{0:T(1024)S(1)}, f32[1280]{0:T(1024)}, u32[]{:S(2)}) copy-start(f32[1280]{0:T(1024)} %param.17) | copy-start | bytes 15364
  2.2 12.6 %all-to-all-start = ((bf16[256,4,320]{0,2,1:T(8,128)(2,1)}), bf16[256,4,320]{0,2,1:T(8,128)(2,1)S(1)}, u32[]{:S(2)}, u32[]{:S(2)}) async-start(bf16[256,4,320]{0,2,1:T(8,128)(2,1)} %bitcast.1), calls=%async_computation | async-start | bytes 1310720 | tf_op jit(solution)/shard_map/all_to_all | solution.py:119
  14.8 1.1 %copy-start.1 = (bf16[1280,320]{0,1:T(8,128)(2,1)S(1)}, bf16[1280,320]{0,1:T(8,128)(2,1)}, u32[]{:S(2)}) copy-start(bf16[1280,320]{0,1:T(8,128)(2,1)} %param.20) | copy-start | bytes 2457604
  19.0 23.9 %copy-start.7 = (s32[64]{0:T(128)S(1)}, s32[64]{0:T(128)}, u32[]{:S(2)}) copy-start(s32[64]{0:T(128)} %param.27) | copy-start | bytes 772
  19.0 12.5 %collective-permute-start = (bf16[272,640]{1,0:T(8,128)(2,1)}, bf16[272,640]{1,0:T(8,128)(2,1)}, u32[]{:S(2)}, u32[]{:S(2)}) collective-permute-start(bf16[272,640]{1,0:T(8,128)(2,1)} %pad_maximum_fusion.2.b0), channel_id=1, source_target_pairs={{0,8},{4,12},{8,16},{12,20},{16,24},{20,28},{24,32},{28,36},{32,40... | collective-permute-start | bytes 1044488 | tf_op jit(solution)/shard_map/ppermute | solution.py:20
  26.3 9.8 %collective-permute-start.1 = (bf16[272,640]{1,0:T(8,128)(2,1)}, bf16[272,640]{1,0:T(8,128)(2,1)}, u32[]{:S(2)}, u32[]{:S(2)}) collective-permute-start(bf16[272,640]{1,0:T(8,128)(2,1)} %pad_maximum_fusion.2.b0), channel_id=1, source_target_pairs={{8,0},{12,4},{16,8},{20,12},{24,16},{28,20},{32,24},{36,28},{40,32... | collective-permute-start | bytes 1044488 | tf_op jit(solution)/shard_map/ppermute | solution.py:20
  38.1 7.2 %collective-permute-start.2 = (bf16[544,640]{1,0:T(8,128)(2,1)}, bf16[544,640]{1,0:T(8,128)(2,1)}, u32[]{:S(2)}, u32[]{:S(2)}) collective-permute-start(bf16[544,640]{1,0:T(8,128)(2,1)} %pad_maximum_fusion), channel_id=1, source_target_pairs={{0,4},{4,0},{8,12},{12,8},{16,20},{20,16},{24,28},{28,24},{32,36},... | collective-permute-start | bytes 2088968 | tf_op jit(solution)/shard_map/ppermute | solution.py:141
  54.5 15.1 %all-to-all-start.1 = ((bf16[4,64,1280]{2,1,0:T(8,128)(2,1)}), bf16[4,64,1280]{2,1,0:T(8,128)(2,1)}, u32[]{:S(2)}, u32[]{:S(2)}) async-start(bf16[4,64,1280]{2,1,0:T(8,128)(2,1)} %bitcast.23), calls=%async_computation.1 | async-start | bytes 1310720 | tf_op jit(solution)/shard_map/all_to_all | solution.py:145
  59.8 11.4 %copy-start.3 = (f32[1280]{0:T(1024)S(1)}, f32[1280]{0:T(1024)}, u32[]{:S(2)}) copy-start(f32[1280]{0:T(1024)} %param.24) | copy-start | bytes 15364
  72.5 8.1 %all-to-all-start.2 = ((bf16[64,4,160]{2,0,1:T(8,128)(2,1)}), bf16[64,4,160]{2,0,1:T(8,128)(2,1)S(1)}, u32[]{:S(2)}, u32[]{:S(2)}) async-start(bf16[64,4,160]{2,0,1:T(8,128)(2,1)} %copy.53), calls=%async_computation.2 | async-start | bytes 262144 | tf_op jit(solution)/shard_map/all_to_all | solution.py:154

commit v10 on v8

--- a/solution.py
+++ b/solution.py
@@ -115,9 +115,7 @@
     position = lax.axis_index("tp")
     seq_index = lax.axis_index("seq")
 
-    gathered = lax.all_to_all(
-        jnp.concatenate([tokens] * tp_size, axis=1), "tp", 1, 1, tiled=True
-    )
+    gathered = lax.all_gather(tokens, "tp", axis=1, tiled=True)
 
     normed = layer_norm(gathered, first_gain).astype(jnp.bfloat16)
     queries = jnp.dot(normed, w_query, preferred_element_type=jnp.float32).astype(jnp.bfloat16)

time: 114 us -> 109 us (0.956)
  blocking collectives: 31.9 us -> 42.7 us
  waiting for transfers between devices: 27 us -> 18.2 us
  other arithmetic: 6.34 us -> 3.42 us
  starting transfers between devices: 28.5 us -> 25.6 us
    all_gather x0 -> x1, blocking collectives: none -> 11.7 us  [body(): gathered = lax.all_gather(tokens, 'tp', axis=1, tiled=True)]
    all_to_all x1 -> x0, waiting for transfers between devices: 7.48 us -> none  [body(): lax.all_to_all(jnp.concatenate([tokens] * tp_size, axis=1), 'tp', 1, 1, t...]
    all_to_all x1 -> x0, starting transfers between devices: 4.96 us -> none  [body(): lax.all_to_all(jnp.concatenate([tokens] * tp_size, axis=1), 'tp', 1, 1, t...]
    ppermute x4, waiting for transfers between devices: 8.27 us -> 5.23 us  [from_behind(): return lax.ppermute(shard, axis, pairs)]
    ppermute x4, starting transfers between devices: 16 us -> 18.7 us  [from_behind(): return lax.ppermute(shard, axis, pairs)]
    concatenate x1 -> x0, other arithmetic: 2.15 us -> none  [body(): jnp.concatenate([tokens] * tp_size, axis=1)]
    all_to_all x1, waiting for transfers between devices: 6.86 us -> 8.59 us  [body(): pieces = lax.all_to_all(partial_sum, 'tp', 0, 0, tiled=True)]
  transfers between devices with their start and end apart: 7 -> 6, of which waited for: 6 -> 4; matrix products, arithmetic and copies ran while one was open for 4% -> 4% of each run, Pallas kernels for 0% -> 0%
where the time goes in v10:
time: 109 us
  blocking collectives  42.7 us (39%)
  starting transfers between devices  25.6 us (23%)
  waiting for transfers between devices  18.2 us (17%)
  Pallas kernels  9.05 us (8%)
  matrix products  5.35 us (5%)
  local copies, waits for them, and re-layouts  4.12 us (4%)
  other arithmetic  3.42 us (3%)
    all_to_all x1, blocking collectives, body(): lax.all_to_all(send_buf, 'seq', 0, 0, tiled=True)  31.1 us
    ppermute x4, starting transfers between devices, from_behind(): return lax.ppermute(shard, axis, pairs)  18.7 us
    all_gather x1, blocking collectives, body(): gathered = lax.all_gather(tokens, 'tp', axis=1, tiled=True)  11.7 us
    pallas_call x1, Pallas kernels, attention(): pl.pallas_call(functools.partial(attn_kernel, heads, rows), out_shape=jax...  9.05 us
    all_to_all x1, waiting for transfers between devices, body(): pieces = lax.all_to_all(partial_sum, 'tp', 0, 0, tiled=True)  8.59 us
    ppermute x4, waiting for transfers between devices, from_behind(): return lax.ppermute(shard, axis, pairs)  5.23 us
    all_to_all x1, waiting for transfers between devices, body(): proj_pieces = lax.all_to_all(partial_proj, 'tp', 1, 0, tiled=True)  4.42 us
    all_to_all x1, starting transfers between devices, body(): pieces = lax.all_to_all(partial_sum, 'tp', 0, 0, tiled=True)  3.61 us
  transfers between devices with their start and end apart: 6, of which 4 were waited for; matrix products, arithmetic and copies ran while one was open for 4% of the time, Pallas kernels for 0%

profile of v10, /device:TPU:1, one launch (start us, length us, event | category | flops | bytes accessed | tf_op | source)
XLA Modules:
  0.0 108.8 jit_solution(11425091850907478022)
XLA Ops:
  0.0 0.8 fusion.26
  0.9 0.7 convert_bitcast_fusion
  1.6 11.7 %all_gather.3 = bf16[256,1280]{0,1:T(8,128)(2,1)S(1)} all-gather(bf16[256,320]{0,1:T(8,128)(2,1)} %param.16), channel_id=1, replica_groups=mesh['seq'=128,'tp'=4] {'tp'}, dimensions={1}, use_global_device_ids=true | all-gather | bytes 819200 | tf_op jit(solution)/shard_map/all_gather | solution.py:118
  13.7 0.5 convolution_convert_fusion.1
  14.4 1.6 %convolution_convert_fusion = bf16[256,320]{0,1:T(8,128)(2,1)S(1)} fusion(bf16[1280,320]{0,1:T(8,128)(2,1)} %param.20, bf16[256,1280]{0,1:T(8,128)(2,1)S(1)} %all_gather.3, f32[1280]{0:T(1024)S(1)} %copy-done.4, f32[256]{0:T(256)S(1)} %add_rsqrt_fusion, f32[256]{0:T(256)S(1)} %broadcast_multiply_fusion), kind=kOutput, calls=%fused_computation.9 | convolution fusion | flops 211435520 | bytes 1645568 | tf_op jit(solution)/shard_map/dot_general | solution.py:123
  16.4 1.3 %collective-permute-start.3 = (bf16[264,640]{1,0:T(8,128)(2,1)S(1)}, bf16[264,640]{1,0:T(8,128)(2,1)}, u32[]{:S(2)}, u32[]{:S(2)}) collective-permute-start(bf16[264,640]{1,0:T(8,128)(2,1)S(1)} %pad_maximum_fusion.b0), channel_id=1, source_target_pairs={{8,0},{12,4},{16,8},{20,12},{24,16},{28,20},{32,24},{36,28},{40,32... | collective-permute-start | bytes 1013768 | tf_op jit(solution)/shard_map/ppermute | solution.py:20
  17.7 10.5 %collective-permute-start.2 = (bf16[264,640]{1,0:T(8,128)(2,1)S(1)}, bf16[264,640]{1,0:T(8,128)(2,1)}, u32[]{:S(2)}, u32[]{:S(2)}) collective-permute-start(bf16[264,640]{1,0:T(8,128)(2,1)S(1)} %pad_maximum_fusion.b0), channel_id=1, source_target_pairs={{4,0},{8,4},{12,8},{16,12},{20,16},{24,20},{28,24},{32,28},{36,32}... | collective-permute-start | bytes 1013768 | tf_op jit(solution)/shard_map/ppermute | solution.py:20
  28.2 5.0 %collective-permute-start.1 = (bf16[264,640]{1,0:T(8,128)(2,1)S(1)}, bf16[264,640]{1,0:T(8,128)(2,1)}, u32[]{:S(2)}, u32[]{:S(2)}) collective-permute-start(bf16[264,640]{1,0:T(8,128)(2,1)S(1)} %pad_maximum_fusion.b0), channel_id=1, source_target_pairs={{0,8},{4,12},{8,16},{12,20},{16,24},{20,28},{24,32},{28,36},{32,40... | collective-permute-start | bytes 1013768 | tf_op jit(solution)/shard_map/ppermute | solution.py:20
  33.2 1.9 %collective-permute-start = (bf16[264,640]{1,0:T(8,128)(2,1)S(1)}, bf16[264,640]{1,0:T(8,128)(2,1)}, u32[]{:S(2)}, u32[]{:S(2)}) collective-permute-start(bf16[264,640]{1,0:T(8,128)(2,1)S(1)} %pad_maximum_fusion.b0), channel_id=1, source_target_pairs={{0,4},{4,8},{8,12},{12,16},{16,20},{20,24},{24,28},{28,32},{32,36}... | collective-permute-start | bytes 1013768 | tf_op jit(solution)/shard_map/ppermute | solution.py:20
  35.1 1.6 %convolution_convert_fusion.2 = bf16[256,320]{0,1:T(8,128)(2,1)S(1)} fusion(bf16[1280,320]{0,1:T(8,128)(2,1)} %param.18, bf16[256,1280]{0,1:T(8,128)(2,1)S(1)} %all_gather.3, f32[1280]{0:T(1024)S(1)} %copy-done.4, f32[256]{0:T(256)S(1)} %add_rsqrt_fusion, f32[256]{0:T(256)S(1)} %broadcast_multiply_fusion), kind=kOutput, calls=%fused_computation.11 | convolution fusion | flops 211435520 | bytes 1645568 | tf_op jit(solution)/shard_map/dot_general | solution.py:121
  37.0 0.8 copy.52.q_ref
  37.8 0.7 gather_fusion
  38.6 1.1 %collective-permute-done.1.b2 = bf16[264,640]{1,0:T(8,128)(2,1)} collective-permute-done((bf16[264,640]{1,0:T(8,128)(2,1)S(1)}, bf16[264,640]{1,0:T(8,128)(2,1)}, u32[]{:S(2)}, u32[]{:S(2)}) %collective-permute-start.1) | collective-permute-done | bytes 337952 | tf_op jit(solution)/shard_map/ppermute | solution.py:20
  39.7 4.1 %collective-permute-done.b1 = bf16[264,640]{1,0:T(8,128)(2,1)} collective-permute-done((bf16[264,640]{1,0:T(8,128)(2,1)S(1)}, bf16[264,640]{1,0:T(8,128)(2,1)}, u32[]{:S(2)}, u32[]{:S(2)}) %collective-permute-start) | collective-permute-done | bytes 337952 | tf_op jit(solution)/shard_map/ppermute | solution.py:20
  43.8 9.0 %shard_map.118 = bf16[256,1280]{1,0:T(8,128)(2,1)} custom-call(bf16[256,320]{1,0:T(8,128)(2,1)} %copy.52.q_ref, bf16[320,1280]{1,0:T(8,128)(2,1)} %w_ref.1, bf16[264,640]{1,0:T(8,128)(2,1)} %copy-done.1, bf16[264,640]{1,0:T(8,128)(2,1)} %collective-permute-done.b1, bf16[264,640]{1,0:T(8,128)(2,1)} %collective-permute-done.1.b2, ...), custom_call_target="tpu_custom_call" | custom-call | flops 671088640 | bytes 3328000 | tf_op jit(solution)/shard_map/pallas_call | solution.py:74
  52.8 3.6 %all-to-all-start = ((bf16[4,64,1280]{2,1,0:T(8,128)(2,1)}), bf16[4,64,1280]{2,1,0:T(8,128)(2,1)S(1)}, u32[]{:S(2)}, u32[]{:S(2)}) async-start(bf16[4,64,1280]{2,1,0:T(8,128)(2,1)} %bitcast.16), calls=%async_computation | async-start | bytes 1310720 | tf_op jit(solution)/shard_map/all_to_all | solution.py:138
  56.7 8.6 %all-to-all-done = bf16[4,64,1280]{2,1,0:T(8,128)(2,1)S(1)} async-done(((bf16[4,64,1280]{2,1,0:T(8,128)(2,1)}), bf16[4,64,1280]{2,1,0:T(8,128)(2,1)S(1)}, u32[]{:S(2)}, u32[]{:S(2)}) %all-to-all-start) | async-done | bytes 655392 | tf_op jit(solution)/shard_map/all_to_all | solution.py:138
  65.9 0.5 convolution_convert_fusion.4
  66.5 0.7 copy.53
  67.1 3.3 %all-to-all-start.1 = ((bf16[64,4,160]{2,0,1:T(8,128)(2,1)}), bf16[64,4,160]{2,0,1:T(8,128)(2,1)S(1)}, u32[]{:S(2)}, u32[]{:S(2)}) async-start(bf16[64,4,160]{2,0,1:T(8,128)(2,1)} %copy.53), calls=%async_computation.1 | async-start | bytes 262144 | tf_op jit(solution)/shard_map/all_to_all | solution.py:147
  70.8 4.4 %all-to-all-done.1 = bf16[64,4,160]{2,0,1:T(8,128)(2,1)S(1)} async-done(((bf16[64,4,160]{2,0,1:T(8,128)(2,1)}), bf16[64,4,160]{2,0,1:T(8,128)(2,1)S(1)}, u32[]{:S(2)}, u32[]{:S(2)}) %all-to-all-start.1) | async-done | bytes 81952 | tf_op jit(solution)/shard_map/all_to_all | solution.py:147
  76.1 31.1 %all_to_all.28 = bf16[128,2,240]{2,1,0:T(2,128)(2,1)S(1)} all-to-all(bf16[128,2,240]{2,1,0:T(2,128)(2,1)S(1)} %reshape.156), channel_id=1, replica_groups=mesh['seq'=128,'tp'=4] {'seq'}, dimensions={0} | all-to-all | bytes 245760 | tf_op jit(solution)/shard_map/all_to_all | solution.py:168
  107.4 0.3 fusion.12
  108.0 0.8 convolution_convert_fusion.5
  (50 shorter events, 3.9 us)
Async XLA Ops:
  0.0 65.8 %copy-start = (bf16[1280,640]{1,0:T(8,128)(2,1)S(1)}, bf16[1280,640]{1,0:T(8,128)(2,1)}, u32[]{:S(2)}) copy-start(bf16[1280,640]{1,0:T(8,128)(2,1)} %param.25) | copy-start | bytes 4915204
  0.0 13.7 %copy-start.4 = (f32[1280]{0:T(1024)S(1)}, f32[1280]{0:T(1024)}, u32[]{:S(2)}) copy-start(f32[1280]{0:T(1024)} %param.17) | copy-start | bytes 15364
  1.6 12.1 %copy-start.3 = (bf16[1280,320]{0,1:T(8,128)(2,1)S(1)}, bf16[1280,320]{0,1:T(8,128)(2,1)}, u32[]{:S(2)}) copy-start(bf16[1280,320]{0,1:T(8,128)(2,1)} %param.19) | copy-start | bytes 2457604
  16.4 20.6 %copy-start.1 = (bf16[264,640]{1,0:T(8,128)(2,1)}, bf16[264,640]{1,0:T(8,128)(2,1)S(1)}, u32[]{:S(2)}) copy-start(bf16[264,640]{1,0:T(8,128)(2,1)S(1)} %pad_maximum_fusion.b0) | copy-start | bytes 1013764
  16.4 22.2 %collective-permute-start.3 = (bf16[264,640]{1,0:T(8,128)(2,1)S(1)}, bf16[264,640]{1,0:T(8,128)(2,1)}, u32[]{:S(2)}, u32[]{:S(2)}) collective-permute-start(bf16[264,640]{1,0:T(8,128)(2,1)S(1)} %pad_maximum_fusion.b0), channel_id=1, source_target_pairs={{8,0},{12,4},{16,8},{20,12},{24,16},{28,20},{32,24},{36,28},{40,32... | collective-permute-start | bytes 1013768 | tf_op jit(solution)/shard_map/ppermute | solution.py:20
  17.7 20.9 %collective-permute-start.2 = (bf16[264,640]{1,0:T(8,128)(2,1)S(1)}, bf16[264,640]{1,0:T(8,128)(2,1)}, u32[]{:S(2)}, u32[]{:S(2)}) collective-permute-start(bf16[264,640]{1,0:T(8,128)(2,1)S(1)} %pad_maximum_fusion.b0), channel_id=1, source_target_pairs={{4,0},{8,4},{12,8},{16,12},{20,16},{24,20},{28,24},{32,28},{36,32}... | collective-permute-start | bytes 1013768 | tf_op jit(solution)/shard_map/ppermute | solution.py:20
  28.2 11.5 %collective-permute-start.1 = (bf16[264,640]{1,0:T(8,128)(2,1)S(1)}, bf16[264,640]{1,0:T(8,128)(2,1)}, u32[]{:S(2)}, u32[]{:S(2)}) collective-permute-start(bf16[264,640]{1,0:T(8,128)(2,1)S(1)} %pad_maximum_fusion.b0), channel_id=1, source_target_pairs={{0,8},{4,12},{8,16},{12,20},{16,24},{20,28},{24,32},{28,36},{32,40... | collective-permute-start | bytes 1013768 | tf_op jit(solution)/shard_map/ppermute | solution.py:20
  33.2 10.6 %collective-permute-start = (bf16[264,640]{1,0:T(8,128)(2,1)S(1)}, bf16[264,640]{1,0:T(8,128)(2,1)}, u32[]{:S(2)}, u32[]{:S(2)}) collective-permute-start(bf16[264,640]{1,0:T(8,128)(2,1)S(1)} %pad_maximum_fusion.b0), channel_id=1, source_target_pairs={{0,4},{4,8},{8,12},{12,16},{16,20},{20,24},{24,28},{28,32},{32,36}... | collective-permute-start | bytes 1013768 | tf_op jit(solution)/shard_map/ppermute | solution.py:20
  52.8 3.6 %copy-start.5 = (s32[64]{0:T(128)S(1)}, s32[64]{0:T(128)}, u32[]{:S(2)}) copy-start(s32[64]{0:T(128)} %param.27) | copy-start | bytes 772
  52.8 12.4 %all-to-all-start = ((bf16[4,64,1280]{2,1,0:T(8,128)(2,1)}), bf16[4,64,1280]{2,1,0:T(8,128)(2,1)S(1)}, u32[]{:S(2)}, u32[]{:S(2)}) async-start(bf16[4,64,1280]{2,1,0:T(8,128)(2,1)} %bitcast.16), calls=%async_computation | async-start | bytes 1310720 | tf_op jit(solution)/shard_map/all_to_all | solution.py:138
  56.5 9.4 %copy-start.2 = (f32[1280]{0:T(1024)S(1)}, f32[1280]{0:T(1024)}, u32[]{:S(2)}) copy-start(f32[1280]{0:T(1024)} %param.24) | copy-start | bytes 15364
  67.1 8.1 %all-to-all-start.1 = ((bf16[64,4,160]{2,0,1:T(8,128)(2,1)}), bf16[64,4,160]{2,0,1:T(8,128)(2,1)S(1)}, u32[]{:S(2)}, u32[]{:S(2)}) async-start(bf16[64,4,160]{2,0,1:T(8,128)(2,1)} %copy.53), calls=%async_computation.1 | async-start | bytes 262144 | tf_op jit(solution)/shard_map/all_to_all | solution.py:147

commit v11 on v10

--- a/solution.py
+++ b/solution.py
@@ -20,46 +20,57 @@
     return lax.ppermute(shard, axis, pairs)
 
 
-def attn_kernel(heads, rows, q_ref, w_ref, b0, b1, b2, b3, b4, out_ref, att_ref):
-    blocks = (b0, b1, b2, b3, b4)
+def attn_kernel(heads, rows, q_hbm, w_hbm, b0, b1, b2, b3, b4, out_ref,
+                q_ref, w_ref, blk_ref, score_ref, att_ref, sems):
+    sources = (b0, b1, b2, b3, b4)
+    nblk = len(sources)
     scale = HD ** (-0.5)
     width = heads * HD
-    side = jnp.transpose(b0[rows:rows + 8, 0:rows].astype(jnp.float32))
+    copies = [pltpu.make_async_copy(sources[0], blk_ref.at[0], sems.at[0]),
+              pltpu.make_async_copy(q_hbm, q_ref, sems.at[nblk])]
+    copies += [pltpu.make_async_copy(sources[b], blk_ref.at[b], sems.at[b]) for b in range(1, nblk)]
+    copies.append(pltpu.make_async_copy(w_hbm, w_ref, sems.at[nblk + 1]))
+    for c in copies:
+        c.start()
+    copies[0].wait()
+    copies[1].wait()
+    side = jnp.transpose(blk_ref[0, rows:rows + 8, 0:rows].astype(jnp.float32))
     qcode = side[:, 1:2]
     order = side[:, 2:3]
     row_id = lax.broadcasted_iota(jnp.int32, (rows, rows), 0)
     col_id = lax.broadcasted_iota(jnp.int32, (rows, rows), 1)
     diag = row_id == col_id
-    masks = []
-    for b, blk in enumerate(blocks):
-        kcode = blk[rows:rows + 1, 0:rows].astype(jnp.float32)
-        m = qcode == kcode
+    row_max = [None] * heads
+    for b in range(nblk):
+        if b >= 1:
+            copies[b + 1].wait()
+        kcode = blk_ref[b, rows:rows + 1, 0:rows].astype(jnp.float32)
+        mask = qcode == kcode
         if b == 0:
-            m = m | diag
-        masks.append(m)
+            mask = mask | diag
+        for h in range(heads):
+            q = q_ref[:, h * HD:(h + 1) * HD]
+            k = blk_ref[b, 0:rows, h * HD:(h + 1) * HD]
+            s = lax.dot_general(q, k, (((1,), (1,)), ((), ())), preferred_element_type=jnp.float32) * scale
+            s = jnp.where(mask, s, -1e30)
+            score_ref[h * nblk + b] = s
+            m = s.max(axis=1, keepdims=True)
+            row_max[h] = m if row_max[h] is None else jnp.maximum(row_max[h], m)
     for h in range(heads):
-        q = q_ref[:, h * HD:(h + 1) * HD]
-        scores = []
-        for b, blk in enumerate(blocks):
-            k = blk[0:rows, h * HD:(h + 1) * HD]
-            s = lax.dot_general(q, k, (((1,), (1,)), ((), ())), preferred_element_type=jnp.float32) * scale
-            scores.append(jnp.where(masks[b], s, -1e30))
-        row_max = scores[0].max(axis=1, keepdims=True)
-        for s in scores[1:]:
-            row_max = jnp.maximum(row_max, s.max(axis=1, keepdims=True))
-        exps = [jnp.exp(s - row_max) for s in scores]
+        exps = [jnp.exp(score_ref[h * nblk + b] - row_max[h]) for b in range(nblk)]
         total = exps[0].sum(axis=1, keepdims=True)
         for e in exps[1:]:
             total = total + e.sum(axis=1, keepdims=True)
         acc = None
-        for b, blk in enumerate(blocks):
+        for b in range(nblk):
             w = (exps[b] / total).astype(jnp.bfloat16)
-            v = blk[0:rows, width + h * HD:width + (h + 1) * HD]
+            v = blk_ref[b, 0:rows, width + h * HD:width + (h + 1) * HD]
             p = jnp.dot(w, v, preferred_element_type=jnp.float32)
             acc = p if acc is None else acc + p
         att_ref[:, h * HD:(h + 1) * HD] = acc.astype(jnp.bfloat16)
     pick = (order == col_id.astype(jnp.float32)).astype(jnp.bfloat16)
     ordered = jnp.dot(pick, att_ref[...], preferred_element_type=jnp.float32)
+    copies[-1].wait()
     mixed = jnp.dot(ordered.astype(jnp.bfloat16), w_ref[...], preferred_element_type=jnp.float32)
     out_ref[...] = mixed.astype(out_ref.dtype)
 
@@ -68,18 +79,26 @@
     rows, width = q.shape
     heads = width // HD
     out_width = w_out.shape[1]
-    vmem = pl.BlockSpec(memory_space=pltpu.VMEM)
-    flops = 2 * 2 * heads * rows * rows * len(blocks) * HD
+    nblk = len(blocks)
+    anywhere = pl.BlockSpec(memory_space=pl.ANY)
+    flops = 2 * 2 * heads * rows * rows * nblk * HD
     flops += 2 * rows * rows * width + 2 * rows * width * out_width
     return pl.pallas_call(
         functools.partial(attn_kernel, heads, rows),
         out_shape=jax.ShapeDtypeStruct((rows, out_width), jnp.bfloat16),
-        in_specs=[vmem] * (2 + len(blocks)),
-        out_specs=vmem,
-        scratch_shapes=[pltpu.VMEM((rows, width), jnp.bfloat16)],
+        in_specs=[anywhere] * (2 + nblk),
+        out_specs=pl.BlockSpec(memory_space=pltpu.VMEM),
+        scratch_shapes=[
+            pltpu.VMEM(q.shape, jnp.bfloat16),
+            pltpu.VMEM(w_out.shape, jnp.bfloat16),
+            pltpu.VMEM((nblk,) + blocks[0].shape, jnp.bfloat16),
+            pltpu.VMEM((heads * nblk, rows, rows), jnp.float32),
+            pltpu.VMEM((rows, width), jnp.bfloat16),
+            pltpu.SemaphoreType.DMA((nblk + 2,)),
+        ],
         cost_estimate=pl.CostEstimate(
             flops=flops,
-            transcendentals=heads * rows * rows * len(blocks),
+            transcendentals=heads * rows * rows * nblk,
             bytes_accessed=sum(b.size * 2 for b in blocks) + q.size * 2 + w_out.size * 2 + rows * out_width * 2,
         ),
     )(q, w_out, *blocks)

time: 109 us -> 109 us (level)
  no operation moved by 1% of the time
where the time goes in v11:
time: 109 us; the launch traced here: 108 us
  blocking collectives  42.7 us (39%)
  starting transfers between devices  25.5 us (23%)
  waiting for transfers between devices  18.2 us (17%)
  Pallas kernels  8.42 us (8%)
  matrix products  5.35 us (5%)
  local copies, waits for them, and re-layouts  4.12 us (4%)
  other arithmetic  3.42 us (3%)
    all_to_all x1, blocking collectives, body(): lax.all_to_all(send_buf, 'seq', 0, 0, tiled=True)  31 us
    ppermute x4, starting transfers between devices, from_behind(): return lax.ppermute(shard, axis, pairs)  18.7 us
    all_gather x1, blocking collectives, body(): gathered = lax.all_gather(tokens, 'tp', axis=1, tiled=True)  11.7 us
    all_to_all x1, waiting for transfers between devices, body(): pieces = lax.all_to_all(partial_sum, 'tp', 0, 0, tiled=True)  8.59 us
    pallas_call x1, Pallas kernels, attention(): pl.pallas_call(functools.partial(attn_kernel, heads, rows), out_shape=jax...  8.42 us
    ppermute x4, waiting for transfers between devices, from_behind(): return lax.ppermute(shard, axis, pairs)  5.23 us
    all_to_all x1, waiting for transfers between devices, body(): proj_pieces = lax.all_to_all(partial_proj, 'tp', 1, 0, tiled=True)  4.42 us
    all_to_all x1, starting transfers between devices, body(): pieces = lax.all_to_all(partial_sum, 'tp', 0, 0, tiled=True)  3.49 us
  transfers between devices with their start and end apart: 6, of which 4 were waited for; matrix products, arithmetic and copies ran while one was open for 4% of the time, Pallas kernels for 0%

profile of v11, /device:TPU:1, one launch (start us, length us, event | category | flops | bytes accessed | tf_op | source)
XLA Modules:
  0.0 108.1 jit_solution(305313676282736054)
XLA Ops:
  0.0 0.8 fusion.26
  0.9 0.7 convert_bitcast_fusion
  1.6 11.7 %all_gather.3 = bf16[256,1280]{0,1:T(8,128)(2,1)S(1)} all-gather(bf16[256,320]{0,1:T(8,128)(2,1)} %param.16), channel_id=1, replica_groups=mesh['seq'=128,'tp'=4] {'tp'}, dimensions={1}, use_global_device_ids=true | all-gather | bytes 819200 | tf_op jit(solution)/shard_map/all_gather | solution.py:137
  13.7 0.5 convolution_convert_fusion.1
  14.4 1.6 %convolution_convert_fusion = bf16[256,320]{0,1:T(8,128)(2,1)S(1)} fusion(bf16[1280,320]{0,1:T(8,128)(2,1)} %param.20, bf16[256,1280]{0,1:T(8,128)(2,1)S(1)} %all_gather.3, f32[1280]{0:T(1024)S(1)} %copy-done.4, f32[256]{0:T(256)S(1)} %add_rsqrt_fusion, f32[256]{0:T(256)S(1)} %broadcast_multiply_fusion), kind=kOutput, calls=%fused_computation.9 | convolution fusion | flops 211435520 | bytes 1645568 | tf_op jit(solution)/shard_map/dot_general | solution.py:142
  16.4 1.3 %collective-permute-start.3 = (bf16[264,640]{1,0:T(8,128)(2,1)S(1)}, bf16[264,640]{1,0:T(8,128)(2,1)}, u32[]{:S(2)}, u32[]{:S(2)}) collective-permute-start(bf16[264,640]{1,0:T(8,128)(2,1)S(1)} %pad_maximum_fusion.b0), channel_id=1, source_target_pairs={{8,0},{12,4},{16,8},{20,12},{24,16},{28,20},{32,24},{36,28},{40,32... | collective-permute-start | bytes 1013768 | tf_op jit(solution)/shard_map/ppermute | solution.py:20
  17.7 10.5 %collective-permute-start.2 = (bf16[264,640]{1,0:T(8,128)(2,1)S(1)}, bf16[264,640]{1,0:T(8,128)(2,1)}, u32[]{:S(2)}, u32[]{:S(2)}) collective-permute-start(bf16[264,640]{1,0:T(8,128)(2,1)S(1)} %pad_maximum_fusion.b0), channel_id=1, source_target_pairs={{4,0},{8,4},{12,8},{16,12},{20,16},{24,20},{28,24},{32,28},{36,32}... | collective-permute-start | bytes 1013768 | tf_op jit(solution)/shard_map/ppermute | solution.py:20
  28.2 5.0 %collective-permute-start.1 = (bf16[264,640]{1,0:T(8,128)(2,1)S(1)}, bf16[264,640]{1,0:T(8,128)(2,1)}, u32[]{:S(2)}, u32[]{:S(2)}) collective-permute-start(bf16[264,640]{1,0:T(8,128)(2,1)S(1)} %pad_maximum_fusion.b0), channel_id=1, source_target_pairs={{0,8},{4,12},{8,16},{12,20},{16,24},{20,28},{24,32},{28,36},{32,40... | collective-permute-start | bytes 1013768 | tf_op jit(solution)/shard_map/ppermute | solution.py:20
  33.2 1.9 %collective-permute-start = (bf16[264,640]{1,0:T(8,128)(2,1)S(1)}, bf16[264,640]{1,0:T(8,128)(2,1)}, u32[]{:S(2)}, u32[]{:S(2)}) collective-permute-start(bf16[264,640]{1,0:T(8,128)(2,1)S(1)} %pad_maximum_fusion.b0), channel_id=1, source_target_pairs={{0,4},{4,8},{8,12},{12,16},{16,20},{20,24},{24,28},{28,32},{32,36}... | collective-permute-start | bytes 1013768 | tf_op jit(solution)/shard_map/ppermute | solution.py:20
  35.1 1.6 %convolution_convert_fusion.2 = bf16[256,320]{0,1:T(8,128)(2,1)S(1)} fusion(bf16[1280,320]{0,1:T(8,128)(2,1)} %param.18, bf16[256,1280]{0,1:T(8,128)(2,1)S(1)} %all_gather.3, f32[1280]{0:T(1024)S(1)} %copy-done.4, f32[256]{0:T(256)S(1)} %add_rsqrt_fusion, f32[256]{0:T(256)S(1)} %broadcast_multiply_fusion), kind=kOutput, calls=%fused_computation.11 | convolution fusion | flops 211435520 | bytes 1645568 | tf_op jit(solution)/shard_map/dot_general | solution.py:140
  37.0 0.8 copy.52.q_hbm
  37.8 0.7 gather_fusion
  38.6 1.1 %collective-permute-done.1.b2 = bf16[264,640]{1,0:T(8,128)(2,1)} collective-permute-done((bf16[264,640]{1,0:T(8,128)(2,1)S(1)}, bf16[264,640]{1,0:T(8,128)(2,1)}, u32[]{:S(2)}, u32[]{:S(2)}) %collective-permute-start.1) | collective-permute-done | bytes 337952 | tf_op jit(solution)/shard_map/ppermute | solution.py:20
  39.7 4.1 %collective-permute-done.b1 = bf16[264,640]{1,0:T(8,128)(2,1)} collective-permute-done((bf16[264,640]{1,0:T(8,128)(2,1)S(1)}, bf16[264,640]{1,0:T(8,128)(2,1)}, u32[]{:S(2)}, u32[]{:S(2)}) %collective-permute-start) | collective-permute-done | bytes 337952 | tf_op jit(solution)/shard_map/ppermute | solution.py:20
  43.8 8.4 %shard_map.118 = bf16[256,1280]{1,0:T(8,128)(2,1)} custom-call(bf16[256,320]{1,0:T(8,128)(2,1)} %copy.52.q_hbm, bf16[320,1280]{1,0:T(8,128)(2,1)} %w_hbm.1, bf16[264,640]{1,0:T(8,128)(2,1)} %copy-done.1, bf16[264,640]{1,0:T(8,128)(2,1)} %collective-permute-done.b1, bf16[264,640]{1,0:T(8,128)(2,1)} %collective-permute-done.1.b2, ...), custom_call_target="tpu_custom_call" | custom-call | flops 671088640 | bytes 3328000 | tf_op jit(solution)/shard_map/pallas_call | solution.py:86
  52.2 3.5 %all-to-all-start = ((bf16[4,64,1280]{2,1,0:T(8,128)(2,1)}), bf16[4,64,1280]{2,1,0:T(8,128)(2,1)S(1)}, u32[]{:S(2)}, u32[]{:S(2)}) async-start(bf16[4,64,1280]{2,1,0:T(8,128)(2,1)} %bitcast.16), calls=%async_computation | async-start | bytes 1310720 | tf_op jit(solution)/shard_map/all_to_all | solution.py:157
  56.0 8.6 %all-to-all-done = bf16[4,64,1280]{2,1,0:T(8,128)(2,1)S(1)} async-done(((bf16[4,64,1280]{2,1,0:T(8,128)(2,1)}), bf16[4,64,1280]{2,1,0:T(8,128)(2,1)S(1)}, u32[]{:S(2)}, u32[]{:S(2)}) %all-to-all-start) | async-done | bytes 655392 | tf_op jit(solution)/shard_map/all_to_all | solution.py:157
  65.1 0.5 convolution_convert_fusion.4
  65.7 0.7 copy.53
  66.4 3.3 %all-to-all-start.1 = ((bf16[64,4,160]{2,0,1:T(8,128)(2,1)}), bf16[64,4,160]{2,0,1:T(8,128)(2,1)S(1)}, u32[]{:S(2)}, u32[]{:S(2)}) async-start(bf16[64,4,160]{2,0,1:T(8,128)(2,1)} %copy.53), calls=%async_computation.1 | async-start | bytes 262144 | tf_op jit(solution)/shard_map/all_to_all | solution.py:166
  70.1 4.4 %all-to-all-done.1 = bf16[64,4,160]{2,0,1:T(8,128)(2,1)S(1)} async-done(((bf16[64,4,160]{2,0,1:T(8,128)(2,1)}), bf16[64,4,160]{2,0,1:T(8,128)(2,1)S(1)}, u32[]{:S(2)}, u32[]{:S(2)}) %all-to-all-start.1) | async-done | bytes 81952 | tf_op jit(solution)/shard_map/all_to_all | solution.py:166
  75.4 31.0 %all_to_all.28 = bf16[128,2,240]{2,1,0:T(2,128)(2,1)S(1)} all-to-all(bf16[128,2,240]{2,1,0:T(2,128)(2,1)S(1)} %reshape.156), channel_id=1, replica_groups=mesh['seq'=128,'tp'=4] {'seq'}, dimensions={0} | all-to-all | bytes 245760 | tf_op jit(solution)/shard_map/all_to_all | solution.py:187
  106.6 0.3 fusion.12
  107.3 0.8 convolution_convert_fusion.5
  (50 shorter events, 3.9 us)
Async XLA Ops:
  0.0 65.1 %copy-start = (bf16[1280,640]{1,0:T(8,128)(2,1)S(1)}, bf16[1280,640]{1,0:T(8,128)(2,1)}, u32[]{:S(2)}) copy-start(bf16[1280,640]{1,0:T(8,128)(2,1)} %param.25) | copy-start | bytes 4915204
  0.0 13.7 %copy-start.4 = (f32[1280]{0:T(1024)S(1)}, f32[1280]{0:T(1024)}, u32[]{:S(2)}) copy-start(f32[1280]{0:T(1024)} %param.17) | copy-start | bytes 15364
  1.6 12.1 %copy-start.3 = (bf16[1280,320]{0,1:T(8,128)(2,1)S(1)}, bf16[1280,320]{0,1:T(8,128)(2,1)}, u32[]{:S(2)}) copy-start(bf16[1280,320]{0,1:T(8,128)(2,1)} %param.19) | copy-start | bytes 2457604
  16.4 20.6 %copy-start.1 = (bf16[264,640]{1,0:T(8,128)(2,1)}, bf16[264,640]{1,0:T(8,128)(2,1)S(1)}, u32[]{:S(2)}) copy-start(bf16[264,640]{1,0:T(8,128)(2,1)S(1)} %pad_maximum_fusion.b0) | copy-start | bytes 1013764
  16.4 22.2 %collective-permute-start.3 = (bf16[264,640]{1,0:T(8,128)(2,1)S(1)}, bf16[264,640]{1,0:T(8,128)(2,1)}, u32[]{:S(2)}, u32[]{:S(2)}) collective-permute-start(bf16[264,640]{1,0:T(8,128)(2,1)S(1)} %pad_maximum_fusion.b0), channel_id=1, source_target_pairs={{8,0},{12,4},{16,8},{20,12},{24,16},{28,20},{32,24},{36,28},{40,32... | collective-permute-start | bytes 1013768 | tf_op jit(solution)/shard_map/ppermute | solution.py:20
  17.7 20.9 %collective-permute-start.2 = (bf16[264,640]{1,0:T(8,128)(2,1)S(1)}, bf16[264,640]{1,0:T(8,128)(2,1)}, u32[]{:S(2)}, u32[]{:S(2)}) collective-permute-start(bf16[264,640]{1,0:T(8,128)(2,1)S(1)} %pad_maximum_fusion.b0), channel_id=1, source_target_pairs={{4,0},{8,4},{12,8},{16,12},{20,16},{24,20},{28,24},{32,28},{36,32}... | collective-permute-start | bytes 1013768 | tf_op jit(solution)/shard_map/ppermute | solution.py:20
  28.2 11.5 %collective-permute-start.1 = (bf16[264,640]{1,0:T(8,128)(2,1)S(1)}, bf16[264,640]{1,0:T(8,128)(2,1)}, u32[]{:S(2)}, u32[]{:S(2)}) collective-permute-start(bf16[264,640]{1,0:T(8,128)(2,1)S(1)} %pad_maximum_fusion.b0), channel_id=1, source_target_pairs={{0,8},{4,12},{8,16},{12,20},{16,24},{20,28},{24,32},{28,36},{32,40... | collective-permute-start | bytes 1013768 | tf_op jit(solution)/shard_map/ppermute | solution.py:20
  33.2 10.6 %collective-permute-start = (bf16[264,640]{1,0:T(8,128)(2,1)S(1)}, bf16[264,640]{1,0:T(8,128)(2,1)}, u32[]{:S(2)}, u32[]{:S(2)}) collective-permute-start(bf16[264,640]{1,0:T(8,128)(2,1)S(1)} %pad_maximum_fusion.b0), channel_id=1, source_target_pairs={{0,4},{4,8},{8,12},{12,16},{16,20},{20,24},{24,28},{28,32},{32,36}... | collective-permute-start | bytes 1013768 | tf_op jit(solution)/shard_map/ppermute | solution.py:20
  52.2 3.5 %copy-start.5 = (s32[64]{0:T(128)S(1)}, s32[64]{0:T(128)}, u32[]{:S(2)}) copy-start(s32[64]{0:T(128)} %param.27) | copy-start | bytes 772
  52.2 12.3 %all-to-all-start = ((bf16[4,64,1280]{2,1,0:T(8,128)(2,1)}), bf16[4,64,1280]{2,1,0:T(8,128)(2,1)S(1)}, u32[]{:S(2)}, u32[]{:S(2)}) async-start(bf16[4,64,1280]{2,1,0:T(8,128)(2,1)} %bitcast.16), calls=%async_computation | async-start | bytes 1310720 | tf_op jit(solution)/shard_map/all_to_all | solution.py:157
  55.7 9.4 %copy-start.2 = (f32[1280]{0:T(1024)S(1)}, f32[1280]{0:T(1024)}, u32[]{:S(2)}) copy-start(f32[1280]{0:T(1024)} %param.24) | copy-start | bytes 15364
  66.4 8.1 %all-to-all-start.1 = ((bf16[64,4,160]{2,0,1:T(8,128)(2,1)}), bf16[64,4,160]{2,0,1:T(8,128)(2,1)S(1)}, u32[]{:S(2)}, u32[]{:S(2)}) async-start(bf16[64,4,160]{2,0,1:T(8,128)(2,1)} %copy.53), calls=%async_computation.1 | async-start | bytes 262144 | tf_op jit(solution)/shard_map/all_to_all | solution.py:166

commit v12 on v11

--- a/solution.py
+++ b/solution.py
@@ -163,8 +163,9 @@
     partial_proj = jnp.dot(picked, w_merge, preferred_element_type=jnp.float32)
     partial_proj = partial_proj.astype(jnp.bfloat16)
     width = partial_proj.shape[1] // tp_size
-    proj_pieces = lax.all_to_all(partial_proj, "tp", 1, 0, tiled=True)
-    projected = jnp.sum(proj_pieces.reshape(tp_size, chunk, width).astype(jnp.float32), axis=0)
+    proj_all = lax.all_gather(partial_proj, "tp", axis=0, tiled=False)
+    proj_pieces = lax.dynamic_slice_in_dim(proj_all, position * width, width, 2)
+    projected = jnp.sum(proj_pieces.astype(jnp.float32), axis=0)
     projected = projected.astype(jnp.bfloat16)
     slot_count = projected.shape[0]
 

time: 109 us -> 112 us (1.028)
  blocking collectives: 42.7 us -> 53.4 us
  waiting for transfers between devices: 18.2 us -> 13.5 us
  starting transfers between devices: 25.5 us -> 23 us
  other arithmetic: 3.42 us -> 4.64 us
    all_gather x0 -> x1, blocking collectives: none -> 10.5 us  [body(): proj_all = lax.all_gather(partial_proj, 'tp', axis=0, tiled=False)]
    all_to_all x1 -> x0, waiting for transfers between devices: 4.42 us -> none  [body(): proj_pieces = lax.all_to_all(partial_proj, 'tp', 1, 0, tiled=True)]
    all_to_all x1 -> x0, starting transfers between devices: 3.32 us -> none  [body(): proj_pieces = lax.all_to_all(partial_proj, 'tp', 1, 0, tiled=True)]
  transfers between devices with their start and end apart: 6 -> 5, of which waited for: 4 -> 3; matrix products, arithmetic and copies ran while one was open for 4% -> 4% of each run, Pallas kernels for 0% -> 0%
where the time goes in v12:
time: 112 us
  blocking collectives  53.4 us (48%)
  starting transfers between devices  23 us (21%)
  waiting for transfers between devices  13.5 us (12%)
  Pallas kernels  8.43 us (8%)
  matrix products  5.34 us (5%)
  other arithmetic  4.64 us (4%)
  local copies, waits for them, and re-layouts  3.35 us (3%)
    all_to_all x1, blocking collectives, body(): lax.all_to_all(send_buf, 'seq', 0, 0, tiled=True)  31.5 us
    ppermute x4, starting transfers between devices, from_behind(): return lax.ppermute(shard, axis, pairs)  18.8 us
    all_gather x1, blocking collectives, body(): gathered = lax.all_gather(tokens, 'tp', axis=1, tiled=True)  11.5 us
    all_gather x1, blocking collectives, body(): proj_all = lax.all_gather(partial_proj, 'tp', axis=0, tiled=False)  10.5 us
    pallas_call x1, Pallas kernels, attention(): pl.pallas_call(functools.partial(attn_kernel, heads, rows), out_shape=jax...  8.43 us
    all_to_all x1, waiting for transfers between devices, body(): pieces = lax.all_to_all(partial_sum, 'tp', 0, 0, tiled=True)  7.5 us
    ppermute x4, waiting for transfers between devices, from_behind(): return lax.ppermute(shard, axis, pairs)  6.03 us
    all_to_all x1, starting transfers between devices, body(): pieces = lax.all_to_all(partial_sum, 'tp', 0, 0, tiled=True)  4.17 us
  transfers between devices with their start and end apart: 5, of which 3 were waited for; matrix products, arithmetic and copies ran while one was open for 4% of the time, Pallas kernels for 0%

profile of v12, /device:TPU:1, one launch (start us, length us, event | category | flops | bytes accessed | tf_op | source)
XLA Modules:
  0.0 112.0 jit_solution(13491641863491595784)
XLA Ops:
  0.0 0.9 fusion.26
  0.9 0.7 convert_bitcast_fusion
  1.7 11.5 %all_gather.9 = bf16[256,1280]{0,1:T(8,128)(2,1)S(1)} all-gather(bf16[256,320]{0,1:T(8,128)(2,1)} %param.16), channel_id=1, replica_groups=mesh['seq'=128,'tp'=4] {'tp'}, dimensions={1}, use_global_device_ids=true | all-gather | bytes 819200 | tf_op jit(solution)/shard_map/all_gather | solution.py:137
  13.6 0.5 convolution_convert_fusion.1
  14.3 1.6 %convolution_convert_fusion = bf16[256,320]{0,1:T(8,128)(2,1)S(1)} fusion(bf16[1280,320]{0,1:T(8,128)(2,1)} %param.20, bf16[256,1280]{0,1:T(8,128)(2,1)S(1)} %all_gather.9, f32[1280]{0:T(1024)S(1)} %copy-done.6, f32[256]{0:T(256)S(1)} %add_rsqrt_fusion, f32[256]{0:T(256)S(1)} %broadcast_multiply_fusion), kind=kOutput, calls=%fused_computation.9 | convolution fusion | flops 211435520 | bytes 1645568 | tf_op jit(solution)/shard_map/dot_general | solution.py:142
  16.3 1.4 %collective-permute-start.3 = (bf16[264,640]{1,0:T(8,128)(2,1)S(1)}, bf16[264,640]{1,0:T(8,128)(2,1)S(1)}, u32[]{:S(2)}, u32[]{:S(2)}) collective-permute-start(bf16[264,640]{1,0:T(8,128)(2,1)S(1)} %pad_maximum_fusion.b0), channel_id=1, source_target_pairs={{8,0},{12,4},{16,8},{20,12},{24,16},{28,20},{32,24},{36,28},{40,32... | collective-permute-start | bytes 1013768 | tf_op jit(solution)/shard_map/ppermute | solution.py:20
  17.7 10.5 %collective-permute-start.2 = (bf16[264,640]{1,0:T(8,128)(2,1)S(1)}, bf16[264,640]{1,0:T(8,128)(2,1)S(1)}, u32[]{:S(2)}, u32[]{:S(2)}) collective-permute-start(bf16[264,640]{1,0:T(8,128)(2,1)S(1)} %pad_maximum_fusion.b0), channel_id=1, source_target_pairs={{4,0},{8,4},{12,8},{16,12},{20,16},{24,20},{28,24},{32,28},{36,32}... | collective-permute-start | bytes 1013768 | tf_op jit(solution)/shard_map/ppermute | solution.py:20
  28.2 5.0 %collective-permute-start.1 = (bf16[264,640]{1,0:T(8,128)(2,1)S(1)}, bf16[264,640]{1,0:T(8,128)(2,1)}, u32[]{:S(2)}, u32[]{:S(2)}) collective-permute-start(bf16[264,640]{1,0:T(8,128)(2,1)S(1)} %pad_maximum_fusion.b0), channel_id=1, source_target_pairs={{0,8},{4,12},{8,16},{12,20},{16,24},{20,28},{24,32},{28,36},{32,40... | collective-permute-start | bytes 1013768 | tf_op jit(solution)/shard_map/ppermute | solution.py:20
  33.2 1.9 %collective-permute-start = (bf16[264,640]{1,0:T(8,128)(2,1)S(1)}, bf16[264,640]{1,0:T(8,128)(2,1)}, u32[]{:S(2)}, u32[]{:S(2)}) collective-permute-start(bf16[264,640]{1,0:T(8,128)(2,1)S(1)} %pad_maximum_fusion.b0), channel_id=1, source_target_pairs={{0,4},{4,8},{8,12},{12,16},{16,20},{20,24},{24,28},{28,32},{32,36}... | collective-permute-start | bytes 1013768 | tf_op jit(solution)/shard_map/ppermute | solution.py:20
  35.1 1.6 %convolution_convert_fusion.2 = bf16[256,320]{0,1:T(8,128)(2,1)S(1)} fusion(bf16[1280,320]{0,1:T(8,128)(2,1)} %param.18, bf16[256,1280]{0,1:T(8,128)(2,1)S(1)} %all_gather.9, f32[1280]{0:T(1024)S(1)} %copy-done.6, f32[256]{0:T(256)S(1)} %add_rsqrt_fusion, f32[256]{0:T(256)S(1)} %broadcast_multiply_fusion), kind=kOutput, calls=%fused_computation.11 | convolution fusion | flops 211435520 | bytes 1645568 | tf_op jit(solution)/shard_map/dot_general | solution.py:140
  36.8 0.8 copy.49.q_hbm
  37.8 1.9 %collective-permute-done.1.b2 = bf16[264,640]{1,0:T(8,128)(2,1)} collective-permute-done((bf16[264,640]{1,0:T(8,128)(2,1)S(1)}, bf16[264,640]{1,0:T(8,128)(2,1)}, u32[]{:S(2)}, u32[]{:S(2)}) %collective-permute-start.1) | collective-permute-done | bytes 337952 | tf_op jit(solution)/shard_map/ppermute | solution.py:20
  39.7 4.1 %collective-permute-done.b1 = bf16[264,640]{1,0:T(8,128)(2,1)} collective-permute-done((bf16[264,640]{1,0:T(8,128)(2,1)S(1)}, bf16[264,640]{1,0:T(8,128)(2,1)}, u32[]{:S(2)}, u32[]{:S(2)}) %collective-permute-start) | collective-permute-done | bytes 337952 | tf_op jit(solution)/shard_map/ppermute | solution.py:20
  43.8 8.4 %shard_map.118 = bf16[256,1280]{1,0:T(8,128)(2,1)} custom-call(bf16[256,320]{1,0:T(8,128)(2,1)} %copy.49.q_hbm, bf16[320,1280]{1,0:T(8,128)(2,1)} %w_hbm.1, bf16[264,640]{1,0:T(8,128)(2,1)} %copy-done.1, bf16[264,640]{1,0:T(8,128)(2,1)} %collective-permute-done.b1, bf16[264,640]{1,0:T(8,128)(2,1)} %collective-permute-done.1.b2, bf16[264,640]{1,0:T(8,128)(2,1)} %copy-done.3, ...), custom_call_target="tpu_custom_call" | custom-call | flops 671088640 | bytes 3328000 | tf_op jit(solution)/shard_map/pallas_call | solution.py:86
  52.3 4.2 %all-to-all-start = ((bf16[4,64,1280]{2,1,0:T(8,128)(2,1)}), bf16[4,64,1280]{2,1,0:T(8,128)(2,1)}, u32[]{:S(2)}, u32[]{:S(2)}) async-start(bf16[4,64,1280]{2,1,0:T(8,128)(2,1)} %bitcast.17), calls=%async_computation | async-start | bytes 1310720 | tf_op jit(solution)/shard_map/all_to_all | solution.py:157
  57.1 0.7 gather_fusion
  57.8 7.5 %all-to-all-done = bf16[4,64,1280]{2,1,0:T(8,128)(2,1)} async-done(((bf16[4,64,1280]{2,1,0:T(8,128)(2,1)}), bf16[4,64,1280]{2,1,0:T(8,128)(2,1)}, u32[]{:S(2)}, u32[]{:S(2)}) %all-to-all-start) | async-done | bytes 655392 | tf_op jit(solution)/shard_map/all_to_all | solution.py:157
  65.3 1.2 %convert_reduce_fusion.1 = f32[64,1280]{1,0:T(8,128)S(1)} fusion(bf16[4,64,1280]{2,1,0:T(8,128)(2,1)} %all-to-all-done), kind=kLoop, calls=%fused_computation.8 | loop fusion | flops 573440 | bytes 983040 | tf_op jit(solution)/shard_map/reduce_sum | solution.py:158
  67.0 0.5 convolution_convert_fusion.4
  67.5 10.5 %all-gather = bf16[256,640]{1,0:T(8,128)(2,1)S(1)} all-gather(bf16[64,640]{1,0:T(8,128)(2,1)S(1)} %convolution_convert_fusion.4), channel_id=2, replica_groups=mesh['seq'=128,'tp'=4] {'tp'}, dimensions={0}, use_global_device_ids=true | all-gather | bytes 409600 | tf_op jit(solution)/shard_map/all_gather | solution.py:166
  78.5 0.3 fusion.6
  78.9 31.5 %all_to_all.15 = bf16[128,2,240]{2,1,0:T(2,128)(2,1)S(1)} all-to-all(bf16[128,2,240]{2,1,0:T(2,128)(2,1)S(1)} %reshape.152), channel_id=1, replica_groups=mesh['seq'=128,'tp'=4] {'seq'}, dimensions={0} | all-to-all | bytes 245760 | tf_op jit(solution)/shard_map/all_to_all | solution.py:188
  110.6 0.3 fusion.12
  111.2 0.8 convolution_convert_fusion.5
  (51 shorter events, 3.5 us)
Async XLA Ops:
  0.0 67.0 %copy-start = (bf16[1280,640]{1,0:T(8,128)(2,1)S(1)}, bf16[1280,640]{1,0:T(8,128)(2,1)}, u32[]{:S(2)}) copy-start(bf16[1280,640]{1,0:T(8,128)(2,1)} %param.25) | copy-start | bytes 4915204
  0.0 13.6 %copy-start.6 = (f32[1280]{0:T(1024)S(1)}, f32[1280]{0:T(1024)}, u32[]{:S(2)}) copy-start(f32[1280]{0:T(1024)} %param.17) | copy-start | bytes 15364
  0.0 13.6 %copy-start.5 = (bf16[1280,320]{0,1:T(8,128)(2,1)S(1)}, bf16[1280,320]{0,1:T(8,128)(2,1)}, u32[]{:S(2)}) copy-start(bf16[1280,320]{0,1:T(8,128)(2,1)} %param.19) | copy-start | bytes 2457604
  16.3 21.3 %copy-start.1 = (bf16[264,640]{1,0:T(8,128)(2,1)}, bf16[264,640]{1,0:T(8,128)(2,1)S(1)}, u32[]{:S(2)}) copy-start(bf16[264,640]{1,0:T(8,128)(2,1)S(1)} %pad_maximum_fusion.b0) | copy-start | bytes 1013764
  16.3 21.3 %copy-start.7 = (s32[64]{0:T(128)S(1)}, s32[64]{0:T(128)}, u32[]{:S(2)}) copy-start(s32[64]{0:T(128)} %param.27) | copy-start | bytes 772
  16.3 21.5 %collective-permute-start.3 = (bf16[264,640]{1,0:T(8,128)(2,1)S(1)}, bf16[264,640]{1,0:T(8,128)(2,1)S(1)}, u32[]{:S(2)}, u32[]{:S(2)}) collective-permute-start(bf16[264,640]{1,0:T(8,128)(2,1)S(1)} %pad_maximum_fusion.b0), channel_id=1, source_target_pairs={{8,0},{12,4},{16,8},{20,12},{24,16},{28,20},{32,24},{36,28},{40,32... | collective-permute-start | bytes 1013768 | tf_op jit(solution)/shard_map/ppermute | solution.py:20
  17.7 20.0 %collective-permute-start.2 = (bf16[264,640]{1,0:T(8,128)(2,1)S(1)}, bf16[264,640]{1,0:T(8,128)(2,1)S(1)}, u32[]{:S(2)}, u32[]{:S(2)}) collective-permute-start(bf16[264,640]{1,0:T(8,128)(2,1)S(1)} %pad_maximum_fusion.b0), channel_id=1, source_target_pairs={{4,0},{8,4},{12,8},{16,12},{20,16},{24,20},{28,24},{32,28},{36,32}... | collective-permute-start | bytes 1013768 | tf_op jit(solution)/shard_map/ppermute | solution.py:20
  28.2 11.5 %collective-permute-start.1 = (bf16[264,640]{1,0:T(8,128)(2,1)S(1)}, bf16[264,640]{1,0:T(8,128)(2,1)}, u32[]{:S(2)}, u32[]{:S(2)}) collective-permute-start(bf16[264,640]{1,0:T(8,128)(2,1)S(1)} %pad_maximum_fusion.b0), channel_id=1, source_target_pairs={{0,8},{4,12},{8,16},{12,20},{16,24},{20,28},{24,32},{28,36},{32,40... | collective-permute-start | bytes 1013768 | tf_op jit(solution)/shard_map/ppermute | solution.py:20
  33.2 10.6 %collective-permute-start = (bf16[264,640]{1,0:T(8,128)(2,1)S(1)}, bf16[264,640]{1,0:T(8,128)(2,1)}, u32[]{:S(2)}, u32[]{:S(2)}) collective-permute-start(bf16[264,640]{1,0:T(8,128)(2,1)S(1)} %pad_maximum_fusion.b0), channel_id=1, source_target_pairs={{0,4},{4,8},{8,12},{12,16},{16,20},{20,24},{24,28},{28,32},{32,36}... | collective-permute-start | bytes 1013768 | tf_op jit(solution)/shard_map/ppermute | solution.py:20
  37.8 6.1 %copy-start.2 = (bf16[264,640]{1,0:T(8,128)(2,1)}, bf16[264,640]{1,0:T(8,128)(2,1)S(1)}, u32[]{:S(2)}) copy-start(bf16[264,640]{1,0:T(8,128)(2,1)S(1)} %collective-permute-done.3.b4) | copy-start | bytes 1013764
  37.8 6.0 %copy-start.3 = (bf16[264,640]{1,0:T(8,128)(2,1)}, bf16[264,640]{1,0:T(8,128)(2,1)S(1)}, u32[]{:S(2)}) copy-start(bf16[264,640]{1,0:T(8,128)(2,1)S(1)} %collective-permute-done.2.b3) | copy-start | bytes 1013764
  52.3 13.1 %all-to-all-start = ((bf16[4,64,1280]{2,1,0:T(8,128)(2,1)}), bf16[4,64,1280]{2,1,0:T(8,128)(2,1)}, u32[]{:S(2)}, u32[]{:S(2)}) async-start(bf16[4,64,1280]{2,1,0:T(8,128)(2,1)} %bitcast.17), calls=%async_computation | async-start | bytes 1310720 | tf_op jit(solution)/shard_map/all_to_all | solution.py:157
  57.8 9.2 %copy-start.4 = (f32[1280]{0:T(1024)S(1)}, f32[1280]{0:T(1024)}, u32[]{:S(2)}) copy-start(f32[1280]{0:T(1024)} %param.24) | copy-start | bytes 15364

commit v13 on v11

--- a/solution.py
+++ b/solution.py
@@ -178,15 +178,16 @@
     target = jnp.arange(seq_size * CAP)
     send_hot = (send_pos[None, :] == target[:, None]).astype(jnp.bfloat16)
     send_rows = jnp.dot(send_hot, projected, preferred_element_type=jnp.float32)
-    send_rows = send_rows.astype(jnp.bfloat16).reshape(seq_size, CAP, width)
+    send_rows = send_rows.astype(jnp.bfloat16).reshape(seq_size, CAP * width)
     slot_code = (slot + 1).astype(jnp.float32)
     send_slot = jnp.dot(send_hot.astype(jnp.float32), slot_code, precision=lax.Precision.HIGHEST)
-    slot_row = jnp.zeros((seq_size, 1, width), jnp.bfloat16)
-    slot_row = slot_row.at[:, 0, :CAP].set(send_slot.reshape(seq_size, CAP).astype(jnp.bfloat16))
-    send_buf = jnp.concatenate([send_rows, slot_row], axis=1).reshape(seq_size * (CAP + 1), width)
-    recv = lax.all_to_all(send_buf, "seq", 0, 0, tiled=True).reshape(seq_size, CAP + 1, width)
-    recv_rows = recv[:, :CAP, :].reshape(seq_size * CAP, width)
-    recv_slot = recv[:, CAP, :CAP].reshape(seq_size * CAP).astype(jnp.int32) - 1
+    strip = 16
+    slot_strip = jnp.zeros((seq_size, strip), jnp.bfloat16)
+    slot_strip = slot_strip.at[:, :CAP].set(send_slot.reshape(seq_size, CAP).astype(jnp.bfloat16))
+    send_buf = jnp.concatenate([send_rows, slot_strip], axis=1)
+    recv = lax.all_to_all(send_buf, "seq", 0, 0, tiled=True)
+    recv_rows = recv[:, :CAP * width].reshape(seq_size * CAP, width)
+    recv_slot = recv[:, CAP * width:CAP * width + CAP].reshape(seq_size * CAP).astype(jnp.int32) - 1
     recv_hot = (recv_slot[None, :] == lane[:, None]).astype(jnp.bfloat16)
     delivered = jnp.dot(recv_hot, recv_rows, preferred_element_type=jnp.float32)
     return delivered.astype(jnp.bfloat16)

time: 109 us -> 111 us (1.018)
  other arithmetic: 3.42 us -> 6.08 us
    all_to_all x1, waiting for transfers between devices: 8.59 us -> 7.14 us  [body(): pieces = lax.all_to_all(partial_sum, 'tp', 0, 0, tiled=True)]
    another operation x1 -> x3, other arithmetic: 0.84 us -> 2.14 us
    reduce_sum x1, other arithmetic: 0.09 us -> 1.21 us  [body(): jnp.sum(pieces.reshape(tp_size, chunk, -1).astype(jnp.float32), axis=0)]
  transfers between devices with their start and end apart: 6 -> 6, of which waited for: 4 -> 4; matrix products, arithmetic and copies ran while one was open for 4% -> 5% of each run, Pallas kernels for 0% -> 0%
where the time goes in v13:
time: 111 us; the launch traced here: 110 us
  blocking collectives  42 us (38%)
  starting transfers between devices  26.2 us (24%)
  waiting for transfers between devices  17.1 us (15%)
  Pallas kernels  8.42 us (8%)
  other arithmetic  6.08 us (5%)
  matrix products  5.35 us (5%)
  local copies, waits for them, and re-layouts  4.85 us (4%)
    all_to_all x1, blocking collectives, body(): recv = lax.all_to_all(send_buf, 'seq', 0, 0, tiled=True)  30.5 us
    ppermute x4, starting transfers between devices, from_behind(): return lax.ppermute(shard, axis, pairs)  18.7 us
    all_gather x1, blocking collectives, body(): gathered = lax.all_gather(tokens, 'tp', axis=1, tiled=True)  11.5 us
    pallas_call x1, Pallas kernels, attention(): pl.pallas_call(functools.partial(attn_kernel, heads, rows), out_shape=jax...  8.42 us
    all_to_all x1, waiting for transfers between devices, body(): pieces = lax.all_to_all(partial_sum, 'tp', 0, 0, tiled=True)  7.14 us
    ppermute x4, waiting for transfers between devices, from_behind(): return lax.ppermute(shard, axis, pairs)  5.99 us
    all_to_all x1, starting transfers between devices, body(): pieces = lax.all_to_all(partial_sum, 'tp', 0, 0, tiled=True)  4.17 us
    all_to_all x1, waiting for transfers between devices, body(): proj_pieces = lax.all_to_all(partial_proj, 'tp', 1, 0, tiled=True)  3.98 us
  transfers between devices with their start and end apart: 6, of which 4 were waited for; matrix products, arithmetic and copies ran while one was open for 5% of the time, Pallas kernels for 0%

profile of v13, /device:TPU:1, one launch (start us, length us, event | category | flops | bytes accessed | tf_op | source)
XLA Modules:
  0.0 110.3 jit_solution(3071703009273039547)
XLA Ops:
  0.0 0.9 fusion.25
  0.9 0.7 convert_bitcast_fusion
  1.7 11.5 %all_gather.3 = bf16[256,1280]{0,1:T(8,128)(2,1)S(1)} all-gather(bf16[256,320]{0,1:T(8,128)(2,1)} %param.16), channel_id=1, replica_groups=mesh['seq'=128,'tp'=4] {'tp'}, dimensions={1}, use_global_device_ids=true | all-gather | bytes 819200 | tf_op jit(solution)/shard_map/all_gather | solution.py:137
  14.3 1.6 %convolution_convert_fusion = bf16[256,320]{0,1:T(8,128)(2,1)S(1)} fusion(bf16[1280,320]{0,1:T(8,128)(2,1)} %param.20, bf16[256,1280]{0,1:T(8,128)(2,1)S(1)} %all_gather.3, f32[1280]{0:T(1024)S(1)} %copy-done.6, f32[256]{0:T(256)S(1)} %add_rsqrt_fusion, f32[256]{0:T(256)S(1)} %broadcast_multiply_fusion), kind=kOutput, calls=%fused_computation.9 | convolution fusion | flops 211435520 | bytes 1645568 | tf_op jit(solution)/shard_map/dot_general | solution.py:142
  16.3 1.3 %collective-permute-start.3 = (bf16[264,640]{1,0:T(8,128)(2,1)S(1)}, bf16[264,640]{1,0:T(8,128)(2,1)S(1)}, u32[]{:S(2)}, u32[]{:S(2)}) collective-permute-start(bf16[264,640]{1,0:T(8,128)(2,1)S(1)} %pad_maximum_fusion.b0), channel_id=1, source_target_pairs={{8,0},{12,4},{16,8},{20,12},{24,16},{28,20},{32,24},{36,28},{40,32... | collective-permute-start | bytes 1013768 | tf_op jit(solution)/shard_map/ppermute | solution.py:20
  17.6 10.5 %collective-permute-start.2 = (bf16[264,640]{1,0:T(8,128)(2,1)S(1)}, bf16[264,640]{1,0:T(8,128)(2,1)S(1)}, u32[]{:S(2)}, u32[]{:S(2)}) collective-permute-start(bf16[264,640]{1,0:T(8,128)(2,1)S(1)} %pad_maximum_fusion.b0), channel_id=1, source_target_pairs={{4,0},{8,4},{12,8},{16,12},{20,16},{24,20},{28,24},{32,28},{36,32}... | collective-permute-start | bytes 1013768 | tf_op jit(solution)/shard_map/ppermute | solution.py:20
  28.0 5.0 %collective-permute-start.1 = (bf16[264,640]{1,0:T(8,128)(2,1)S(1)}, bf16[264,640]{1,0:T(8,128)(2,1)}, u32[]{:S(2)}, u32[]{:S(2)}) collective-permute-start(bf16[264,640]{1,0:T(8,128)(2,1)S(1)} %pad_maximum_fusion.b0), channel_id=1, source_target_pairs={{0,8},{4,12},{8,16},{12,20},{16,24},{20,28},{24,32},{28,36},{32,40... | collective-permute-start | bytes 1013768 | tf_op jit(solution)/shard_map/ppermute | solution.py:20
  33.1 1.9 %collective-permute-start = (bf16[264,640]{1,0:T(8,128)(2,1)S(1)}, bf16[264,640]{1,0:T(8,128)(2,1)}, u32[]{:S(2)}, u32[]{:S(2)}) collective-permute-start(bf16[264,640]{1,0:T(8,128)(2,1)S(1)} %pad_maximum_fusion.b0), channel_id=1, source_target_pairs={{0,4},{4,8},{8,12},{12,16},{16,20},{20,24},{24,28},{28,32},{32,36}... | collective-permute-start | bytes 1013768 | tf_op jit(solution)/shard_map/ppermute | solution.py:20
  35.0 1.6 %convolution_convert_fusion.2 = bf16[256,320]{0,1:T(8,128)(2,1)S(1)} fusion(bf16[1280,320]{0,1:T(8,128)(2,1)} %param.18, bf16[256,1280]{0,1:T(8,128)(2,1)S(1)} %all_gather.3, f32[1280]{0:T(1024)S(1)} %copy-done.6, f32[256]{0:T(256)S(1)} %add_rsqrt_fusion, f32[256]{0:T(256)S(1)} %broadcast_multiply_fusion), kind=kOutput, calls=%fused_computation.11 | convolution fusion | flops 211435520 | bytes 1645568 | tf_op jit(solution)/shard_map/dot_general | solution.py:140
  36.6 0.8 copy.52.q_hbm
  37.7 1.9 %collective-permute-done.1.b2 = bf16[264,640]{1,0:T(8,128)(2,1)} collective-permute-done((bf16[264,640]{1,0:T(8,128)(2,1)S(1)}, bf16[264,640]{1,0:T(8,128)(2,1)}, u32[]{:S(2)}, u32[]{:S(2)}) %collective-permute-start.1) | collective-permute-done | bytes 337952 | tf_op jit(solution)/shard_map/ppermute | solution.py:20
  39.6 4.1 %collective-permute-done.b1 = bf16[264,640]{1,0:T(8,128)(2,1)} collective-permute-done((bf16[264,640]{1,0:T(8,128)(2,1)S(1)}, bf16[264,640]{1,0:T(8,128)(2,1)}, u32[]{:S(2)}, u32[]{:S(2)}) %collective-permute-start) | collective-permute-done | bytes 337952 | tf_op jit(solution)/shard_map/ppermute | solution.py:20
  43.7 8.4 %shard_map.118 = bf16[256,1280]{1,0:T(8,128)(2,1)} custom-call(bf16[256,320]{1,0:T(8,128)(2,1)} %copy.52.q_hbm, bf16[320,1280]{1,0:T(8,128)(2,1)} %w_hbm.1, bf16[264,640]{1,0:T(8,128)(2,1)} %copy-done.1, bf16[264,640]{1,0:T(8,128)(2,1)} %collective-permute-done.b1, bf16[264,640]{1,0:T(8,128)(2,1)} %collective-permute-done.1.b2, bf16[264,640]{1,0:T(8,128)(2,1)} %copy-done.3, ...), custom_call_target="tpu_custom_call" | custom-call | flops 671088640 | bytes 3328000 | tf_op jit(solution)/shard_map/pallas_call | solution.py:86
  52.1 4.2 %all-to-all-start = ((bf16[4,64,1280]{2,1,0:T(8,128)(2,1)}), bf16[4,64,1280]{2,1,0:T(8,128)(2,1)}, u32[]{:S(2)}, u32[]{:S(2)}) async-start(bf16[4,64,1280]{2,1,0:T(8,128)(2,1)} %bitcast.19), calls=%async_computation | async-start | bytes 1310720 | tf_op jit(solution)/shard_map/all_to_all | solution.py:157
  56.5 0.7 gather_fusion
  58.1 7.1 %all-to-all-done = bf16[4,64,1280]{2,1,0:T(8,128)(2,1)} async-done(((bf16[4,64,1280]{2,1,0:T(8,128)(2,1)}), bf16[4,64,1280]{2,1,0:T(8,128)(2,1)}, u32[]{:S(2)}, u32[]{:S(2)}) %all-to-all-start) | async-done | bytes 655392 | tf_op jit(solution)/shard_map/all_to_all | solution.py:157
  65.2 1.2 %convert_reduce_fusion.1 = f32[64,1280]{1,0:T(8,128)S(1)} fusion(bf16[4,64,1280]{2,1,0:T(8,128)(2,1)} %all-to-all-done), kind=kLoop, calls=%fused_computation.8 | loop fusion | flops 573440 | bytes 983040 | tf_op jit(solution)/shard_map/reduce_sum | solution.py:158
  67.5 0.7 copy.53
  68.2 3.3 %all-to-all-start.1 = ((bf16[64,4,160]{2,0,1:T(8,128)(2,1)}), bf16[64,4,160]{2,0,1:T(8,128)(2,1)S(1)}, u32[]{:S(2)}, u32[]{:S(2)}) async-start(bf16[64,4,160]{2,0,1:T(8,128)(2,1)} %copy.53), calls=%async_computation.1 | async-start | bytes 262144 | tf_op jit(solution)/shard_map/all_to_all | solution.py:166
  71.5 0.7 broadcast_select_fusion
  72.3 4.0 %all-to-all-done.1 = bf16[64,4,160]{2,0,1:T(8,128)(2,1)S(1)} async-done(((bf16[64,4,160]{2,0,1:T(8,128)(2,1)}), bf16[64,4,160]{2,0,1:T(8,128)(2,1)S(1)}, u32[]{:S(2)}, u32[]{:S(2)}) %all-to-all-start.1) | async-done | bytes 81952 | tf_op jit(solution)/shard_map/all_to_all | solution.py:166
  77.4 0.7 reduce.13
  78.2 30.5 %all_to_all.34 = bf16[128,2,168]{2,1,0:T(2,128)(2,1)S(1)} all-to-all(bf16[128,2,168]{2,1,0:T(2,128)(2,1)S(1)} %reshape.135), channel_id=1, replica_groups=mesh['seq'=128,'tp'=4] {'seq'}, dimensions={0} | all-to-all | bytes 172032 | tf_op jit(solution)/shard_map/all_to_all | solution.py:188
  109.5 0.8 convolution_convert_fusion.5
  (60 shorter events, 6.0 us)
Async XLA Ops:
  0.0 66.9 %copy-start = (bf16[1280,640]{1,0:T(8,128)(2,1)S(1)}, bf16[1280,640]{1,0:T(8,128)(2,1)}, u32[]{:S(2)}) copy-start(bf16[1280,640]{1,0:T(8,128)(2,1)} %param.25) | copy-start | bytes 4915204
  0.0 13.6 %copy-start.6 = (f32[1280]{0:T(1024)S(1)}, f32[1280]{0:T(1024)}, u32[]{:S(2)}) copy-start(f32[1280]{0:T(1024)} %param.17) | copy-start | bytes 15364
  0.0 13.6 %copy-start.5 = (bf16[1280,320]{0,1:T(8,128)(2,1)S(1)}, bf16[1280,320]{0,1:T(8,128)(2,1)}, u32[]{:S(2)}) copy-start(bf16[1280,320]{0,1:T(8,128)(2,1)} %param.19) | copy-start | bytes 2457604
  16.3 21.2 %copy-start.1 = (bf16[264,640]{1,0:T(8,128)(2,1)}, bf16[264,640]{1,0:T(8,128)(2,1)S(1)}, u32[]{:S(2)}) copy-start(bf16[264,640]{1,0:T(8,128)(2,1)S(1)} %pad_maximum_fusion.b0) | copy-start | bytes 1013764
  16.3 21.4 %collective-permute-start.3 = (bf16[264,640]{1,0:T(8,128)(2,1)S(1)}, bf16[264,640]{1,0:T(8,128)(2,1)S(1)}, u32[]{:S(2)}, u32[]{:S(2)}) collective-permute-start(bf16[264,640]{1,0:T(8,128)(2,1)S(1)} %pad_maximum_fusion.b0), channel_id=1, source_target_pairs={{8,0},{12,4},{16,8},{20,12},{24,16},{28,20},{32,24},{36,28},{40,32... | collective-permute-start | bytes 1013768 | tf_op jit(solution)/shard_map/ppermute | solution.py:20
  17.6 20.1 %collective-permute-start.2 = (bf16[264,640]{1,0:T(8,128)(2,1)S(1)}, bf16[264,640]{1,0:T(8,128)(2,1)S(1)}, u32[]{:S(2)}, u32[]{:S(2)}) collective-permute-start(bf16[264,640]{1,0:T(8,128)(2,1)S(1)} %pad_maximum_fusion.b0), channel_id=1, source_target_pairs={{4,0},{8,4},{12,8},{16,12},{20,16},{24,20},{28,24},{32,28},{36,32}... | collective-permute-start | bytes 1013768 | tf_op jit(solution)/shard_map/ppermute | solution.py:20
  28.0 11.5 %collective-permute-start.1 = (bf16[264,640]{1,0:T(8,128)(2,1)S(1)}, bf16[264,640]{1,0:T(8,128)(2,1)}, u32[]{:S(2)}, u32[]{:S(2)}) collective-permute-start(bf16[264,640]{1,0:T(8,128)(2,1)S(1)} %pad_maximum_fusion.b0), channel_id=1, source_target_pairs={{0,8},{4,12},{8,16},{12,20},{16,24},{20,28},{24,32},{28,36},{32,40... | collective-permute-start | bytes 1013768 | tf_op jit(solution)/shard_map/ppermute | solution.py:20
  33.1 10.6 %collective-permute-start = (bf16[264,640]{1,0:T(8,128)(2,1)S(1)}, bf16[264,640]{1,0:T(8,128)(2,1)}, u32[]{:S(2)}, u32[]{:S(2)}) collective-permute-start(bf16[264,640]{1,0:T(8,128)(2,1)S(1)} %pad_maximum_fusion.b0), channel_id=1, source_target_pairs={{0,4},{4,8},{8,12},{12,16},{16,20},{20,24},{24,28},{28,32},{32,36}... | collective-permute-start | bytes 1013768 | tf_op jit(solution)/shard_map/ppermute | solution.py:20
  35.0 2.5 %copy-start.7 = (s32[64]{0:T(128)S(1)}, s32[64]{0:T(128)}, u32[]{:S(2)}) copy-start(s32[64]{0:T(128)} %param.27) | copy-start | bytes 772
  37.7 6.0 %copy-start.2 = (bf16[264,640]{1,0:T(8,128)(2,1)}, bf16[264,640]{1,0:T(8,128)(2,1)S(1)}, u32[]{:S(2)}) copy-start(bf16[264,640]{1,0:T(8,128)(2,1)S(1)} %collective-permute-done.3.b4) | copy-start | bytes 1013764
  37.7 6.0 %copy-start.3 = (bf16[264,640]{1,0:T(8,128)(2,1)}, bf16[264,640]{1,0:T(8,128)(2,1)S(1)}, u32[]{:S(2)}) copy-start(bf16[264,640]{1,0:T(8,128)(2,1)S(1)} %collective-permute-done.2.b3) | copy-start | bytes 1013764
  52.1 13.1 %all-to-all-start = ((bf16[4,64,1280]{2,1,0:T(8,128)(2,1)}), bf16[4,64,1280]{2,1,0:T(8,128)(2,1)}, u32[]{:S(2)}, u32[]{:S(2)}) async-start(bf16[4,64,1280]{2,1,0:T(8,128)(2,1)} %bitcast.19), calls=%async_computation | async-start | bytes 1310720 | tf_op jit(solution)/shard_map/all_to_all | solution.py:157
  57.3 9.6 %copy-start.4 = (f32[1280]{0:T(1024)S(1)}, f32[1280]{0:T(1024)}, u32[]{:S(2)}) copy-start(f32[1280]{0:T(1024)} %param.24) | copy-start | bytes 15364
  68.2 8.1 %all-to-all-start.1 = ((bf16[64,4,160]{2,0,1:T(8,128)(2,1)}), bf16[64,4,160]{2,0,1:T(8,128)(2,1)S(1)}, u32[]{:S(2)}, u32[]{:S(2)}) async-start(bf16[64,4,160]{2,0,1:T(8,128)(2,1)} %copy.53), calls=%async_computation.1 | async-start | bytes 262144 | tf_op jit(solution)/shard_map/all_to_all | solution.py:166

commit v14 on v11

--- a/solution.py
+++ b/solution.py
@@ -150,7 +150,7 @@
     code_block = code_block.at[0:3, :row_count].set(code_rows)
     paired = jnp.concatenate([jnp.concatenate([key_rows, value_rows], axis=1), code_block], axis=0)
     pair_list = [paired]
-    for offset in (1, 2, -1, -2):
+    for offset in (1, -1, 2, -2):
         pair_list.append(from_behind(paired, "seq", offset))
     partial_sum = attention(queries, w_out, pair_list)
     chunk = row_count // tp_size

time: 109 us -> 105 us (0.963)
  waiting for transfers between devices: 18.2 us -> 15.1 us
  blocking collectives: 42.7 us -> 41.6 us
    ppermute x4, waiting for transfers between devices: 5.23 us -> 0.63 us  [from_behind(): return lax.ppermute(shard, axis, pairs)]
    all_to_all x1, waiting for transfers between devices: 8.59 us -> 10.1 us  [body(): pieces = lax.all_to_all(partial_sum, 'tp', 0, 0, tiled=True)]
  transfers between devices with their start and end apart: 6 -> 6, of which waited for: 4 -> 3; matrix products, arithmetic and copies ran while one was open for 4% -> 4% of each run, Pallas kernels for 0% -> 0%
where the time goes in v14:
time: 105 us; the launch traced here: 104 us
  blocking collectives  41.6 us (40%)
  starting transfers between devices  25.8 us (25%)
  waiting for transfers between devices  15.1 us (14%)
  Pallas kernels  8.42 us (8%)
  matrix products  5.35 us (5%)
  local copies, waits for them, and re-layouts  4.12 us (4%)
  other arithmetic  3.42 us (3%)
    all_to_all x1, blocking collectives, body(): lax.all_to_all(send_buf, 'seq', 0, 0, tiled=True)  30 us
    ppermute x4, starting transfers between devices, from_behind(): return lax.ppermute(shard, axis, pairs)  19 us
    all_gather x1, blocking collectives, body(): gathered = lax.all_gather(tokens, 'tp', axis=1, tiled=True)  11.7 us
    all_to_all x1, waiting for transfers between devices, body(): pieces = lax.all_to_all(partial_sum, 'tp', 0, 0, tiled=True)  10.1 us
    pallas_call x1, Pallas kernels, attention(): pl.pallas_call(functools.partial(attn_kernel, heads, rows), out_shape=jax...  8.42 us
    all_to_all x1, waiting for transfers between devices, body(): proj_pieces = lax.all_to_all(partial_proj, 'tp', 1, 0, tiled=True)  4.42 us
    all_to_all x1, starting transfers between devices, body(): pieces = lax.all_to_all(partial_sum, 'tp', 0, 0, tiled=True)  3.49 us
    all_to_all x1, starting transfers between devices, body(): proj_pieces = lax.all_to_all(partial_proj, 'tp', 1, 0, tiled=True)  3.32 us
  transfers between devices with their start and end apart: 6, of which 3 were waited for; matrix products, arithmetic and copies ran while one was open for 4% of the time, Pallas kernels for 0%

profile of v14, /device:TPU:1, one launch (start us, length us, event | category | flops | bytes accessed | tf_op | source)
XLA Modules:
  0.0 104.2 jit_solution(8583913257174972584)
XLA Ops:
  0.0 0.8 fusion.26
  0.9 0.7 convert_bitcast_fusion
  1.6 11.7 %all_gather.3 = bf16[256,1280]{0,1:T(8,128)(2,1)S(1)} all-gather(bf16[256,320]{0,1:T(8,128)(2,1)} %param.16), channel_id=1, replica_groups=mesh['seq'=128,'tp'=4] {'tp'}, dimensions={1}, use_global_device_ids=true | all-gather | bytes 819200 | tf_op jit(solution)/shard_map/all_gather | solution.py:137
  13.7 0.5 convolution_convert_fusion.1
  14.4 1.6 %convolution_convert_fusion = bf16[256,320]{0,1:T(8,128)(2,1)S(1)} fusion(bf16[1280,320]{0,1:T(8,128)(2,1)} %param.20, bf16[256,1280]{0,1:T(8,128)(2,1)S(1)} %all_gather.3, f32[1280]{0:T(1024)S(1)} %copy-done.4, f32[256]{0:T(256)S(1)} %add_rsqrt_fusion, f32[256]{0:T(256)S(1)} %broadcast_multiply_fusion), kind=kOutput, calls=%fused_computation.9 | convolution fusion | flops 211435520 | bytes 1645568 | tf_op jit(solution)/shard_map/dot_general | solution.py:142
  16.4 1.3 %collective-permute-start.3 = (bf16[264,640]{1,0:T(8,128)(2,1)S(1)}, bf16[264,640]{1,0:T(8,128)(2,1)}, u32[]{:S(2)}, u32[]{:S(2)}) collective-permute-start(bf16[264,640]{1,0:T(8,128)(2,1)S(1)} %pad_maximum_fusion.b0), channel_id=1, source_target_pairs={{8,0},{12,4},{16,8},{20,12},{24,16},{28,20},{32,24},{36,28},{40,32... | collective-permute-start | bytes 1013768 | tf_op jit(solution)/shard_map/ppermute | solution.py:20
  17.7 6.6 %collective-permute-start.2 = (bf16[264,640]{1,0:T(8,128)(2,1)S(1)}, bf16[264,640]{1,0:T(8,128)(2,1)}, u32[]{:S(2)}, u32[]{:S(2)}) collective-permute-start(bf16[264,640]{1,0:T(8,128)(2,1)S(1)} %pad_maximum_fusion.b0), channel_id=1, source_target_pairs={{0,8},{4,12},{8,16},{12,20},{16,24},{20,28},{24,32},{28,36},{32,40... | collective-permute-start | bytes 1013768 | tf_op jit(solution)/shard_map/ppermute | solution.py:20
  24.3 9.1 %collective-permute-start.1 = (bf16[264,640]{1,0:T(8,128)(2,1)S(1)}, bf16[264,640]{1,0:T(8,128)(2,1)}, u32[]{:S(2)}, u32[]{:S(2)}) collective-permute-start(bf16[264,640]{1,0:T(8,128)(2,1)S(1)} %pad_maximum_fusion.b0), channel_id=1, source_target_pairs={{4,0},{8,4},{12,8},{16,12},{20,16},{24,20},{28,24},{32,28},{36,32}... | collective-permute-start | bytes 1013768 | tf_op jit(solution)/shard_map/ppermute | solution.py:20
  33.4 1.9 %collective-permute-start = (bf16[264,640]{1,0:T(8,128)(2,1)S(1)}, bf16[264,640]{1,0:T(8,128)(2,1)}, u32[]{:S(2)}, u32[]{:S(2)}) collective-permute-start(bf16[264,640]{1,0:T(8,128)(2,1)S(1)} %pad_maximum_fusion.b0), channel_id=1, source_target_pairs={{0,4},{4,8},{8,12},{12,16},{16,20},{20,24},{24,28},{28,32},{32,36}... | collective-permute-start | bytes 1013768 | tf_op jit(solution)/shard_map/ppermute | solution.py:20
  35.4 1.6 %convolution_convert_fusion.2 = bf16[256,320]{0,1:T(8,128)(2,1)S(1)} fusion(bf16[1280,320]{0,1:T(8,128)(2,1)} %param.18, bf16[256,1280]{0,1:T(8,128)(2,1)S(1)} %all_gather.3, f32[1280]{0:T(1024)S(1)} %copy-done.4, f32[256]{0:T(256)S(1)} %add_rsqrt_fusion, f32[256]{0:T(256)S(1)} %broadcast_multiply_fusion), kind=kOutput, calls=%fused_computation.11 | convolution fusion | flops 211435520 | bytes 1645568 | tf_op jit(solution)/shard_map/dot_general | solution.py:140
  37.3 0.8 copy.52.q_hbm
  38.1 0.7 gather_fusion
  38.9 0.6 collective-permute-done.b1
  39.5 8.4 %shard_map.118 = bf16[256,1280]{1,0:T(8,128)(2,1)} custom-call(bf16[256,320]{1,0:T(8,128)(2,1)} %copy.52.q_hbm, bf16[320,1280]{1,0:T(8,128)(2,1)} %w_hbm.1, bf16[264,640]{1,0:T(8,128)(2,1)} %copy-done.1, bf16[264,640]{1,0:T(8,128)(2,1)} %collective-permute-done.b1, bf16[264,640]{1,0:T(8,128)(2,1)} %collective-permute-done.1.b2, ...), custom_call_target="tpu_custom_call" | custom-call | flops 671088640 | bytes 3328000 | tf_op jit(solution)/shard_map/pallas_call | solution.py:86
  47.9 3.5 %all-to-all-start = ((bf16[4,64,1280]{2,1,0:T(8,128)(2,1)}), bf16[4,64,1280]{2,1,0:T(8,128)(2,1)S(1)}, u32[]{:S(2)}, u32[]{:S(2)}) async-start(bf16[4,64,1280]{2,1,0:T(8,128)(2,1)} %bitcast.16), calls=%async_computation | async-start | bytes 1310720 | tf_op jit(solution)/shard_map/all_to_all | solution.py:157
  51.6 10.1 %all-to-all-done = bf16[4,64,1280]{2,1,0:T(8,128)(2,1)S(1)} async-done(((bf16[4,64,1280]{2,1,0:T(8,128)(2,1)}), bf16[4,64,1280]{2,1,0:T(8,128)(2,1)S(1)}, u32[]{:S(2)}, u32[]{:S(2)}) %all-to-all-start) | async-done | bytes 655392 | tf_op jit(solution)/shard_map/all_to_all | solution.py:157
  62.3 0.5 convolution_convert_fusion.4
  62.9 0.7 copy.53
  63.6 3.3 %all-to-all-start.1 = ((bf16[64,4,160]{2,0,1:T(8,128)(2,1)}), bf16[64,4,160]{2,0,1:T(8,128)(2,1)S(1)}, u32[]{:S(2)}, u32[]{:S(2)}) async-start(bf16[64,4,160]{2,0,1:T(8,128)(2,1)} %copy.53), calls=%async_computation.1 | async-start | bytes 262144 | tf_op jit(solution)/shard_map/all_to_all | solution.py:166
  67.3 4.4 %all-to-all-done.1 = bf16[64,4,160]{2,0,1:T(8,128)(2,1)S(1)} async-done(((bf16[64,4,160]{2,0,1:T(8,128)(2,1)}), bf16[64,4,160]{2,0,1:T(8,128)(2,1)S(1)}, u32[]{:S(2)}, u32[]{:S(2)}) %all-to-all-start.1) | async-done | bytes 81952 | tf_op jit(solution)/shard_map/all_to_all | solution.py:166
  72.1 0.3 fusion.6
  72.6 30.0 %all_to_all.28 = bf16[128,2,240]{2,1,0:T(2,128)(2,1)S(1)} all-to-all(bf16[128,2,240]{2,1,0:T(2,128)(2,1)S(1)} %reshape.156), channel_id=1, replica_groups=mesh['seq'=128,'tp'=4] {'seq'}, dimensions={0} | all-to-all | bytes 245760 | tf_op jit(solution)/shard_map/all_to_all | solution.py:187
  102.7 0.3 fusion.12
  103.4 0.8 convolution_convert_fusion.5
  (50 shorter events, 3.7 us)
Async XLA Ops:
  0.0 62.3 %copy-start = (bf16[1280,640]{1,0:T(8,128)(2,1)S(1)}, bf16[1280,640]{1,0:T(8,128)(2,1)}, u32[]{:S(2)}) copy-start(bf16[1280,640]{1,0:T(8,128)(2,1)} %param.25) | copy-start | bytes 4915204
  0.0 13.7 %copy-start.4 = (f32[1280]{0:T(1024)S(1)}, f32[1280]{0:T(1024)}, u32[]{:S(2)}) copy-start(f32[1280]{0:T(1024)} %param.17) | copy-start | bytes 15364
  1.6 12.1 %copy-start.3 = (bf16[1280,320]{0,1:T(8,128)(2,1)S(1)}, bf16[1280,320]{0,1:T(8,128)(2,1)}, u32[]{:S(2)}) copy-start(bf16[1280,320]{0,1:T(8,128)(2,1)} %param.19) | copy-start | bytes 2457604
  16.4 20.9 %copy-start.1 = (bf16[264,640]{1,0:T(8,128)(2,1)}, bf16[264,640]{1,0:T(8,128)(2,1)S(1)}, u32[]{:S(2)}) copy-start(bf16[264,640]{1,0:T(8,128)(2,1)S(1)} %pad_maximum_fusion.b0) | copy-start | bytes 1013764
  16.4 22.4 %collective-permute-start.3 = (bf16[264,640]{1,0:T(8,128)(2,1)S(1)}, bf16[264,640]{1,0:T(8,128)(2,1)}, u32[]{:S(2)}, u32[]{:S(2)}) collective-permute-start(bf16[264,640]{1,0:T(8,128)(2,1)S(1)} %pad_maximum_fusion.b0), channel_id=1, source_target_pairs={{8,0},{12,4},{16,8},{20,12},{24,16},{28,20},{32,24},{36,28},{40,32... | collective-permute-start | bytes 1013768 | tf_op jit(solution)/shard_map/ppermute | solution.py:20
  17.7 21.2 %collective-permute-start.2 = (bf16[264,640]{1,0:T(8,128)(2,1)S(1)}, bf16[264,640]{1,0:T(8,128)(2,1)}, u32[]{:S(2)}, u32[]{:S(2)}) collective-permute-start(bf16[264,640]{1,0:T(8,128)(2,1)S(1)} %pad_maximum_fusion.b0), channel_id=1, source_target_pairs={{0,8},{4,12},{8,16},{12,20},{16,24},{20,28},{24,32},{28,36},{32,40... | collective-permute-start | bytes 1013768 | tf_op jit(solution)/shard_map/ppermute | solution.py:20
  24.3 14.6 %collective-permute-start.1 = (bf16[264,640]{1,0:T(8,128)(2,1)S(1)}, bf16[264,640]{1,0:T(8,128)(2,1)}, u32[]{:S(2)}, u32[]{:S(2)}) collective-permute-start(bf16[264,640]{1,0:T(8,128)(2,1)S(1)} %pad_maximum_fusion.b0), channel_id=1, source_target_pairs={{4,0},{8,4},{12,8},{16,12},{20,16},{24,20},{28,24},{32,28},{36,32}... | collective-permute-start | bytes 1013768 | tf_op jit(solution)/shard_map/ppermute | solution.py:20
  33.4 6.0 %collective-permute-start = (bf16[264,640]{1,0:T(8,128)(2,1)S(1)}, bf16[264,640]{1,0:T(8,128)(2,1)}, u32[]{:S(2)}, u32[]{:S(2)}) collective-permute-start(bf16[264,640]{1,0:T(8,128)(2,1)S(1)} %pad_maximum_fusion.b0), channel_id=1, source_target_pairs={{0,4},{4,8},{8,12},{12,16},{16,20},{20,24},{24,28},{28,32},{32,36}... | collective-permute-start | bytes 1013768 | tf_op jit(solution)/shard_map/ppermute | solution.py:20
  47.9 3.5 %copy-start.5 = (s32[64]{0:T(128)S(1)}, s32[64]{0:T(128)}, u32[]{:S(2)}) copy-start(s32[64]{0:T(128)} %param.27) | copy-start | bytes 772
  47.9 13.8 %all-to-all-start = ((bf16[4,64,1280]{2,1,0:T(8,128)(2,1)}), bf16[4,64,1280]{2,1,0:T(8,128)(2,1)S(1)}, u32[]{:S(2)}, u32[]{:S(2)}) async-start(bf16[4,64,1280]{2,1,0:T(8,128)(2,1)} %bitcast.16), calls=%async_computation | async-start | bytes 1310720 | tf_op jit(solution)/shard_map/all_to_all | solution.py:157
  51.4 10.9 %copy-start.2 = (f32[1280]{0:T(1024)S(1)}, f32[1280]{0:T(1024)}, u32[]{:S(2)}) copy-start(f32[1280]{0:T(1024)} %param.24) | copy-start | bytes 15364
  63.6 8.1 %all-to-all-start.1 = ((bf16[64,4,160]{2,0,1:T(8,128)(2,1)}), bf16[64,4,160]{2,0,1:T(8,128)(2,1)S(1)}, u32[]{:S(2)}, u32[]{:S(2)}) async-start(bf16[64,4,160]{2,0,1:T(8,128)(2,1)} %copy.53), calls=%async_computation.1 | async-start | bytes 262144 | tf_op jit(solution)/shard_map/all_to_all | solution.py:166
